TPU v7x, 256 devices: a whole 4x4x8 slice. The times are simulated.
256 devices in a mesh: kx: 2 (over core), ky: 4 (over x), kz: 32 (over z, y).
Axes of the slice: x: 4, y: 4, z: 8, core: 2. Of those that a mesh axis runs over, the one named last changes fastest.
Arguments:
- populations: float32 [16, 8, 4, 64, 512], P('kx', None, None, 'ky', 'kz'), may hold values from -6 to 6
- force: float32 [16, 3, 4, 64, 512], P('kx', None, None, 'ky', 'kz'), may hold values from -3 to 3
- rate: float32 [16, 4, 64, 512], P('kx', None, 'ky', 'kz'), may hold values from 0.05 to 0.5
- tiles: bfloat16 [4, 1024, 1024], replicated, may hold values from -0.1875 to 0.1875
- send_planes: int32 [2, 4, 32, 32, 2], P('kx', 'ky', 'kz'), may hold values from 0 to 7
- recv_target: int32 [2, 4, 32, 32, 2], P('kx', 'ky', 'kz'), may hold values from 0 to 7
- recv_tile: int32 [2, 4, 32, 32, 2], P('kx', 'ky', 'kz'), may hold values from 0 to 3
- recv_count: int32 [2, 4, 32, 32], P('kx', 'ky', 'kz'), may hold values from 0 to 2, as said below
Outputs:
- final_populations: float32 [16, 8, 4, 64, 512], P('kx', None, None, 'ky', 'kz')
Inputs may be any that keep to these rules, and one draw needn't show every extreme that they name: `recv_count`: every receiving brick has some source brick with all 2 slots valid, and some receiving brick has all 2 slots valid from every source brick.
All inputs are finite; a program needn't handle non-finite values.
Results may differ from a plain program's by a relative error of at most 0.0042.
Values may be sent and summed in bfloat16 or wider, within the bound.
No kernel may reach another device: no remote copies, remote signals or barrier semaphores. Data moves between devices by JAX's collectives and lax.ppermute only.
A program may use at most 128 MiB of HBM per device.

v0:
```python
import jax
import jax.numpy as jnp
from jax import lax
from jax.experimental import pallas as pl
from jax.experimental.pallas import tpu as pltpu
from jax.sharding import PartitionSpec as P

ITERS = 2
F32 = jnp.float32
BF16 = jnp.bfloat16


def _split3(h):
    hi = h.astype(BF16)
    rest = h - hi.astype(F32)
    mid = rest.astype(BF16)
    lo = (rest - mid.astype(F32)).astype(BF16)
    return hi, mid, lo


def _exact_dot(h, m):
    hi, mid, lo = _split3(h)
    out = jnp.dot(hi, m, preferred_element_type=F32)
    out = out + jnp.dot(mid, m, preferred_element_type=F32)
    return out + jnp.dot(lo, m, preferred_element_type=F32)


def _select(kind, shape, k_axis):
    k = lax.broadcasted_iota(jnp.int32, shape, k_axis)
    c = lax.broadcasted_iota(jnp.int32, shape, 1 - k_axis)
    z = k & 15
    y = (k >> 4) & 15
    g = k >> 4
    b = k >> 8
    if kind == "z_lo":
        hit = (z < 2) & (c == g * 2 + z)
    elif kind == "z_hi":
        hit = (z >= 14) & (c == g * 2 + z - 14)
    elif kind == "y_lo":
        hit = (y < 2) & (c == b * 32 + y * 16 + z)
    else:
        hit = (y >= 14) & (c == b * 32 + (y - 14) * 16 + z)
    return jnp.where(hit, 1.0, 0.0).astype(BF16)


def _compress(cur, kind):
    lanes = cur.shape[1]
    return _exact_dot(cur, _select(kind, (lanes, 128), 0))


def _expand(h, kind, lanes):
    return _exact_dot(h, _select(kind, (128, lanes), 1))


def _emit_halos(cur, rnd_ref, zlo_ref, zhi_ref, ylo_ref, yhi_ref):
    rnd_ref[...] = cur.astype(BF16)
    zlo_ref[...] = _compress(cur, "z_lo")
    zhi_ref[...] = _compress(cur, "z_hi")
    ylo_ref[...] = _compress(cur, "y_lo")
    yhi_ref[...] = _compress(cur, "y_hi")


def _prep_kernel(cur_ref, rnd_ref, zlo_ref, zhi_ref, ylo_ref, yhi_ref):
    _emit_halos(cur_ref[...], rnd_ref, zlo_ref, zhi_ref, ylo_ref, yhi_ref)


def _finish_kernel(p_ref, coll_ref, q_ref, cur_ref, rnd_ref, zlo_ref, zhi_ref, ylo_ref, yhi_ref):
    cur = (p_ref[...] + coll_ref[...]) - q_ref[...]
    cur_ref[...] = cur
    _emit_halos(cur, rnd_ref, zlo_ref, zhi_ref, ylo_ref, yhi_ref)


def _deriv(a1, m1, a2, m2):
    return (8.0 * (a1 - m1) - (a2 - m2)) / 12.0


def _drift_kernel(cur_ref, xlo_ref, xhi_ref, hyp_ref, hym_ref, hzp_ref, hzm_ref,
                  fx_ref, fy_ref, fz_ref, rate_ref, p_ref, q_ref, ext_ref):
    rows, lanes = cur_ref.shape
    cur = cur_ref[...]
    ext_ref[0:16, :] = xlo_ref[...]
    ext_ref[16:16 + rows, :] = cur
    ext_ref[16 + rows:32 + rows, :] = xhi_ref[...]
    dx = _deriv(ext_ref[24:24 + rows, :], ext_ref[8:8 + rows, :],
                ext_ref[32:32 + rows, :], ext_ref[0:rows, :])

    k = lax.broadcasted_iota(jnp.int32, (rows, lanes), 1)
    z = k & 15
    y = (k >> 4) & 15

    eyp = _expand(hyp_ref[...], "y_hi", lanes)
    eym = _expand(hym_ref[...], "y_lo", lanes)
    yp1 = jnp.where(y == 15, pltpu.roll(eyp, 16, 1), pltpu.roll(cur, lanes - 16, 1))
    yp2 = jnp.where(y >= 14, eyp, pltpu.roll(cur, lanes - 32, 1))
    ym1 = jnp.where(y == 0, pltpu.roll(eym, lanes - 16, 1), pltpu.roll(cur, 16, 1))
    ym2 = jnp.where(y <= 1, eym, pltpu.roll(cur, 32, 1))
    dy = _deriv(yp1, ym1, yp2, ym2)

    ezp = _expand(hzp_ref[...], "z_hi", lanes)
    ezm = _expand(hzm_ref[...], "z_lo", lanes)
    zp1 = jnp.where(z == 15, pltpu.roll(ezp, 1, 1), pltpu.roll(cur, lanes - 1, 1))
    zp2 = jnp.where(z >= 14, ezp, pltpu.roll(cur, lanes - 2, 1))
    zm1 = jnp.where(z == 0, pltpu.roll(ezm, lanes - 1, 1), pltpu.roll(cur, 1, 1))
    zm2 = jnp.where(z <= 1, ezm, pltpu.roll(cur, 2, 1))
    dz = _deriv(zp1, zm1, zp2, zm2)

    drift = fx_ref[...] * dx
    drift = drift + fy_ref[...] * dy
    drift = drift + fz_ref[...] * dz
    p_ref[...] = cur - drift
    q_ref[...] = rate_ref[...] * cur


def _shapes(rows, lanes):
    plane = jax.ShapeDtypeStruct((rows, lanes), F32)
    halo = jax.ShapeDtypeStruct((rows, 128), F32)
    return [jax.ShapeDtypeStruct((rows, lanes), BF16), halo, halo, halo, halo], plane


def _prep(cur):
    rest, _ = _shapes(*cur.shape)
    return pl.pallas_call(_prep_kernel, out_shape=rest)(cur)


def _finish(p, coll, q):
    rest, plane = _shapes(*p.shape)
    outs = pl.pallas_call(_finish_kernel, out_shape=[plane] + rest)(p, coll, q)
    return outs[0], outs[1:]


def _drift(cur, xlo, xhi, hyp, hym, hzp, hzm, fx, fy, fz, rate):
    rows, lanes = cur.shape
    plane = jax.ShapeDtypeStruct((rows, lanes), F32)
    return pl.pallas_call(
        _drift_kernel,
        out_shape=[plane, plane],
        scratch_shapes=[pltpu.VMEM((rows + 32, lanes), F32)],
    )(cur, xlo, xhi, hyp, hym, hzp, hzm, fx, fy, fz, rate)


def _ring(axis):
    size = lax.axis_size(axis)
    up = [(i, (i + 1) % size) for i in range(size)]
    down = [(j, i) for i, j in up]
    return up, down


def per_device(populations, force, rate, tiles, send_planes, recv_target, recv_tile, recv_count):
    width_x, drive_count, band_count, width_y, width_z = populations.shape
    rows = width_x * drive_count
    lanes = band_count * width_y * width_z
    peer_count = lax.axis_size("kz")
    slot_cap = send_planes.shape[-1]
    tile_count = tiles.shape[0]
    plane_list = send_planes.reshape(peer_count * slot_cap)
    slot_count = recv_count.reshape(peer_count)
    target_ids = recv_target.reshape(peer_count, slot_cap)
    tile_ids = recv_tile.reshape(peer_count, slot_cap)
    usable = lax.broadcasted_iota(jnp.int32, (peer_count, slot_cap), 1) < slot_count[:, None]
    tile_match = (
        tile_ids[None, None] == jnp.arange(tile_count, dtype=jnp.int32)[:, None, None, None]
    )
    plane_match = (
        target_ids[None, None] == jnp.arange(width_x, dtype=jnp.int32)[None, :, None, None]
    )
    selector = (tile_match & plane_match & usable[None, None]).astype(BF16)
    selector = selector.reshape(tile_count * width_x, peer_count * slot_cap)

    def spread(a):
        a = a.reshape(width_x, 1, lanes)
        return jnp.broadcast_to(a, (width_x, drive_count, lanes)).reshape(rows, lanes)

    fx = spread(force[:, 0])
    fy = spread(force[:, 1])
    fz = spread(force[:, 2])
    rate_wide = spread(rate)

    up_x, down_x = _ring("kx")
    up_y, down_y = _ring("ky")
    up_z, down_z = _ring("kz")

    cur = populations.reshape(rows, lanes)
    rnd, zlo, zhi, ylo, yhi = _prep(cur)
    for iteration in range(ITERS):
        xlo = lax.ppermute(cur[rows - 16:], "kx", up_x)
        xhi = lax.ppermute(cur[:16], "kx", down_x)
        hym = lax.ppermute(yhi, "ky", up_y)
        hyp = lax.ppermute(ylo, "ky", down_y)
        hzm = lax.ppermute(zhi, "kz", up_z)
        hzp = lax.ppermute(zlo, "kz", down_z)
        plane_rows = rnd.reshape(width_x, drive_count, lanes)
        outgoing = plane_rows[plane_list].reshape(peer_count, slot_cap, drive_count, lanes)
        incoming = lax.all_to_all(outgoing, "kz", split_axis=0, concat_axis=0, tiled=True)
        p, q = _drift(cur, xlo, xhi, hyp, hym, hzp, hzm, fx, fy, fz, rate_wide)
        summed = lax.dot_general(
            selector,
            incoming.reshape(peer_count * slot_cap, drive_count, lanes),
            (((1,), (0,)), ((), ())),
            preferred_element_type=F32,
        )
        grouped = summed.astype(BF16).reshape(tile_count, rows, lanes)
        coll = lax.dot_general(
            grouped, tiles, (((0, 2), (0, 2)), ((), ())), preferred_element_type=F32
        )
        if iteration + 1 < ITERS:
            cur, (rnd, zlo, zhi, ylo, yhi) = _finish(p, coll, q)
        else:
            cur = (p + coll) - q
    return cur.reshape(width_x, drive_count, band_count, width_y, width_z)


def solution(mesh):
    placed = (
        P("kx", None, None, "ky", "kz"),
        P("kx", None, None, "ky", "kz"),
        P("kx", None, "ky", "kz"),
        P(),
        P("kx", "ky", "kz", None, None),
        P("kx", "ky", "kz", None, None),
        P("kx", "ky", "kz", None, None),
        P("kx", "ky", "kz", None),
    )
    return jax.shard_map(
        per_device,
        mesh=mesh,
        in_specs=placed,
        out_specs=P("kx", None, None, "ky", "kz"),
        check_vma=False,
    )
```

profile of v0, /device:TPU:6, one launch (start us, length us, event | category | flops | bytes accessed | tf_op | source)
XLA Modules:
  0.0 116.2 jit_solution(9883189732319173342)
XLA Ops:
  0.0 0.9 copy.34
  1.1 3.8 %reshape.176.cur_ref = f32[64,1024]{1,0:T(8,128)} reshape(f32[8,8,4,16,16]{4,3,2,1,0:T(8,128)} %param.8) | data formatting | bytes 524288 | tf_op jit(solution)/shard_map/reshape | solution.py:182
  4.9 2.6 %shard_map.82 = (bf16[64,1024]{1,0:T(8,128)(2,1)}, f32[64,128]{1,0:T(8,128)}, f32[64,128]{1,0:T(8,128)}, f32[64,128]{1,0:T(8,128)}, f32[64,128]{1,0:T(8,128)}) custom-call(f32[64,1024]{1,0:T(8,128)} %reshape.176.cur_ref), custom_call_target="tpu_custom_call" | custom-call | tf_op jit(solution)/shard_map/pallas_call | solution.py:122
  7.5 1.5 %gather_fusion = bf16[64,8,1024]{2,1,0:T(8,128)(2,1)S(1)} fusion(bf16[8,8,1024]{2,1,0:T(8,128)(2,1)} %bitcast.58, s32[1024]{0:T(1024)S(1)} %pad_clamp_fusion), kind=kCustom, calls=%fused_computation | custom fusion | bytes 2097408 | tf_op jit(solution)/shard_map/gather | solution.py:192
  9.0 2.1 %copy.35 = bf16[32,2,8,1024]{3,1,2,0:T(2,128)(2,1)} copy(bf16[32,2,8,1024]{3,2,1,0:T(8,128)(2,1)S(1)} %bitcast.60) | data formatting | bytes 2097152 | tf_op jit(solution)/shard_map/reshape | solution.py:192
  11.0 11.5 %all-to-all-start = ((bf16[32,2,8,1024]{3,1,2,0:T(2,128)(2,1)}), bf16[32,2,8,1024]{3,1,2,0:T(2,128)(2,1)S(1)}, u32[]{:S(2)}, u32[]{:S(2)}) async-start(bf16[32,2,8,1024]{3,1,2,0:T(2,128)(2,1)} %copy.35), calls=%async_computation | async-start | bytes 2097152 | tf_op jit(solution)/shard_map/all_to_all | solution.py:193
  22.5 0.9 collective-permute-start.2
  23.4 2.4 %collective-permute-start.3 = (f32[64,128]{1,0:T(8,128)}, f32[64,128]{1,0:T(8,128)S(1)}, u32[]{:S(2)}, u32[]{:S(2)}) collective-permute-start(f32[64,128]{1,0:T(8,128)} %get-tuple-element.21), channel_id=1, source_target_pairs={{0,32},{32,64},{64,96},{96,0},{1,33},{33,65},{65,97},{97,1},{2,34}... | collective-permute-start | bytes 98312 | tf_op jit(solution)/shard_map/ppermute | solution.py:187
  25.8 5.2 %collective-permute-start.4 = (f32[64,128]{1,0:T(8,128)}, f32[64,128]{1,0:T(8,128)S(1)}, u32[]{:S(2)}, u32[]{:S(2)}) collective-permute-start(f32[64,128]{1,0:T(8,128)} %get-tuple-element.22), channel_id=1, source_target_pairs={{1,0},{2,1},{3,2},{4,3},{5,4},{6,5},{7,6},{8,7},{9,8},{10,9},{11,1... | collective-permute-start | bytes 98312 | tf_op jit(solution)/shard_map/ppermute | solution.py:190
  31.1 1.1 fusion.3
  32.1 1.3 %slice.28 = f32[16,1024]{1,0:T(8,128)S(1)} reshape(f32[2,8,4,16,16]{4,3,2,1,0:T(8,128)} %get-tuple-element.36) | data formatting | bytes 131072 | tf_op jit(solution)/shard_map/slice | solution.py:185
  33.9 1.2 %fusion.4 = (f32[8,1,4,16,16]{4,3,2,1,0:T(8,128)S(1)}, f32[8,1,4,16,16]{4,3,2,1,0:T(8,128)S(1)}, f32[8,1,4,16,16]{4,3,2,1,0:T(8,128)S(1)}) fusion(f32[8,3,4,16,16]{4,3,2,1,0:T(8,128)} %param.9), kind=kLoop, calls=%fused_computation.21 | loop fusion | bytes 196608 | tf_op jit(solution)/shard_map/slice | solution.py:175
  35.7 0.9 broadcast_bitcast_fusion.2
  36.6 0.8 broadcast_bitcast_fusion
  37.5 1.3 %slice.30 = f32[16,1024]{1,0:T(8,128)S(1)} reshape(f32[2,8,4,16,16]{4,3,2,1,0:T(8,128)} %get-tuple-element.35) | data formatting | bytes 131072 | tf_op jit(solution)/shard_map/slice | solution.py:186
  39.9 4.1 %collective-permute-done.4.hzp_ref = f32[64,128]{1,0:T(8,128)S(1)} collective-permute-done((f32[64,128]{1,0:T(8,128)}, f32[64,128]{1,0:T(8,128)S(1)}, u32[]{:S(2)}, u32[]{:S(2)}) %collective-permute-start.4) | collective-permute-done | bytes 32800 | tf_op jit(solution)/shard_map/ppermute | solution.py:190
  44.0 5.8 %collective-permute-done.5.hzm_ref = f32[64,128]{1,0:T(8,128)S(1)} collective-permute-done((f32[64,128]{1,0:T(8,128)}, f32[64,128]{1,0:T(8,128)S(1)}, u32[]{:S(2)}, u32[]{:S(2)}) %collective-permute-start.5) | collective-permute-done | bytes 32800 | tf_op jit(solution)/shard_map/ppermute | solution.py:189
  50.5 3.3 %shard_map.83 = (f32[64,1024]{1,0:T(8,128)}, f32[64,1024]{1,0:T(8,128)}) custom-call(f32[64,1024]{1,0:T(8,128)} %reshape.176.cur_ref, f32[16,1024]{1,0:T(8,128)} %copy-done.4, f32[16,1024]{1,0:T(8,128)} %copy-done.7, f32[64,128]{1,0:T(8,128)} %copy-done.8, f32[64,128]{1,0:T(8,128)} %copy-done.9, f32[64,128]{1,0:T(8,128)} %copy-done.10, ...), custom_call_target="tpu_custom_call" | custom-call | tf_op jit(solution)/shard_map/pallas_call | solution.py:134
  55.6 6.8 %convolution_bitcast_fusion.1.coll_ref = f32[64,1024]{1,0:T(8,128)} fusion(bf16[4,64,1024]{2,1,0:T(8,128)(2,1)S(1)} %bitcast.61, bf16[4,1024,1024]{2,1,0:T(8,128)(2,1)} %param.11), kind=kOutput, calls=%fused_computation.5 | convolution fusion | flops 536870912 | bytes 9175040 | tf_op jit(solution)/shard_map/dot_general | solution.py:202
  62.3 2.7 %shard_map.84 = (f32[64,1024]{1,0:T(8,128)}, bf16[64,1024]{1,0:T(8,128)(2,1)}, f32[64,128]{1,0:T(8,128)}, f32[64,128]{1,0:T(8,128)}, f32[64,128]{1,0:T(8,128)}, /*index=5*/f32[64,128]{1,0:T(8,128)}) custom-call(f32[64,1024]{1,0:T(8,128)} %get-tuple-element.24.p_ref, f32[64,1024]{1,0:T(8,128)} %convolution_bitcast_fusion.1.coll_ref, ...), custom_call_target="tpu_custom_call" | custom-call | tf_op jit(solution)/shard_map/pallas_call | solution.py:127
  65.1 1.5 %gather_fusion.1 = bf16[64,8,1024]{2,1,0:T(8,128)(2,1)S(1)} fusion(bf16[8,8,1024]{2,1,0:T(8,128)(2,1)} %bitcast.57, s32[1024]{0:T(1024)S(1)} %pad_clamp_fusion), kind=kCustom, calls=%fused_computation.1 | custom fusion | bytes 2097408 | tf_op jit(solution)/shard_map/gather | solution.py:192
  66.6 2.1 %copy.39 = bf16[32,2,8,1024]{3,1,2,0:T(2,128)(2,1)} copy(bf16[32,2,8,1024]{3,2,1,0:T(8,128)(2,1)S(1)} %bitcast.59) | data formatting | bytes 2097152 | tf_op jit(solution)/shard_map/reshape | solution.py:192
  68.6 6.2 %all-to-all-start.1 = ((bf16[32,2,8,1024]{3,1,2,0:T(2,128)(2,1)}), bf16[32,2,8,1024]{3,1,2,0:T(2,128)(2,1)S(1)}, u32[]{:S(2)}, u32[]{:S(2)}) async-start(bf16[32,2,8,1024]{3,1,2,0:T(2,128)(2,1)} %copy.39), calls=%async_computation.1 | async-start | bytes 2097152 | tf_op jit(solution)/shard_map/all_to_all | solution.py:193
  74.8 0.9 collective-permute-start.8
  75.7 0.9 fusion.5
  77.2 2.4 %collective-permute-start.9 = (f32[64,128]{1,0:T(8,128)}, f32[64,128]{1,0:T(8,128)S(1)}, u32[]{:S(2)}, u32[]{:S(2)}) collective-permute-start(f32[64,128]{1,0:T(8,128)} %get-tuple-element.29), channel_id=1, source_target_pairs={{0,32},{32,64},{64,96},{96,0},{1,33},{33,65},{65,97},{97,1},{2,34}... | collective-permute-start | bytes 98312 | tf_op jit(solution)/shard_map/ppermute | solution.py:187
  79.6 5.2 %collective-permute-start.10 = (f32[64,128]{1,0:T(8,128)}, f32[64,128]{1,0:T(8,128)S(1)}, u32[]{:S(2)}, u32[]{:S(2)}) collective-permute-start(f32[64,128]{1,0:T(8,128)} %get-tuple-element.30), channel_id=1, source_target_pairs={{1,0},{2,1},{3,2},{4,3},{5,4},{6,5},{7,6},{8,7},{9,8},{10,9},{11,1... | collective-permute-start | bytes 98312 | tf_op jit(solution)/shard_map/ppermute | solution.py:190
  84.8 11.0 %collective-permute-done.10.hzp_ref = f32[64,128]{1,0:T(8,128)S(1)} collective-permute-done((f32[64,128]{1,0:T(8,128)}, f32[64,128]{1,0:T(8,128)S(1)}, u32[]{:S(2)}, u32[]{:S(2)}) %collective-permute-start.10) | collective-permute-done | bytes 32800 | tf_op jit(solution)/shard_map/ppermute | solution.py:190
  95.9 5.8 %collective-permute-done.11.hzm_ref = f32[64,128]{1,0:T(8,128)S(1)} collective-permute-done((f32[64,128]{1,0:T(8,128)}, f32[64,128]{1,0:T(8,128)S(1)}, u32[]{:S(2)}, u32[]{:S(2)}) %collective-permute-start.11) | collective-permute-done | bytes 32800 | tf_op jit(solution)/shard_map/ppermute | solution.py:189
  103.0 3.3 %shard_map.85 = (f32[64,1024]{1,0:T(8,128)}, f32[64,1024]{1,0:T(8,128)}) custom-call(f32[64,1024]{1,0:T(8,128)} %get-tuple-element.27.cur_ref, f32[16,1024]{1,0:T(8,128)} %copy-done.6, f32[16,1024]{1,0:T(8,128)} %copy-done.5, f32[64,128]{1,0:T(8,128)} %copy-done.12, f32[64,128]{1,0:T(8,128)} %copy-done.13, f32[64,128]{1,0:T(8,128)} %copy-done.14, ...), custom_call_target="tpu_custom_call" | custom-call | tf_op jit(solution)/shard_map/pallas_call | solution.py:134
  108.1 6.1 %convolution_bitcast_fusion = f32[64,1024]{1,0:T(8,128)S(1)} fusion(bf16[4,64,1024]{2,1,0:T(8,128)(2,1)S(1)} %bitcast.62, bf16[4,1024,1024]{2,1,0:T(8,128)(2,1)} %param.11), kind=kOutput, calls=%fused_computation.4 | convolution fusion | flops 536870912 | bytes 9175040 | tf_op jit(solution)/shard_map/dot_general | solution.py:202
  114.2 2.0 %reshape.190 = f32[8,8,4,16,16]{4,3,2,1,0:T(8,128)} reshape(f32[64,1024]{1,0:T(8,128)S(1)} %add_subtract_fusion) | data formatting | bytes 524288 | tf_op jit(solution)/shard_map/reshape | solution.py:209
  (77 shorter events, 8.5 us)
Async XLA Ops:
  0.0 31.1 %copy-start = (f32[8,8,4,16,16]{4,3,2,1,0:T(8,128)S(1)}, f32[8,8,4,16,16]{4,3,2,1,0:T(8,128)}, u32[]{:S(2)}) copy-start(f32[8,8,4,16,16]{4,3,2,1,0:T(8,128)} %param.8) | copy-start | bytes 786436
  0.0 33.5 %copy-start.16 = (s32[1,1,1,32,2]{3,4,2,1,0:T(2,128)S(1)}, s32[1,1,1,32,2]{3,4,2,1,0:T(2,128)}, u32[]{:S(2)}) copy-start(s32[1,1,1,32,2]{3,4,2,1,0:T(2,128)} %param.13) | copy-start | bytes 772
  0.0 33.6 %copy-start.17 = (s32[1,1,1,32,2]{3,4,2,1,0:T(2,128)S(1)}, s32[1,1,1,32,2]{3,4,2,1,0:T(2,128)}, u32[]{:S(2)}) copy-start(s32[1,1,1,32,2]{3,4,2,1,0:T(2,128)} %param.14) | copy-start | bytes 772
  0.0 33.7 %copy-start.1 = (f32[8,4,16,16]{3,2,1,0:T(8,128)S(1)}, f32[8,4,16,16]{3,2,1,0:T(8,128)}, u32[]{:S(2)}) copy-start(f32[8,4,16,16]{3,2,1,0:T(8,128)} %param.10) | copy-start | bytes 98308
  0.0 37.4 %copy-start.18 = (s32[1,1,1,32]{3,2,1,0:T(1,128)S(1)}, s32[1,1,1,32]{3,2,1,0:T(1,128)}, u32[]{:S(2)}) copy-start(s32[1,1,1,32]{3,2,1,0:T(1,128)} %param.15) | copy-start | bytes 388
  11.0 42.7 %all-to-all-start = ((bf16[32,2,8,1024]{3,1,2,0:T(2,128)(2,1)}), bf16[32,2,8,1024]{3,1,2,0:T(2,128)(2,1)S(1)}, u32[]{:S(2)}, u32[]{:S(2)}) async-start(bf16[32,2,8,1024]{3,1,2,0:T(2,128)(2,1)} %copy.35), calls=%async_computation | async-start | bytes 2097152 | tf_op jit(solution)/shard_map/all_to_all | solution.py:193
  22.5 16.3 %collective-permute-start.2 = (f32[64,128]{1,0:T(8,128)}, f32[64,128]{1,0:T(8,128)S(1)}, u32[]{:S(2)}, u32[]{:S(2)}) collective-permute-start(f32[64,128]{1,0:T(8,128)} %get-tuple-element.20), channel_id=1, source_target_pairs={{32,0},{64,32},{96,64},{0,96},{33,1},{65,33},{97,65},{1,97},{34,2}... | collective-permute-start | bytes 98312 | tf_op jit(solution)/shard_map/ppermute | solution.py:188
  23.4 16.5 %collective-permute-start.3 = (f32[64,128]{1,0:T(8,128)}, f32[64,128]{1,0:T(8,128)S(1)}, u32[]{:S(2)}, u32[]{:S(2)}) collective-permute-start(f32[64,128]{1,0:T(8,128)} %get-tuple-element.21), channel_id=1, source_target_pairs={{0,32},{32,64},{64,96},{96,0},{1,33},{33,65},{65,97},{97,1},{2,34}... | collective-permute-start | bytes 98312 | tf_op jit(solution)/shard_map/ppermute | solution.py:187
  25.8 18.2 %collective-permute-start.4 = (f32[64,128]{1,0:T(8,128)}, f32[64,128]{1,0:T(8,128)S(1)}, u32[]{:S(2)}, u32[]{:S(2)}) collective-permute-start(f32[64,128]{1,0:T(8,128)} %get-tuple-element.22), channel_id=1, source_target_pairs={{1,0},{2,1},{3,2},{4,3},{5,4},{6,5},{7,6},{8,7},{9,8},{10,9},{11,1... | collective-permute-start | bytes 98312 | tf_op jit(solution)/shard_map/ppermute | solution.py:190
  31.0 18.8 %collective-permute-start.5 = (f32[64,128]{1,0:T(8,128)}, f32[64,128]{1,0:T(8,128)S(1)}, u32[]{:S(2)}, u32[]{:S(2)}) collective-permute-start(f32[64,128]{1,0:T(8,128)} %get-tuple-element.23), channel_id=1, source_target_pairs={{0,1},{1,2},{2,3},{3,4},{4,5},{5,6},{6,7},{7,8},{8,9},{9,10},{10,1... | collective-permute-start | bytes 98312 | tf_op jit(solution)/shard_map/ppermute | solution.py:189
  33.4 16.4 %collective-permute-start = (f32[16,1024]{1,0:T(8,128)S(1)}, f32[16,1024]{1,0:T(8,128)S(1)}, u32[]{:S(2)}, u32[]{:S(2)}) collective-permute-start(f32[16,1024]{1,0:T(8,128)S(1)} %slice.28), channel_id=1, source_target_pairs={{0,128},{128,0},{1,129},{129,1},{2,130},{130,2},{3,131},{131,3},{4... | collective-permute-start | bytes 196616 | tf_op jit(solution)/shard_map/ppermute | solution.py:185
  38.8 11.0 %copy-start.8 = (f32[64,128]{1,0:T(8,128)}, f32[64,128]{1,0:T(8,128)S(1)}, u32[]{:S(2)}) copy-start(f32[64,128]{1,0:T(8,128)S(1)} %collective-permute-done.2.hyp_ref) | copy-start | bytes 98308
  38.9 11.0 %collective-permute-start.1 = (f32[16,1024]{1,0:T(8,128)S(1)}, f32[16,1024]{1,0:T(8,128)S(1)}, u32[]{:S(2)}, u32[]{:S(2)}) collective-permute-start(f32[16,1024]{1,0:T(8,128)S(1)} %slice.30), channel_id=1, source_target_pairs={{128,0},{0,128},{129,1},{1,129},{130,2},{2,130},{131,3},{3,131},{1... | collective-permute-start | bytes 196616 | tf_op jit(solution)/shard_map/ppermute | solution.py:186
  39.9 9.9 %copy-start.9 = (f32[64,128]{1,0:T(8,128)}, f32[64,128]{1,0:T(8,128)S(1)}, u32[]{:S(2)}) copy-start(f32[64,128]{1,0:T(8,128)S(1)} %collective-permute-done.3.hym_ref) | copy-start | bytes 98308
  44.0 5.9 %copy-start.10 = (f32[64,128]{1,0:T(8,128)}, f32[64,128]{1,0:T(8,128)S(1)}, u32[]{:S(2)}) copy-start(f32[64,128]{1,0:T(8,128)S(1)} %collective-permute-done.4.hzp_ref) | copy-start | bytes 98308
  49.8 0.6 copy-start.4
  49.8 0.6 copy-start.7
  68.6 37.6 %all-to-all-start.1 = ((bf16[32,2,8,1024]{3,1,2,0:T(2,128)(2,1)}), bf16[32,2,8,1024]{3,1,2,0:T(2,128)(2,1)S(1)}, u32[]{:S(2)}, u32[]{:S(2)}) async-start(bf16[32,2,8,1024]{3,1,2,0:T(2,128)(2,1)} %copy.39), calls=%async_computation.1 | async-start | bytes 2097152 | tf_op jit(solution)/shard_map/all_to_all | solution.py:193
  74.8 10.0 %collective-permute-start.8 = (f32[64,128]{1,0:T(8,128)}, f32[64,128]{1,0:T(8,128)S(1)}, u32[]{:S(2)}, u32[]{:S(2)}) collective-permute-start(f32[64,128]{1,0:T(8,128)} %get-tuple-element.28), channel_id=1, source_target_pairs={{32,0},{64,32},{96,64},{0,96},{33,1},{65,33},{97,65},{1,97},{34,2}... | collective-permute-start | bytes 98312 | tf_op jit(solution)/shard_map/ppermute | solution.py:188
  76.6 25.1 %collective-permute-start.7 = (f32[16,1024]{1,0:T(8,128)S(1)}, f32[16,1024]{1,0:T(8,128)S(1)}, u32[]{:S(2)}, u32[]{:S(2)}) collective-permute-start(f32[16,1024]{1,0:T(8,128)S(1)} %get-tuple-element.40), channel_id=1, source_target_pairs={{128,0},{0,128},{129,1},{1,129},{130,2},{2,130},{131,3},{3,131},{1... | collective-permute-start | bytes 196616 | tf_op jit(solution)/shard_map/ppermute | solution.py:186
  76.7 25.0 %collective-permute-start.6 = (f32[16,1024]{1,0:T(8,128)S(1)}, f32[16,1024]{1,0:T(8,128)S(1)}, u32[]{:S(2)}, u32[]{:S(2)}) collective-permute-start(f32[16,1024]{1,0:T(8,128)S(1)} %get-tuple-element.41), channel_id=1, source_target_pairs={{0,128},{128,0},{1,129},{129,1},{2,130},{130,2},{3,131},{131,3},{4... | collective-permute-start | bytes 196616 | tf_op jit(solution)/shard_map/ppermute | solution.py:185
  77.2 7.6 %collective-permute-start.9 = (f32[64,128]{1,0:T(8,128)}, f32[64,128]{1,0:T(8,128)S(1)}, u32[]{:S(2)}, u32[]{:S(2)}) collective-permute-start(f32[64,128]{1,0:T(8,128)} %get-tuple-element.29), channel_id=1, source_target_pairs={{0,32},{32,64},{64,96},{96,0},{1,33},{33,65},{65,97},{97,1},{2,34}... | collective-permute-start | bytes 98312 | tf_op jit(solution)/shard_map/ppermute | solution.py:187
  79.6 16.3 %collective-permute-start.10 = (f32[64,128]{1,0:T(8,128)}, f32[64,128]{1,0:T(8,128)S(1)}, u32[]{:S(2)}, u32[]{:S(2)}) collective-permute-start(f32[64,128]{1,0:T(8,128)} %get-tuple-element.30), channel_id=1, source_target_pairs={{1,0},{2,1},{3,2},{4,3},{5,4},{6,5},{7,6},{8,7},{9,8},{10,9},{11,1... | collective-permute-start | bytes 98312 | tf_op jit(solution)/shard_map/ppermute | solution.py:190
  84.8 16.9 %copy-start.12 = (f32[64,128]{1,0:T(8,128)}, f32[64,128]{1,0:T(8,128)S(1)}, u32[]{:S(2)}) copy-start(f32[64,128]{1,0:T(8,128)S(1)} %collective-permute-done.8.hyp_ref) | copy-start | bytes 98308
  84.8 16.9 %collective-permute-start.11 = (f32[64,128]{1,0:T(8,128)}, f32[64,128]{1,0:T(8,128)S(1)}, u32[]{:S(2)}, u32[]{:S(2)}) collective-permute-start(f32[64,128]{1,0:T(8,128)} %get-tuple-element.31), channel_id=1, source_target_pairs={{0,1},{1,2},{2,3},{3,4},{4,5},{5,6},{6,7},{7,8},{8,9},{9,10},{10,1... | collective-permute-start | bytes 98312 | tf_op jit(solution)/shard_map/ppermute | solution.py:189
  84.8 16.9 %copy-start.13 = (f32[64,128]{1,0:T(8,128)}, f32[64,128]{1,0:T(8,128)S(1)}, u32[]{:S(2)}) copy-start(f32[64,128]{1,0:T(8,128)S(1)} %collective-permute-done.9.hym_ref) | copy-start | bytes 98308
  95.9 5.9 %copy-start.14 = (f32[64,128]{1,0:T(8,128)}, f32[64,128]{1,0:T(8,128)S(1)}, u32[]{:S(2)}) copy-start(f32[64,128]{1,0:T(8,128)S(1)} %collective-permute-done.10.hzp_ref) | copy-start | bytes 98308
  101.7 0.6 copy-start.15
  101.7 0.6 copy-start.5
  102.3 0.6 copy-start.6
  106.2 7.9 %copy-start.2 = (f32[64,1024]{1,0:T(8,128)S(1)}, f32[64,1024]{1,0:T(8,128)}, u32[]{:S(2)}) copy-start(f32[64,1024]{1,0:T(8,128)} %get-tuple-element.32) | copy-start | bytes 786436
  106.2 7.9 %copy-start.3 = (f32[64,1024]{1,0:T(8,128)S(1)}, f32[64,1024]{1,0:T(8,128)}, u32[]{:S(2)}) copy-start(f32[64,1024]{1,0:T(8,128)} %get-tuple-element.34) | copy-start | bytes 786436
  (1 other events, 0.6 us)
where the time goes:
time: 117 us; the launch traced here: 116 us
  starting transfers between devices  36.1 us (31%)
  local copies, waits for them, and re-layouts  27.2 us (23%)
  waiting for transfers between devices  26.8 us (23%)
  matrix products  13.5 us (12%)
  Pallas kernels  11.8 us (10%)
    all_to_all x2, starting transfers between devices, per_device(): lax.all_to_all(outgoing, 'kz', split_axis=0, concat_axis=0, tiled=True)  17.6 us
    ppermute x2, waiting for transfers between devices, per_device(): hzp = lax.ppermute(zlo, 'kz', down_z)  15.1 us
    dot_general x2, matrix products, per_device(): lax.dot_general(grouped, tiles, (((0, 2), (0, 2)), ((), ())), preferred_e...  12.8 us
    ppermute x2, waiting for transfers between devices, per_device(): hzm = lax.ppermute(zhi, 'kz', up_z)  11.7 us
    ppermute x2, starting transfers between devices, per_device(): hzp = lax.ppermute(zlo, 'kz', down_z)  10.4 us
    pallas_call x2, Pallas kernels, _drift(): pl.pallas_call(_drift_kernel, out_shape=[plane, plane], scratch_shapes=[p...  6.53 us
    ppermute x2, starting transfers between devices, per_device(): hym = lax.ppermute(yhi, 'ky', up_y)  4.81 us
    reshape x2, local copies, waits for them, and re-layouts, per_device(): plane_rows[plane_list].reshape(peer_count, slot_cap, drive_count, lanes)  4.1 us
  transfers between devices with their start and end apart: 14, of which 4 were waited for; matrix products, arithmetic and copies ran while one was open for 8% of the time, Pallas kernels for 6%

commit v1 on v0

--- a/solution.py
+++ b/solution.py
@@ -1,3 +1,5 @@
+import functools
+
 import jax
 import jax.numpy as jnp
 from jax import lax
@@ -52,22 +54,55 @@
     return _exact_dot(h, _select(kind, (128, lanes), 1))
 
 
-def _emit_halos(cur, rnd_ref, zlo_ref, zhi_ref, ylo_ref, yhi_ref):
-    rnd_ref[...] = cur.astype(BF16)
+def _emit_halos(cur, zlo_ref, zhi_ref, ylo_ref, yhi_ref):
     zlo_ref[...] = _compress(cur, "z_lo")
     zhi_ref[...] = _compress(cur, "z_hi")
     ylo_ref[...] = _compress(cur, "y_lo")
     yhi_ref[...] = _compress(cur, "y_hi")
 
 
-def _prep_kernel(cur_ref, rnd_ref, zlo_ref, zhi_ref, ylo_ref, yhi_ref):
-    _emit_halos(cur_ref[...], rnd_ref, zlo_ref, zhi_ref, ylo_ref, yhi_ref)
-
-
-def _finish_kernel(p_ref, coll_ref, q_ref, cur_ref, rnd_ref, zlo_ref, zhi_ref, ylo_ref, yhi_ref):
-    cur = (p_ref[...] + coll_ref[...]) - q_ref[...]
-    cur_ref[...] = cur
-    _emit_halos(cur, rnd_ref, zlo_ref, zhi_ref, ylo_ref, yhi_ref)
+def _emit_send(plist_ref, cur_ref, snd_ref):
+    peers, both, _ = snd_ref.shape
+    slot_cap = both // 8
+    for s in range(peers):
+        parts = []
+        for c in range(slot_cap):
+            plane = plist_ref[s * slot_cap + c]
+            parts.append(cur_ref[pl.ds(pl.multiple_of(plane * 8, 8), 8), :])
+        snd_ref[s] = jnp.concatenate(parts, axis=0).astype(BF16)
+
+
+def _prep_kernel(plist_ref, cur_ref, snd_ref, zlo_ref, zhi_ref, ylo_ref, yhi_ref):
+    _emit_send(plist_ref, cur_ref, snd_ref)
+    _emit_halos(cur_ref[...], zlo_ref, zhi_ref, ylo_ref, yhi_ref)
+
+
+def _finish_kernel(last, plist_ref, sel_ref, inc_ref, p_ref, q_ref, w_ref, *refs):
+    if last:
+        cur_ref, g_scr, acc_scr = refs
+    else:
+        cur_ref, snd_ref, zlo_ref, zhi_ref, ylo_ref, yhi_ref, g_scr, acc_scr = refs
+    t = pl.program_id(0)
+    rows = p_ref.shape[0]
+
+    @pl.when(t == 0)
+    def _():
+        summed = jnp.dot(sel_ref[...], inc_ref[...], preferred_element_type=F32)
+        g_scr[...] = summed.astype(BF16)
+        acc_scr[...] = jnp.zeros_like(acc_scr)
+
+    grouped = g_scr[pl.ds(pl.multiple_of(t * rows, rows), rows), :]
+    acc_scr[...] += lax.dot_general(
+        grouped, w_ref[0], (((1,), (1,)), ((), ())), preferred_element_type=F32
+    )
+
+    @pl.when(t == pl.num_programs(0) - 1)
+    def _():
+        cur = (p_ref[...] + acc_scr[...]) - q_ref[...]
+        cur_ref[...] = cur
+        if not last:
+            _emit_halos(cur, zlo_ref, zhi_ref, ylo_ref, yhi_ref)
+            _emit_send(plist_ref, cur_ref, snd_ref)
 
 
 def _deriv(a1, m1, a2, m2):
@@ -111,20 +146,59 @@
     q_ref[...] = rate_ref[...] * cur
 
 
-def _shapes(rows, lanes):
-    plane = jax.ShapeDtypeStruct((rows, lanes), F32)
+def _full(shape):
+    zeros = (0,) * len(shape)
+    return pl.BlockSpec(shape, lambda *_: zeros)
+
+
+def _rest_shapes(rows, lanes, peers, both):
     halo = jax.ShapeDtypeStruct((rows, 128), F32)
-    return [jax.ShapeDtypeStruct((rows, lanes), BF16), halo, halo, halo, halo], plane
-
-
-def _prep(cur):
-    rest, _ = _shapes(*cur.shape)
-    return pl.pallas_call(_prep_kernel, out_shape=rest)(cur)
-
-
-def _finish(p, coll, q):
-    rest, plane = _shapes(*p.shape)
-    outs = pl.pallas_call(_finish_kernel, out_shape=[plane] + rest)(p, coll, q)
+    snd = jax.ShapeDtypeStruct((peers, both, lanes), BF16)
+    return [snd, halo, halo, halo, halo]
+
+
+def _prep(plist, cur, peers, both):
+    rows, lanes = cur.shape
+    shapes = _rest_shapes(rows, lanes, peers, both)
+    return pl.pallas_call(
+        _prep_kernel,
+        out_shape=shapes,
+        grid_spec=pltpu.PrefetchScalarGridSpec(
+            num_scalar_prefetch=1,
+            grid=(1,),
+            in_specs=[_full(cur.shape)],
+            out_specs=[_full(x.shape) for x in shapes],
+        ),
+    )(plist, cur)
+
+
+def _finish(last, plist, sel, inc, p, q, tiles, peers, both):
+    rows, lanes = p.shape
+    tile_count = tiles.shape[0]
+    shapes = [jax.ShapeDtypeStruct((rows, lanes), F32)]
+    if not last:
+        shapes += _rest_shapes(rows, lanes, peers, both)
+    outs = pl.pallas_call(
+        functools.partial(_finish_kernel, last),
+        out_shape=shapes,
+        grid_spec=pltpu.PrefetchScalarGridSpec(
+            num_scalar_prefetch=1,
+            grid=(tile_count,),
+            in_specs=[
+                _full(sel.shape),
+                _full(inc.shape),
+                _full(p.shape),
+                _full(q.shape),
+                pl.BlockSpec((1,) + tiles.shape[1:], lambda t, *_: (t, 0, 0)),
+            ],
+            out_specs=[_full(x.shape) for x in shapes],
+            scratch_shapes=[
+                pltpu.VMEM((tile_count * rows, lanes), BF16),
+                pltpu.VMEM((rows, lanes), F32),
+            ],
+        ),
+        compiler_params=pltpu.CompilerParams(dimension_semantics=("arbitrary",)),
+    )(plist, sel, inc, p, q, tiles)
     return outs[0], outs[1:]
 
 
@@ -165,6 +239,11 @@
     )
     selector = (tile_match & plane_match & usable[None, None]).astype(BF16)
     selector = selector.reshape(tile_count * width_x, peer_count * slot_cap)
+    eye = jnp.eye(drive_count, dtype=BF16)
+    sel_big = (selector[:, None, :, None] * eye[None, :, None, :]).reshape(
+        tile_count * width_x * drive_count, peer_count * slot_cap * drive_count
+    )
+    both = slot_cap * drive_count
 
     def spread(a):
         a = a.reshape(width_x, 1, lanes)
@@ -180,32 +259,21 @@
     up_z, down_z = _ring("kz")
 
     cur = populations.reshape(rows, lanes)
-    rnd, zlo, zhi, ylo, yhi = _prep(cur)
+    snd, zlo, zhi, ylo, yhi = _prep(plane_list, cur, peer_count, both)
     for iteration in range(ITERS):
+        last = iteration + 1 == ITERS
         xlo = lax.ppermute(cur[rows - 16:], "kx", up_x)
         xhi = lax.ppermute(cur[:16], "kx", down_x)
         hym = lax.ppermute(yhi, "ky", up_y)
         hyp = lax.ppermute(ylo, "ky", down_y)
         hzm = lax.ppermute(zhi, "kz", up_z)
         hzp = lax.ppermute(zlo, "kz", down_z)
-        plane_rows = rnd.reshape(width_x, drive_count, lanes)
-        outgoing = plane_rows[plane_list].reshape(peer_count, slot_cap, drive_count, lanes)
-        incoming = lax.all_to_all(outgoing, "kz", split_axis=0, concat_axis=0, tiled=True)
+        incoming = lax.all_to_all(snd, "kz", split_axis=0, concat_axis=0, tiled=True)
         p, q = _drift(cur, xlo, xhi, hyp, hym, hzp, hzm, fx, fy, fz, rate_wide)
-        summed = lax.dot_general(
-            selector,
-            incoming.reshape(peer_count * slot_cap, drive_count, lanes),
-            (((1,), (0,)), ((), ())),
-            preferred_element_type=F32,
-        )
-        grouped = summed.astype(BF16).reshape(tile_count, rows, lanes)
-        coll = lax.dot_general(
-            grouped, tiles, (((0, 2), (0, 2)), ((), ())), preferred_element_type=F32
-        )
-        if iteration + 1 < ITERS:
-            cur, (rnd, zlo, zhi, ylo, yhi) = _finish(p, coll, q)
-        else:
-            cur = (p + coll) - q
+        inc = incoming.reshape(peer_count * both, lanes)
+        cur, rest = _finish(last, plane_list, sel_big, inc, p, q, tiles, peer_count, both)
+        if not last:
+            snd, zlo, zhi, ylo, yhi = rest
     return cur.reshape(width_x, drive_count, band_count, width_y, width_z)
 
 

time: 117 us -> 116 us (level)
  Pallas kernels: 11.8 us -> 27.8 us
  matrix products: 13.5 us -> 0 us
  waiting for transfers between devices: 26.8 us -> 17.1 us
  starting transfers between devices: 36.1 us -> 38.4 us
  other arithmetic: 0.54 us -> 2.74 us
  local copies, waits for them, and re-layouts: 27.2 us -> 28.6 us
    pallas_call x2 -> x3, Pallas kernels: 5.27 us -> 21.2 us  [the longest x2 17.5 us: _finish(): pl.pallas_call(functools.partial(_finish_kernel, last), out_shape=shapes,...]
    dot_general x4 -> x0, matrix products: 13.5 us -> none  [the longest x2 12.8 us: per_device(): lax.dot_general(grouped, tiles, (((0, 2), (0, 2)), ((), ())), preferred_e...]
    mul x0 -> x1, local copies, waits for them, and re-layouts: none -> 7.66 us  [per_device(): selector[:, None, :, None] * eye[None, :, None, :]]
    ppermute x2, waiting for transfers between devices: 11.7 us -> 6.42 us  [per_device(): hzm = lax.ppermute(zhi, 'kz', up_z)]
    reshape x4 -> x0, local copies, waits for them, and re-layouts: 4.98 us -> none  [the longest x2 4.1 us: per_device(): plane_rows[plane_list].reshape(peer_count, slot_cap, drive_count, lanes)]
    ppermute x2, waiting for transfers between devices: 15.1 us -> 10.7 us  [per_device(): hzp = lax.ppermute(zlo, 'kz', down_z)]
    gather x2 -> x0, local copies, waits for them, and re-layouts: 3.03 us -> none  [per_device(): plane_rows[plane_list].reshape(peer_count, slot_cap, drive_count, lanes)]
    all_to_all x2, starting transfers between devices: 17.6 us -> 20 us  [per_device(): lax.all_to_all(snd, 'kz', split_axis=0, concat_axis=0, tiled=True)]
  transfers between devices with their start and end apart: 14 -> 14, of which waited for: 4 -> 2; matrix products, arithmetic and copies ran while one was open for 8% -> 17% of each run, Pallas kernels for 6% -> 6%
where the time goes in v1:
time: 116 us; the launch traced here: 115 us
  starting transfers between devices  38.4 us (33%)
  local copies, waits for them, and re-layouts  28.6 us (25%)
  Pallas kernels  27.8 us (24%)
  waiting for transfers between devices  17.1 us (15%)
  other arithmetic  2.74 us (2%)
    all_to_all x2, starting transfers between devices, per_device(): lax.all_to_all(snd, 'kz', split_axis=0, concat_axis=0, tiled=True)  20 us
    pallas_call x2, Pallas kernels, _finish(): pl.pallas_call(functools.partial(_finish_kernel, last), out_shape=shapes,...  17.5 us
    ppermute x2, waiting for transfers between devices, per_device(): hzp = lax.ppermute(zlo, 'kz', down_z)  10.7 us
    ppermute x2, starting transfers between devices, per_device(): hzp = lax.ppermute(zlo, 'kz', down_z)  10.4 us
    mul x1, local copies, waits for them, and re-layouts, per_device(): selector[:, None, :, None] * eye[None, :, None, :]  7.66 us
    pallas_call x2, Pallas kernels, _drift(): pl.pallas_call(_drift_kernel, out_shape=[plane, plane], scratch_shapes=[p...  6.57 us
    ppermute x2, waiting for transfers between devices, per_device(): hzm = lax.ppermute(zhi, 'kz', up_z)  6.42 us
    ppermute x2, starting transfers between devices, per_device(): hym = lax.ppermute(yhi, 'ky', up_y)  5.54 us
  transfers between devices with their start and end apart: 14, of which 2 were waited for; matrix products, arithmetic and copies ran while one was open for 17% of the time, Pallas kernels for 6%

profile of v1, /device:TPU:6, one launch (start us, length us, event | category | flops | bytes accessed | tf_op | source)
XLA Modules:
  0.0 115.0 jit_solution(13979047194004388389)
XLA Ops:
  0.0 0.9 copy.12
  0.9 0.6 reshape.104.plist_ref
  1.6 3.8 %reshape.105.cur_ref = f32[64,1024]{1,0:T(8,128)} reshape(f32[8,8,4,16,16]{4,3,2,1,0:T(8,128)} %param.8) | data formatting | bytes 524288 | tf_op jit(solution)/shard_map/reshape | solution.py:261
  5.4 3.7 %shard_map.82 = (bf16[32,16,1024]{2,1,0:T(8,128)(2,1)}, f32[64,128]{1,0:T(8,128)}, f32[64,128]{1,0:T(8,128)}, f32[64,128]{1,0:T(8,128)}, f32[64,128]{1,0:T(8,128)}) custom-call(s32[64]{0:T(128)} %reshape.104.plist_ref, f32[64,1024]{1,0:T(8,128)} %reshape.105.cur_ref), custom_call_target="tpu_custom_call" | custom-call | tf_op jit(solution)/shard_map/pallas_call | solution.py:163
  9.1 11.6 %all-to-all-start = ((bf16[32,16,1024]{2,1,0:T(8,128)(2,1)}), bf16[32,16,1024]{2,1,0:T(8,128)(2,1)S(1)}, u32[]{:S(2)}, u32[]{:S(2)}) async-start(bf16[32,16,1024]{2,1,0:T(8,128)(2,1)} %get-tuple-element.20), calls=%async_computation | async-start | bytes 2097152 | tf_op jit(solution)/shard_map/all_to_all | solution.py:271
  20.7 1.1 fusion.1
  21.8 1.4 %slice.28 = f32[16,1024]{1,0:T(8,128)S(1)} reshape(f32[2,8,4,16,16]{4,3,2,1,0:T(8,128)} %get-tuple-element.36) | data formatting | bytes 131072 | tf_op jit(solution)/shard_map/slice | solution.py:265
  23.3 1.3 %slice.30 = f32[16,1024]{1,0:T(8,128)S(1)} reshape(f32[2,8,4,16,16]{4,3,2,1,0:T(8,128)} %get-tuple-element.35) | data formatting | bytes 131072 | tf_op jit(solution)/shard_map/slice | solution.py:266
  24.6 0.6 collective-permute-start.1
  25.1 0.8 collective-permute-start.2
  26.0 2.4 %collective-permute-start.3 = (f32[64,128]{1,0:T(8,128)S(1)}, f32[64,128]{1,0:T(8,128)S(1)}, u32[]{:S(2)}, u32[]{:S(2)}) collective-permute-start(f32[64,128]{1,0:T(8,128)S(1)} %copy-done.21), channel_id=1, source_target_pairs={{0,32},{32,64},{64,96},{96,0},{1,33},{33,65},{65,97},{97,1},{2,34}... | collective-permute-start | bytes 98312 | tf_op jit(solution)/shard_map/ppermute | solution.py:267
  28.4 5.2 %collective-permute-start.4 = (f32[64,128]{1,0:T(8,128)S(1)}, f32[64,128]{1,0:T(8,128)S(1)}, u32[]{:S(2)}, u32[]{:S(2)}) collective-permute-start(f32[64,128]{1,0:T(8,128)S(1)} %copy-done.20), channel_id=1, source_target_pairs={{1,0},{2,1},{3,2},{4,3},{5,4},{6,5},{7,6},{8,7},{9,8},{10,9},{11,1... | collective-permute-start | bytes 98312 | tf_op jit(solution)/shard_map/ppermute | solution.py:270
  34.7 1.2 %fusion.2 = (f32[8,1,4,16,16]{4,3,2,1,0:T(8,128)S(1)}, f32[8,1,4,16,16]{4,3,2,1,0:T(8,128)S(1)}, f32[8,1,4,16,16]{4,3,2,1,0:T(8,128)S(1)}) fusion(f32[8,3,4,16,16]{4,3,2,1,0:T(8,128)} %param.9), kind=kLoop, calls=%fused_computation.12 | loop fusion | bytes 196608 | tf_op jit(solution)/shard_map/slice | solution.py:254
  36.2 2.3 %broadcast_multiply_fusion = bf16[32,8,64,8]{3,2,1,0:T(8,128)(2,1)} fusion(bf16[8,8]{1,0:T(8,128)(2,1)S(1)} %fusion, bf16[32,64]{1,0:T(8,128)(2,1)S(1)} %copy.15), kind=kLoop, calls=%fused_computation | loop fusion | flops 131072 | bytes 266368 | tf_op jit(solution)/shard_map/mul | solution.py:243
  38.5 0.9 broadcast_bitcast_fusion.2
  40.0 0.9 broadcast_bitcast_fusion
  40.9 7.7 %mul.20.sel_ref = bf16[256,512]{1,0:T(8,128)(2,1)} reshape(bf16[32,8,64,8]{3,2,1,0:T(8,128)(2,1)} %broadcast_multiply_fusion) | data formatting | bytes 524288 | tf_op jit(solution)/shard_map/mul | solution.py:243
  49.2 3.3 %shard_map.83 = (f32[64,1024]{1,0:T(8,128)}, f32[64,1024]{1,0:T(8,128)}) custom-call(f32[64,1024]{1,0:T(8,128)} %reshape.105.cur_ref, f32[16,1024]{1,0:T(8,128)} %copy-done.4, f32[16,1024]{1,0:T(8,128)} %copy-done.5, f32[64,128]{1,0:T(8,128)} %copy-done.8, f32[64,128]{1,0:T(8,128)} %copy-done.9, f32[64,128]{1,0:T(8,128)} %copy-done.10, ...), custom_call_target="tpu_custom_call" | custom-call | tf_op jit(solution)/shard_map/pallas_call | solution.py:208
  52.5 1.0 copy-done.1
  53.5 9.6 %shard_map.84 = (f32[64,1024]{1,0:T(8,128)}, bf16[32,16,1024]{2,1,0:T(8,128)(2,1)}, f32[64,128]{1,0:T(8,128)}, f32[64,128]{1,0:T(8,128)}, f32[64,128]{1,0:T(8,128)}, /*index=5*/f32[64,128]{1,0:T(8,128)}) custom-call(s32[64]{0:T(128)} %reshape.104.plist_ref, bf16[256,512]{1,0:T(8,128)(2,1)} %mul.20.sel_ref, bf16[512,1024]{1,0:T(8,128)(2,1)} %bitcast.35, ...), custom_call_target="tpu_custom_call" | custom-call | tf_op jit(solution)/shard_map/pallas_call | solution.py:181
  63.1 8.4 %all-to-all-start.1 = ((bf16[32,16,1024]{2,1,0:T(8,128)(2,1)}), bf16[32,16,1024]{2,1,0:T(8,128)(2,1)S(1)}, u32[]{:S(2)}, u32[]{:S(2)}) async-start(bf16[32,16,1024]{2,1,0:T(8,128)(2,1)} %get-tuple-element.27), calls=%async_computation.1 | async-start | bytes 2097152 | tf_op jit(solution)/shard_map/all_to_all | solution.py:271
  71.5 0.9 fusion.3
  73.1 3.1 %collective-permute-start.9 = (f32[64,128]{1,0:T(8,128)}, f32[64,128]{1,0:T(8,128)S(1)}, u32[]{:S(2)}, u32[]{:S(2)}) collective-permute-start(f32[64,128]{1,0:T(8,128)} %get-tuple-element.30), channel_id=1, source_target_pairs={{0,32},{32,64},{64,96},{96,0},{1,33},{33,65},{65,97},{97,1},{2,34}... | collective-permute-start | bytes 98312 | tf_op jit(solution)/shard_map/ppermute | solution.py:267
  76.2 5.2 %collective-permute-start.10 = (f32[64,128]{1,0:T(8,128)}, f32[64,128]{1,0:T(8,128)S(1)}, u32[]{:S(2)}, u32[]{:S(2)}) collective-permute-start(f32[64,128]{1,0:T(8,128)} %get-tuple-element.31), channel_id=1, source_target_pairs={{1,0},{2,1},{3,2},{4,3},{5,4},{6,5},{7,6},{8,7},{9,8},{10,9},{11,1... | collective-permute-start | bytes 98312 | tf_op jit(solution)/shard_map/ppermute | solution.py:270
  81.4 10.7 %collective-permute-done.10.hzp_ref = f32[64,128]{1,0:T(8,128)S(1)} collective-permute-done((f32[64,128]{1,0:T(8,128)}, f32[64,128]{1,0:T(8,128)S(1)}, u32[]{:S(2)}, u32[]{:S(2)}) %collective-permute-start.10) | collective-permute-done | bytes 32800 | tf_op jit(solution)/shard_map/ppermute | solution.py:270
  92.1 6.4 %collective-permute-done.11.hzm_ref = f32[64,128]{1,0:T(8,128)S(1)} collective-permute-done((f32[64,128]{1,0:T(8,128)}, f32[64,128]{1,0:T(8,128)S(1)}, u32[]{:S(2)}, u32[]{:S(2)}) %collective-permute-start.11) | collective-permute-done | bytes 32800 | tf_op jit(solution)/shard_map/ppermute | solution.py:269
  98.6 0.6 copy-done.15
  99.2 0.6 copy-done.7
  99.8 3.3 %shard_map.85 = (f32[64,1024]{1,0:T(8,128)}, f32[64,1024]{1,0:T(8,128)}) custom-call(f32[64,1024]{1,0:T(8,128)} %get-tuple-element.28.cur_ref, f32[16,1024]{1,0:T(8,128)} %copy-done.6, f32[16,1024]{1,0:T(8,128)} %copy-done.7, f32[64,128]{1,0:T(8,128)} %copy-done.11, f32[64,128]{1,0:T(8,128)} %copy-done.12, f32[64,128]{1,0:T(8,128)} %copy-done.13, ...), custom_call_target="tpu_custom_call" | custom-call | tf_op jit(solution)/shard_map/pallas_call | solution.py:208
  103.1 1.0 copy-done.2
  104.0 8.0 %shard_map.86 = f32[64,1024]{1,0:T(8,128)} custom-call(s32[64]{0:T(128)} %reshape.104.plist_ref, bf16[256,512]{1,0:T(8,128)(2,1)} %mul.20.sel_ref, bf16[512,1024]{1,0:T(8,128)(2,1)} %bitcast.36, f32[64,1024]{1,0:T(8,128)} %get-tuple-element.33.p_ref, f32[64,1024]{1,0:T(8,128)} %get-tuple-element.34.q_ref, bf16[4,1024,1024]{2,1,0:T(8,128)(2,1)} %w_ref.3), custom_call_target="tpu_custom_call" | custom-call | tf_op jit(solution)/shard_map/pallas_call | solution.py:181
  112.0 3.0 %reshape.112 = f32[8,8,4,16,16]{4,3,2,1,0:T(8,128)} reshape(f32[64,1024]{1,0:T(8,128)} %shard_map.86) | data formatting | bytes 524288 | tf_op jit(solution)/shard_map/reshape | solution.py:277
  (78 shorter events, 3.5 us)
Async XLA Ops:
  0.0 20.7 %copy-start = (f32[8,8,4,16,16]{4,3,2,1,0:T(8,128)S(1)}, f32[8,8,4,16,16]{4,3,2,1,0:T(8,128)}, u32[]{:S(2)}) copy-start(f32[8,8,4,16,16]{4,3,2,1,0:T(8,128)} %param.8) | copy-start | bytes 786436
  0.0 33.6 %copy-start.16 = (s32[1,1,1,32,2]{3,4,2,1,0:T(2,128)S(1)}, s32[1,1,1,32,2]{3,4,2,1,0:T(2,128)}, u32[]{:S(2)}) copy-start(s32[1,1,1,32,2]{3,4,2,1,0:T(2,128)} %param.13) | copy-start | bytes 772
  0.0 33.7 %copy-start.17 = (s32[1,1,1,32,2]{3,4,2,1,0:T(2,128)S(1)}, s32[1,1,1,32,2]{3,4,2,1,0:T(2,128)}, u32[]{:S(2)}) copy-start(s32[1,1,1,32,2]{3,4,2,1,0:T(2,128)} %param.14) | copy-start | bytes 772
  0.0 34.3 %copy-start.18 = (s32[1,1,1,32]{3,2,1,0:T(1,128)S(1)}, s32[1,1,1,32]{3,2,1,0:T(1,128)}, u32[]{:S(2)}) copy-start(s32[1,1,1,32]{3,2,1,0:T(1,128)} %param.15) | copy-start | bytes 388
  9.1 16.1 %copy-start.22 = (f32[64,128]{1,0:T(8,128)S(1)}, f32[64,128]{1,0:T(8,128)}, u32[]{:S(2)}) copy-start(f32[64,128]{1,0:T(8,128)} %get-tuple-element.21) | copy-start | bytes 98308
  9.1 16.9 %copy-start.21 = (f32[64,128]{1,0:T(8,128)S(1)}, f32[64,128]{1,0:T(8,128)}, u32[]{:S(2)}) copy-start(f32[64,128]{1,0:T(8,128)} %get-tuple-element.22) | copy-start | bytes 98308
  9.1 19.3 %copy-start.20 = (f32[64,128]{1,0:T(8,128)S(1)}, f32[64,128]{1,0:T(8,128)}, u32[]{:S(2)}) copy-start(f32[64,128]{1,0:T(8,128)} %get-tuple-element.23) | copy-start | bytes 98308
  9.1 43.5 %all-to-all-start = ((bf16[32,16,1024]{2,1,0:T(8,128)(2,1)}), bf16[32,16,1024]{2,1,0:T(8,128)(2,1)S(1)}, u32[]{:S(2)}, u32[]{:S(2)}) async-start(bf16[32,16,1024]{2,1,0:T(8,128)(2,1)} %get-tuple-element.20), calls=%async_computation | async-start | bytes 2097152 | tf_op jit(solution)/shard_map/all_to_all | solution.py:271
  21.8 17.6 %copy-start.3 = (f32[8,4,16,16]{3,2,1,0:T(8,128)S(1)}, f32[8,4,16,16]{3,2,1,0:T(8,128)}, u32[]{:S(2)}) copy-start(f32[8,4,16,16]{3,2,1,0:T(8,128)} %param.10) | copy-start | bytes 98308
  23.1 25.4 %collective-permute-start = (f32[16,1024]{1,0:T(8,128)S(1)}, f32[16,1024]{1,0:T(8,128)S(1)}, u32[]{:S(2)}, u32[]{:S(2)}) collective-permute-start(f32[16,1024]{1,0:T(8,128)S(1)} %slice.28), channel_id=1, source_target_pairs={{0,128},{128,0},{1,129},{129,1},{2,130},{130,2},{3,131},{131,3},{4... | collective-permute-start | bytes 196616 | tf_op jit(solution)/shard_map/ppermute | solution.py:265
  23.2 16.5 %copy-start.19 = (f32[64,128]{1,0:T(8,128)S(1)}, f32[64,128]{1,0:T(8,128)}, u32[]{:S(2)}) copy-start(f32[64,128]{1,0:T(8,128)} %get-tuple-element.24) | copy-start | bytes 98308
  24.6 24.0 %collective-permute-start.1 = (f32[16,1024]{1,0:T(8,128)S(1)}, f32[16,1024]{1,0:T(8,128)S(1)}, u32[]{:S(2)}, u32[]{:S(2)}) collective-permute-start(f32[16,1024]{1,0:T(8,128)S(1)} %slice.30), channel_id=1, source_target_pairs={{128,0},{0,128},{129,1},{1,129},{130,2},{2,130},{131,3},{3,131},{1... | collective-permute-start | bytes 196616 | tf_op jit(solution)/shard_map/ppermute | solution.py:266
  25.1 14.6 %collective-permute-start.2 = (f32[64,128]{1,0:T(8,128)S(1)}, f32[64,128]{1,0:T(8,128)S(1)}, u32[]{:S(2)}, u32[]{:S(2)}) collective-permute-start(f32[64,128]{1,0:T(8,128)S(1)} %copy-done.22), channel_id=1, source_target_pairs={{32,0},{64,32},{96,64},{0,96},{33,1},{65,33},{97,65},{1,97},{34,2}... | collective-permute-start | bytes 98312 | tf_op jit(solution)/shard_map/ppermute | solution.py:268
  26.0 22.6 %collective-permute-start.3 = (f32[64,128]{1,0:T(8,128)S(1)}, f32[64,128]{1,0:T(8,128)S(1)}, u32[]{:S(2)}, u32[]{:S(2)}) collective-permute-start(f32[64,128]{1,0:T(8,128)S(1)} %copy-done.21), channel_id=1, source_target_pairs={{0,32},{32,64},{64,96},{96,0},{1,33},{33,65},{65,97},{97,1},{2,34}... | collective-permute-start | bytes 98312 | tf_op jit(solution)/shard_map/ppermute | solution.py:267
  28.4 20.2 %collective-permute-start.4 = (f32[64,128]{1,0:T(8,128)S(1)}, f32[64,128]{1,0:T(8,128)S(1)}, u32[]{:S(2)}, u32[]{:S(2)}) collective-permute-start(f32[64,128]{1,0:T(8,128)S(1)} %copy-done.20), channel_id=1, source_target_pairs={{1,0},{2,1},{3,2},{4,3},{5,4},{6,5},{7,6},{8,7},{9,8},{10,9},{11,1... | collective-permute-start | bytes 98312 | tf_op jit(solution)/shard_map/ppermute | solution.py:270
  39.7 8.9 %copy-start.8 = (f32[64,128]{1,0:T(8,128)}, f32[64,128]{1,0:T(8,128)S(1)}, u32[]{:S(2)}) copy-start(f32[64,128]{1,0:T(8,128)S(1)} %collective-permute-done.2.hyp_ref) | copy-start | bytes 98308
  39.7 8.8 %collective-permute-start.5 = (f32[64,128]{1,0:T(8,128)S(1)}, f32[64,128]{1,0:T(8,128)S(1)}, u32[]{:S(2)}, u32[]{:S(2)}) collective-permute-start(f32[64,128]{1,0:T(8,128)S(1)} %copy-done.19), channel_id=1, source_target_pairs={{0,1},{1,2},{2,3},{3,4},{4,5},{5,6},{6,7},{7,8},{8,9},{9,10},{10,1... | collective-permute-start | bytes 98312 | tf_op jit(solution)/shard_map/ppermute | solution.py:269
  48.6 0.6 copy-start.14
  48.6 0.6 copy-start.5
  52.5 1.0 copy-start.1
  63.1 40.0 %all-to-all-start.1 = ((bf16[32,16,1024]{2,1,0:T(8,128)(2,1)}), bf16[32,16,1024]{2,1,0:T(8,128)(2,1)S(1)}, u32[]{:S(2)}, u32[]{:S(2)}) async-start(bf16[32,16,1024]{2,1,0:T(8,128)(2,1)} %get-tuple-element.27), calls=%async_computation.1 | async-start | bytes 2097152 | tf_op jit(solution)/shard_map/all_to_all | solution.py:271
  72.4 9.0 %collective-permute-start.8 = (f32[64,128]{1,0:T(8,128)}, f32[64,128]{1,0:T(8,128)S(1)}, u32[]{:S(2)}, u32[]{:S(2)}) collective-permute-start(f32[64,128]{1,0:T(8,128)} %get-tuple-element.29), channel_id=1, source_target_pairs={{32,0},{64,32},{96,64},{0,96},{33,1},{65,33},{97,65},{1,97},{34,2}... | collective-permute-start | bytes 98312 | tf_op jit(solution)/shard_map/ppermute | solution.py:268
  72.5 26.1 %collective-permute-start.6 = (f32[16,1024]{1,0:T(8,128)S(1)}, f32[16,1024]{1,0:T(8,128)S(1)}, u32[]{:S(2)}, u32[]{:S(2)}) collective-permute-start(f32[16,1024]{1,0:T(8,128)S(1)} %get-tuple-element.41), channel_id=1, source_target_pairs={{0,128},{128,0},{1,129},{129,1},{2,130},{130,2},{3,131},{131,3},{4... | collective-permute-start | bytes 196616 | tf_op jit(solution)/shard_map/ppermute | solution.py:265
  72.6 26.0 %collective-permute-start.7 = (f32[16,1024]{1,0:T(8,128)S(1)}, f32[16,1024]{1,0:T(8,128)S(1)}, u32[]{:S(2)}, u32[]{:S(2)}) collective-permute-start(f32[16,1024]{1,0:T(8,128)S(1)} %get-tuple-element.40), channel_id=1, source_target_pairs={{128,0},{0,128},{129,1},{1,129},{130,2},{2,130},{131,3},{3,131},{1... | collective-permute-start | bytes 196616 | tf_op jit(solution)/shard_map/ppermute | solution.py:266
  73.1 8.4 %collective-permute-start.9 = (f32[64,128]{1,0:T(8,128)}, f32[64,128]{1,0:T(8,128)S(1)}, u32[]{:S(2)}, u32[]{:S(2)}) collective-permute-start(f32[64,128]{1,0:T(8,128)} %get-tuple-element.30), channel_id=1, source_target_pairs={{0,32},{32,64},{64,96},{96,0},{1,33},{33,65},{65,97},{97,1},{2,34}... | collective-permute-start | bytes 98312 | tf_op jit(solution)/shard_map/ppermute | solution.py:267
  76.2 15.9 %collective-permute-start.10 = (f32[64,128]{1,0:T(8,128)}, f32[64,128]{1,0:T(8,128)S(1)}, u32[]{:S(2)}, u32[]{:S(2)}) collective-permute-start(f32[64,128]{1,0:T(8,128)} %get-tuple-element.31), channel_id=1, source_target_pairs={{1,0},{2,1},{3,2},{4,3},{5,4},{6,5},{7,6},{8,7},{9,8},{10,9},{11,1... | collective-permute-start | bytes 98312 | tf_op jit(solution)/shard_map/ppermute | solution.py:270
  81.4 17.1 %copy-start.11 = (f32[64,128]{1,0:T(8,128)}, f32[64,128]{1,0:T(8,128)S(1)}, u32[]{:S(2)}) copy-start(f32[64,128]{1,0:T(8,128)S(1)} %collective-permute-done.8.hyp_ref) | copy-start | bytes 98308
  81.4 17.1 %collective-permute-start.11 = (f32[64,128]{1,0:T(8,128)}, f32[64,128]{1,0:T(8,128)S(1)}, u32[]{:S(2)}, u32[]{:S(2)}) collective-permute-start(f32[64,128]{1,0:T(8,128)} %get-tuple-element.32), channel_id=1, source_target_pairs={{0,1},{1,2},{2,3},{3,4},{4,5},{5,6},{6,7},{7,8},{8,9},{9,10},{10,1... | collective-permute-start | bytes 98312 | tf_op jit(solution)/shard_map/ppermute | solution.py:269
  81.4 17.1 %copy-start.12 = (f32[64,128]{1,0:T(8,128)}, f32[64,128]{1,0:T(8,128)S(1)}, u32[]{:S(2)}) copy-start(f32[64,128]{1,0:T(8,128)S(1)} %collective-permute-done.9.hym_ref) | copy-start | bytes 98308
  92.1 6.5 %copy-start.13 = (f32[64,128]{1,0:T(8,128)}, f32[64,128]{1,0:T(8,128)S(1)}, u32[]{:S(2)}) copy-start(f32[64,128]{1,0:T(8,128)S(1)} %collective-permute-done.10.hzp_ref) | copy-start | bytes 98308
  98.5 0.6 copy-start.6
  103.1 1.0 copy-start.2
  (5 other events, 3.0 us)

commit v2 on v1

--- a/solution.py
+++ b/solution.py
@@ -72,8 +72,11 @@
         snd_ref[s] = jnp.concatenate(parts, axis=0).astype(BF16)
 
 
-def _prep_kernel(plist_ref, cur_ref, snd_ref, zlo_ref, zhi_ref, ylo_ref, yhi_ref):
+def _send_kernel(plist_ref, cur_ref, snd_ref):
     _emit_send(plist_ref, cur_ref, snd_ref)
+
+
+def _halo_kernel(cur_ref, zlo_ref, zhi_ref, ylo_ref, yhi_ref):
     _emit_halos(cur_ref[...], zlo_ref, zhi_ref, ylo_ref, yhi_ref)
 
 
@@ -81,7 +84,7 @@
     if last:
         cur_ref, g_scr, acc_scr = refs
     else:
-        cur_ref, snd_ref, zlo_ref, zhi_ref, ylo_ref, yhi_ref, g_scr, acc_scr = refs
+        cur_ref, snd_ref, g_scr, acc_scr = refs
     t = pl.program_id(0)
     rows = p_ref.shape[0]
 
@@ -101,7 +104,6 @@
         cur = (p_ref[...] + acc_scr[...]) - q_ref[...]
         cur_ref[...] = cur
         if not last:
-            _emit_halos(cur, zlo_ref, zhi_ref, ylo_ref, yhi_ref)
             _emit_send(plist_ref, cur_ref, snd_ref)
 
 
@@ -151,25 +153,27 @@
     return pl.BlockSpec(shape, lambda *_: zeros)
 
 
-def _rest_shapes(rows, lanes, peers, both):
-    halo = jax.ShapeDtypeStruct((rows, 128), F32)
-    snd = jax.ShapeDtypeStruct((peers, both, lanes), BF16)
-    return [snd, halo, halo, halo, halo]
-
-
-def _prep(plist, cur, peers, both):
-    rows, lanes = cur.shape
-    shapes = _rest_shapes(rows, lanes, peers, both)
+def _send_shape(lanes, peers, both):
+    return jax.ShapeDtypeStruct((peers, both, lanes), BF16)
+
+
+def _send(plist, cur, peers, both):
+    shape = _send_shape(cur.shape[1], peers, both)
     return pl.pallas_call(
-        _prep_kernel,
-        out_shape=shapes,
+        _send_kernel,
+        out_shape=shape,
         grid_spec=pltpu.PrefetchScalarGridSpec(
             num_scalar_prefetch=1,
             grid=(1,),
             in_specs=[_full(cur.shape)],
-            out_specs=[_full(x.shape) for x in shapes],
+            out_specs=_full(shape.shape),
         ),
     )(plist, cur)
+
+
+def _halos(cur):
+    halo = jax.ShapeDtypeStruct((cur.shape[0], 128), F32)
+    return pl.pallas_call(_halo_kernel, out_shape=[halo] * 4)(cur)
 
 
 def _finish(last, plist, sel, inc, p, q, tiles, peers, both):
@@ -177,7 +181,7 @@
     tile_count = tiles.shape[0]
     shapes = [jax.ShapeDtypeStruct((rows, lanes), F32)]
     if not last:
-        shapes += _rest_shapes(rows, lanes, peers, both)
+        shapes.append(_send_shape(lanes, peers, both))
     outs = pl.pallas_call(
         functools.partial(_finish_kernel, last),
         out_shape=shapes,
@@ -238,11 +242,17 @@
         target_ids[None, None] == jnp.arange(width_x, dtype=jnp.int32)[None, :, None, None]
     )
     selector = (tile_match & plane_match & usable[None, None]).astype(BF16)
-    selector = selector.reshape(tile_count * width_x, peer_count * slot_cap)
-    eye = jnp.eye(drive_count, dtype=BF16)
-    sel_big = (selector[:, None, :, None] * eye[None, :, None, :]).reshape(
-        tile_count * width_x * drive_count, peer_count * slot_cap * drive_count
-    )
+    flat_tile = jnp.repeat(tile_ids.reshape(-1), drive_count)
+    flat_target = jnp.repeat(target_ids.reshape(-1), drive_count)
+    flat_usable = jnp.repeat(usable.reshape(-1), drive_count)
+    big_rows = tile_count * width_x * drive_count
+    big_cols = peer_count * slot_cap * drive_count
+    r = lax.broadcasted_iota(jnp.int32, (big_rows, big_cols), 0)
+    col = lax.broadcasted_iota(jnp.int32, (big_rows, big_cols), 1)
+    hit = (r // (width_x * drive_count)) == flat_tile[None, :]
+    hit = hit & (((r // drive_count) % width_x) == flat_target[None, :])
+    hit = hit & flat_usable[None, :] & ((r % drive_count) == (col % drive_count))
+    sel_big = hit.astype(BF16)
     both = slot_cap * drive_count
 
     def spread(a):
@@ -259,9 +269,10 @@
     up_z, down_z = _ring("kz")
 
     cur = populations.reshape(rows, lanes)
-    snd, zlo, zhi, ylo, yhi = _prep(plane_list, cur, peer_count, both)
+    snd = _send(plane_list, cur, peer_count, both)
     for iteration in range(ITERS):
         last = iteration + 1 == ITERS
+        zlo, zhi, ylo, yhi = _halos(cur)
         xlo = lax.ppermute(cur[rows - 16:], "kx", up_x)
         xhi = lax.ppermute(cur[:16], "kx", down_x)
         hym = lax.ppermute(yhi, "ky", up_y)
@@ -273,7 +284,7 @@
         inc = incoming.reshape(peer_count * both, lanes)
         cur, rest = _finish(last, plane_list, sel_big, inc, p, q, tiles, peer_count, both)
         if not last:
-            snd, zlo, zhi, ylo, yhi = rest
+            (snd,) = rest
     return cur.reshape(width_x, drive_count, band_count, width_y, width_z)
 
 

time: 116 us -> 113 us (0.974)
  waiting for transfers between devices: 17.1 us -> 27.4 us
  local copies, waits for them, and re-layouts: 28.6 us -> 18.6 us
  starting transfers between devices: 38.4 us -> 34.2 us
  Pallas kernels: 27.8 us -> 31 us
  other arithmetic: 2.74 us -> 1.32 us
    all_to_all x2, waiting for transfers between devices: 0.01 us -> 13.6 us  [per_device(): lax.all_to_all(snd, 'kz', split_axis=0, concat_axis=0, tiled=True)]
    mul x1 -> x0, local copies, waits for them, and re-layouts: 7.66 us -> none  [per_device(): selector[:, None, :, None] * eye[None, :, None, :]]
    all_to_all x2, starting transfers between devices: 20 us -> 13 us  [per_device(): lax.all_to_all(snd, 'kz', split_axis=0, concat_axis=0, tiled=True)]
    pallas_call x1 -> x3, Pallas kernels: 3.65 us -> 7.98 us  [the longest x2 5.29 us: _halos(): return pl.pallas_call(_halo_kernel, out_shape=[halo] * 4)(cur)]
    ppermute x2, starting transfers between devices: 10.4 us -> 13.5 us  [per_device(): hzp = lax.ppermute(zlo, 'kz', down_z)]
    ppermute x2, waiting for transfers between devices: 10.7 us -> 8.32 us  [per_device(): hzp = lax.ppermute(zlo, 'kz', down_z)]
    mul x1 -> x0, other arithmetic: 2.31 us -> none  [per_device(): selector[:, None, :, None] * eye[None, :, None, :]]
    slice x3, local copies, waits for them, and re-layouts: 3.28 us -> 1.36 us  [per_device(): xhi = lax.ppermute(cur[:16], 'kx', down_x)]
  transfers between devices with their start and end apart: 14 -> 14, of which waited for: 2 -> 3; matrix products, arithmetic and copies ran while one was open for 17% -> 8% of each run, Pallas kernels for 6% -> 10%
where the time goes in v2:
time: 113 us
  starting transfers between devices  34.2 us (30%)
  Pallas kernels  31 us (27%)
  waiting for transfers between devices  27.4 us (24%)
  local copies, waits for them, and re-layouts  18.6 us (16%)
  other arithmetic  1.32 us (1%)
    pallas_call x2, Pallas kernels, _finish(): pl.pallas_call(functools.partial(_finish_kernel, last), out_shape=shapes,...  16.4 us
    all_to_all x2, waiting for transfers between devices, per_device(): lax.all_to_all(snd, 'kz', split_axis=0, concat_axis=0, tiled=True)  13.6 us
    ppermute x2, starting transfers between devices, per_device(): hzp = lax.ppermute(zlo, 'kz', down_z)  13.5 us
    all_to_all x2, starting transfers between devices, per_device(): lax.all_to_all(snd, 'kz', split_axis=0, concat_axis=0, tiled=True)  13 us
    ppermute x2, waiting for transfers between devices, per_device(): hzp = lax.ppermute(zlo, 'kz', down_z)  8.32 us
    pallas_call x2, Pallas kernels, _drift(): pl.pallas_call(_drift_kernel, out_shape=[plane, plane], scratch_shapes=[p...  6.53 us
    ppermute x2, starting transfers between devices, per_device(): hym = lax.ppermute(yhi, 'ky', up_y)  5.54 us
    ppermute x2, waiting for transfers between devices, per_device(): hzm = lax.ppermute(zhi, 'kz', up_z)  5.44 us
  transfers between devices with their start and end apart: 14, of which 3 were waited for; matrix products, arithmetic and copies ran while one was open for 8% of the time, Pallas kernels for 10%

profile of v2, /device:TPU:6, one launch (start us, length us, event | category | flops | bytes accessed | tf_op | source)
XLA Modules:
  0.0 112.8 jit_solution(2727566609325984097)
XLA Ops:
  0.0 3.9 %reshape.43.cur_ref = f32[64,1024]{1,0:T(8,128)} reshape(f32[8,8,4,16,16]{4,3,2,1,0:T(8,128)} %param.8) | data formatting | bytes 524288 | tf_op jit(solution)/shard_map/reshape | solution.py:271
  3.9 2.7 %shard_map.83 = (f32[64,128]{1,0:T(8,128)}, f32[64,128]{1,0:T(8,128)}, f32[64,128]{1,0:T(8,128)}, f32[64,128]{1,0:T(8,128)}) custom-call(f32[64,1024]{1,0:T(8,128)} %reshape.43.cur_ref), custom_call_target="tpu_custom_call" | custom-call | tf_op jit(solution)/shard_map/pallas_call | solution.py:176
  6.6 0.8 collective-permute-start.2
  7.4 2.4 %collective-permute-start.3 = (f32[64,128]{1,0:T(8,128)}, f32[64,128]{1,0:T(8,128)S(1)}, u32[]{:S(2)}, u32[]{:S(2)}) collective-permute-start(f32[64,128]{1,0:T(8,128)} %get-tuple-element.20), channel_id=1, source_target_pairs={{0,32},{32,64},{64,96},{96,0},{1,33},{33,65},{65,97},{97,1},{2,34}... | collective-permute-start | bytes 98312 | tf_op jit(solution)/shard_map/ppermute | solution.py:278
  9.8 8.3 %collective-permute-start.4 = (f32[64,128]{1,0:T(8,128)}, f32[64,128]{1,0:T(8,128)S(1)}, u32[]{:S(2)}, u32[]{:S(2)}) collective-permute-start(f32[64,128]{1,0:T(8,128)} %get-tuple-element.21), channel_id=1, source_target_pairs={{1,0},{2,1},{3,2},{4,3},{5,4},{6,5},{7,6},{8,7},{9,8},{10,9},{11,1... | collective-permute-start | bytes 98312 | tf_op jit(solution)/shard_map/ppermute | solution.py:281
  18.2 0.7 reshape.42.plist_ref
  18.9 2.7 %shard_map.82 = bf16[32,16,1024]{2,1,0:T(8,128)(2,1)} custom-call(s32[64]{0:T(128)} %reshape.42.plist_ref, f32[64,1024]{1,0:T(8,128)} %reshape.43.cur_ref), custom_call_target="tpu_custom_call" | custom-call | tf_op jit(solution)/shard_map/pallas_call | solution.py:162
  21.6 7.3 %all-to-all-start = ((bf16[32,16,1024]{2,1,0:T(8,128)(2,1)}), bf16[32,16,1024]{2,1,0:T(8,128)(2,1)S(1)}, u32[]{:S(2)}, u32[]{:S(2)}) async-start(bf16[32,16,1024]{2,1,0:T(8,128)(2,1)} %shard_map.82), calls=%async_computation | async-start | bytes 2097152 | tf_op jit(solution)/shard_map/all_to_all | solution.py:282
  28.8 1.1 fusion.14
  29.9 1.3 %slice.28 = f32[16,1024]{1,0:T(8,128)S(1)} reshape(f32[2,8,4,16,16]{4,3,2,1,0:T(8,128)} %get-tuple-element.34) | data formatting | bytes 131072 | tf_op jit(solution)/shard_map/slice | solution.py:276
  31.5 1.2 %fusion.15 = (f32[8,1,4,16,16]{4,3,2,1,0:T(8,128)S(1)}, f32[8,1,4,16,16]{4,3,2,1,0:T(8,128)S(1)}, f32[8,1,4,16,16]{4,3,2,1,0:T(8,128)S(1)}) fusion(f32[8,3,4,16,16]{4,3,2,1,0:T(8,128)} %param.9), kind=kLoop, calls=%fused_computation.37 | loop fusion | bytes 196608 | tf_op jit(solution)/shard_map/slice | solution.py:264
  33.3 0.8 broadcast_bitcast_fusion.2
  34.2 0.9 broadcast_bitcast_fusion
  36.4 0.6 collective-permute-start.1
  37.0 1.2 %fusion.3.sel_ref = bf16[256,512]{1,0:T(8,128)(2,1)} fusion(s32[512]{0:T(512)S(1)} %get-tuple-element.40, s32[512]{0:T(512)S(1)} %get-tuple-element.41, s32[256]{0:T(256)S(1)} %get-tuple-element.46, s32[256]{0:T(256)S(1)} %get-tuple-element.47, s32[512]{0:T(512)S(1)} %eq.30, s32[256]{0:T(256)S(1)} %get-tuple-element.43, s32[256]{0:T(256)S(1)} %get-tuple-element.48, ...), kind=kLoop, calls=%fused_computation.10 | loop fusion | flops 2883584 | bytes 278272 | tf_op jit(solution)/shard_map/convert_element_type | solution.py:255
  38.3 0.5 copy-done.11
  38.9 3.3 %shard_map.84 = (f32[64,1024]{1,0:T(8,128)}, f32[64,1024]{1,0:T(8,128)}) custom-call(f32[64,1024]{1,0:T(8,128)} %reshape.43.cur_ref, f32[16,1024]{1,0:T(8,128)} %copy-done.6, f32[16,1024]{1,0:T(8,128)} %copy-done.7, f32[64,128]{1,0:T(8,128)} %copy-done.10, f32[64,128]{1,0:T(8,128)} %copy-done.11, f32[64,128]{1,0:T(8,128)} %copy-done.12, ...), custom_call_target="tpu_custom_call" | custom-call | tf_op jit(solution)/shard_map/pallas_call | solution.py:212
  42.1 13.6 %all-to-all-done = bf16[32,16,1024]{2,1,0:T(8,128)(2,1)S(1)} async-done(((bf16[32,16,1024]{2,1,0:T(8,128)(2,1)}), bf16[32,16,1024]{2,1,0:T(8,128)(2,1)S(1)}, u32[]{:S(2)}, u32[]{:S(2)}) %all-to-all-start) | async-done | bytes 1048608 | tf_op jit(solution)/shard_map/all_to_all | solution.py:282
  55.8 1.0 copy-done.1
  56.7 8.5 %shard_map.85 = (f32[64,1024]{1,0:T(8,128)}, bf16[32,16,1024]{2,1,0:T(8,128)(2,1)}) custom-call(s32[64]{0:T(128)} %reshape.42.plist_ref, bf16[256,512]{1,0:T(8,128)(2,1)} %fusion.3.sel_ref, bf16[512,1024]{1,0:T(8,128)(2,1)} %bitcast.31, f32[64,1024]{1,0:T(8,128)} %get-tuple-element.23.p_ref, f32[64,1024]{1,0:T(8,128)} %get-tuple-element.24.q_ref, ...), custom_call_target="tpu_custom_call" | custom-call | tf_op jit(solution)/shard_map/pallas_call | solution.py:185
  65.2 5.7 %all-to-all-start.1 = ((bf16[32,16,1024]{2,1,0:T(8,128)(2,1)}), bf16[32,16,1024]{2,1,0:T(8,128)(2,1)S(1)}, u32[]{:S(2)}, u32[]{:S(2)}) async-start(bf16[32,16,1024]{2,1,0:T(8,128)(2,1)} %get-tuple-element.25), calls=%async_computation.1 | async-start | bytes 2097152 | tf_op jit(solution)/shard_map/all_to_all | solution.py:282
  70.9 2.6 %shard_map.86 = (f32[64,128]{1,0:T(8,128)}, f32[64,128]{1,0:T(8,128)}, f32[64,128]{1,0:T(8,128)}, f32[64,128]{1,0:T(8,128)}) custom-call(f32[64,1024]{1,0:T(8,128)} %get-tuple-element.26.cur_ref), custom_call_target="tpu_custom_call" | custom-call | tf_op jit(solution)/shard_map/pallas_call | solution.py:176
  74.2 3.1 %collective-permute-start.9 = (f32[64,128]{1,0:T(8,128)}, f32[64,128]{1,0:T(8,128)S(1)}, u32[]{:S(2)}, u32[]{:S(2)}) collective-permute-start(f32[64,128]{1,0:T(8,128)} %get-tuple-element.28), channel_id=1, source_target_pairs={{0,32},{32,64},{64,96},{96,0},{1,33},{33,65},{65,97},{97,1},{2,34}... | collective-permute-start | bytes 98312 | tf_op jit(solution)/shard_map/ppermute | solution.py:278
  77.3 5.2 %collective-permute-start.10 = (f32[64,128]{1,0:T(8,128)}, f32[64,128]{1,0:T(8,128)S(1)}, u32[]{:S(2)}, u32[]{:S(2)}) collective-permute-start(f32[64,128]{1,0:T(8,128)} %get-tuple-element.29), channel_id=1, source_target_pairs={{1,0},{2,1},{3,2},{4,3},{5,4},{6,5},{7,6},{8,7},{9,8},{10,9},{11,1... | collective-permute-start | bytes 98312 | tf_op jit(solution)/shard_map/ppermute | solution.py:281
  82.6 8.3 %collective-permute-done.10.hzp_ref = f32[64,128]{1,0:T(8,128)S(1)} collective-permute-done((f32[64,128]{1,0:T(8,128)}, f32[64,128]{1,0:T(8,128)S(1)}, u32[]{:S(2)}, u32[]{:S(2)}) %collective-permute-start.10) | collective-permute-done | bytes 32800 | tf_op jit(solution)/shard_map/ppermute | solution.py:281
  90.9 5.4 %collective-permute-done.11.hzm_ref = f32[64,128]{1,0:T(8,128)S(1)} collective-permute-done((f32[64,128]{1,0:T(8,128)}, f32[64,128]{1,0:T(8,128)S(1)}, u32[]{:S(2)}, u32[]{:S(2)}) %collective-permute-start.11) | collective-permute-done | bytes 32800 | tf_op jit(solution)/shard_map/ppermute | solution.py:280
  96.4 0.6 copy-done.17
  97.0 0.6 copy-done.9
  97.6 3.3 %shard_map.87 = (f32[64,1024]{1,0:T(8,128)}, f32[64,1024]{1,0:T(8,128)}) custom-call(f32[64,1024]{1,0:T(8,128)} %get-tuple-element.26.cur_ref, f32[16,1024]{1,0:T(8,128)} %copy-done.9, f32[16,1024]{1,0:T(8,128)} %copy-done.8, f32[64,128]{1,0:T(8,128)} %copy-done.14, f32[64,128]{1,0:T(8,128)} %copy-done.15, f32[64,128]{1,0:T(8,128)} %copy-done.16, ...), custom_call_target="tpu_custom_call" | custom-call | tf_op jit(solution)/shard_map/pallas_call | solution.py:212
  100.9 1.0 copy-done.2
  101.9 8.0 %shard_map.88 = f32[64,1024]{1,0:T(8,128)} custom-call(s32[64]{0:T(128)} %reshape.42.plist_ref, bf16[256,512]{1,0:T(8,128)(2,1)} %fusion.3.sel_ref, bf16[512,1024]{1,0:T(8,128)(2,1)} %bitcast.32, f32[64,1024]{1,0:T(8,128)} %get-tuple-element.31.p_ref, f32[64,1024]{1,0:T(8,128)} %get-tuple-element.32.q_ref, bf16[4,1024,1024]{2,1,0:T(8,128)(2,1)} %w_ref.3), custom_call_target="tpu_custom_call" | custom-call | tf_op jit(solution)/shard_map/pallas_call | solution.py:185
  109.8 3.0 %reshape.50 = f32[8,8,4,16,16]{4,3,2,1,0:T(8,128)} reshape(f32[64,1024]{1,0:T(8,128)} %shard_map.88) | data formatting | bytes 524288 | tf_op jit(solution)/shard_map/reshape | solution.py:288
  (82 shorter events, 3.1 us)
Async XLA Ops:
  0.0 18.1 %copy-start.18 = (s32[1,1,1,32,2]{3,4,2,1,0:T(2,128)S(1)}, s32[1,1,1,32,2]{3,4,2,1,0:T(2,128)}, u32[]{:S(2)}) copy-start(s32[1,1,1,32,2]{3,4,2,1,0:T(2,128)} %param.12) | copy-start | bytes 772
  3.9 25.0 %copy-start = (f32[8,8,4,16,16]{4,3,2,1,0:T(8,128)S(1)}, f32[8,8,4,16,16]{4,3,2,1,0:T(8,128)}, u32[]{:S(2)}) copy-start(f32[8,8,4,16,16]{4,3,2,1,0:T(8,128)} %param.8) | copy-start | bytes 786436
  6.6 29.8 %collective-permute-start.2 = (f32[64,128]{1,0:T(8,128)}, f32[64,128]{1,0:T(8,128)S(1)}, u32[]{:S(2)}, u32[]{:S(2)}) collective-permute-start(f32[64,128]{1,0:T(8,128)} %get-tuple-element.19), channel_id=1, source_target_pairs={{32,0},{64,32},{96,64},{0,96},{33,1},{65,33},{97,65},{1,97},{34,2}... | collective-permute-start | bytes 98312 | tf_op jit(solution)/shard_map/ppermute | solution.py:279
  7.4 30.8 %collective-permute-start.3 = (f32[64,128]{1,0:T(8,128)}, f32[64,128]{1,0:T(8,128)S(1)}, u32[]{:S(2)}, u32[]{:S(2)}) collective-permute-start(f32[64,128]{1,0:T(8,128)} %get-tuple-element.20), channel_id=1, source_target_pairs={{0,32},{32,64},{64,96},{96,0},{1,33},{33,65},{65,97},{97,1},{2,34}... | collective-permute-start | bytes 98312 | tf_op jit(solution)/shard_map/ppermute | solution.py:278
  9.8 28.4 %collective-permute-start.4 = (f32[64,128]{1,0:T(8,128)}, f32[64,128]{1,0:T(8,128)S(1)}, u32[]{:S(2)}, u32[]{:S(2)}) collective-permute-start(f32[64,128]{1,0:T(8,128)} %get-tuple-element.21), channel_id=1, source_target_pairs={{1,0},{2,1},{3,2},{4,3},{5,4},{6,5},{7,6},{8,7},{9,8},{10,9},{11,1... | collective-permute-start | bytes 98312 | tf_op jit(solution)/shard_map/ppermute | solution.py:281
  18.1 20.1 %collective-permute-start.5 = (f32[64,128]{1,0:T(8,128)}, f32[64,128]{1,0:T(8,128)S(1)}, u32[]{:S(2)}, u32[]{:S(2)}) collective-permute-start(f32[64,128]{1,0:T(8,128)} %get-tuple-element.22), channel_id=1, source_target_pairs={{0,1},{1,2},{2,3},{3,4},{4,5},{5,6},{6,7},{7,8},{8,9},{9,10},{10,1... | collective-permute-start | bytes 98312 | tf_op jit(solution)/shard_map/ppermute | solution.py:280
  21.6 9.8 %copy-start.5 = (f32[8,4,16,16]{3,2,1,0:T(8,128)S(1)}, f32[8,4,16,16]{3,2,1,0:T(8,128)}, u32[]{:S(2)}) copy-start(f32[8,4,16,16]{3,2,1,0:T(8,128)} %param.10) | copy-start | bytes 98308
  21.6 34.2 %all-to-all-start = ((bf16[32,16,1024]{2,1,0:T(8,128)(2,1)}), bf16[32,16,1024]{2,1,0:T(8,128)(2,1)S(1)}, u32[]{:S(2)}, u32[]{:S(2)}) async-start(bf16[32,16,1024]{2,1,0:T(8,128)(2,1)} %shard_map.82), calls=%async_computation | async-start | bytes 2097152 | tf_op jit(solution)/shard_map/all_to_all | solution.py:282
  29.9 3.3 %copy-start.21 = (s32[1,1,1,32]{3,2,1,0:T(1,128)S(1)}, s32[1,1,1,32]{3,2,1,0:T(1,128)}, u32[]{:S(2)}) copy-start(s32[1,1,1,32]{3,2,1,0:T(1,128)} %param.15) | copy-start | bytes 388
  31.2 4.1 %copy-start.19 = (s32[1,1,1,32,2]{3,4,2,1,0:T(2,128)S(1)}, s32[1,1,1,32,2]{3,4,2,1,0:T(2,128)}, u32[]{:S(2)}) copy-start(s32[1,1,1,32,2]{3,4,2,1,0:T(2,128)} %param.13) | copy-start | bytes 772
  31.3 4.3 %copy-start.20 = (s32[1,1,1,32,2]{3,4,2,1,0:T(2,128)S(1)}, s32[1,1,1,32,2]{3,4,2,1,0:T(2,128)}, u32[]{:S(2)}) copy-start(s32[1,1,1,32,2]{3,4,2,1,0:T(2,128)} %param.14) | copy-start | bytes 772
  31.3 4.8 %copy-start.3 = (f32[2,8,4,16,16]{4,3,2,1,0:T(8,128)S(1)}, f32[2,8,4,16,16]{4,3,2,1,0:T(8,128)}, u32[]{:S(2)}) copy-start(f32[2,8,4,16,16]{4,3,2,1,0:T(8,128)} %get-tuple-element.33) | copy-start | bytes 196612
  31.3 6.9 %collective-permute-start = (f32[16,1024]{1,0:T(8,128)S(1)}, f32[16,1024]{1,0:T(8,128)S(1)}, u32[]{:S(2)}, u32[]{:S(2)}) collective-permute-start(f32[16,1024]{1,0:T(8,128)S(1)} %slice.28), channel_id=1, source_target_pairs={{0,128},{128,0},{1,129},{129,1},{2,130},{130,2},{3,131},{131,3},{4... | collective-permute-start | bytes 196616 | tf_op jit(solution)/shard_map/ppermute | solution.py:276
  36.4 1.9 %copy-start.10 = (f32[64,128]{1,0:T(8,128)}, f32[64,128]{1,0:T(8,128)S(1)}, u32[]{:S(2)}) copy-start(f32[64,128]{1,0:T(8,128)S(1)} %collective-permute-done.2.hyp_ref) | copy-start | bytes 98308
  36.4 1.9 %collective-permute-start.1 = (f32[16,1024]{1,0:T(8,128)S(1)}, f32[16,1024]{1,0:T(8,128)S(1)}, u32[]{:S(2)}, u32[]{:S(2)}) collective-permute-start(f32[16,1024]{1,0:T(8,128)S(1)} %slice.30), channel_id=1, source_target_pairs={{128,0},{0,128},{129,1},{1,129},{130,2},{2,130},{131,3},{3,131},{1... | collective-permute-start | bytes 196616 | tf_op jit(solution)/shard_map/ppermute | solution.py:277
  38.2 0.6 copy-start.6
  38.2 0.6 copy-start.7
  55.8 1.0 copy-start.1
  65.2 8.3 %copy-start.4 = (f32[64,1024]{1,0:T(8,128)S(1)}, f32[64,1024]{1,0:T(8,128)}, u32[]{:S(2)}) copy-start(f32[64,1024]{1,0:T(8,128)} %get-tuple-element.26.cur_ref) | copy-start | bytes 786436
  65.2 35.7 %all-to-all-start.1 = ((bf16[32,16,1024]{2,1,0:T(8,128)(2,1)}), bf16[32,16,1024]{2,1,0:T(8,128)(2,1)S(1)}, u32[]{:S(2)}, u32[]{:S(2)}) async-start(bf16[32,16,1024]{2,1,0:T(8,128)(2,1)} %get-tuple-element.25), calls=%async_computation.1 | async-start | bytes 2097152 | tf_op jit(solution)/shard_map/all_to_all | solution.py:282
  73.5 9.0 %collective-permute-start.8 = (f32[64,128]{1,0:T(8,128)}, f32[64,128]{1,0:T(8,128)S(1)}, u32[]{:S(2)}, u32[]{:S(2)}) collective-permute-start(f32[64,128]{1,0:T(8,128)} %get-tuple-element.27), channel_id=1, source_target_pairs={{32,0},{64,32},{96,64},{0,96},{33,1},{65,33},{97,65},{1,97},{34,2}... | collective-permute-start | bytes 98312 | tf_op jit(solution)/shard_map/ppermute | solution.py:279
  73.6 22.7 %collective-permute-start.7 = (f32[16,1024]{1,0:T(8,128)S(1)}, f32[16,1024]{1,0:T(8,128)S(1)}, u32[]{:S(2)}, u32[]{:S(2)}) collective-permute-start(f32[16,1024]{1,0:T(8,128)S(1)} %get-tuple-element.38), channel_id=1, source_target_pairs={{128,0},{0,128},{129,1},{1,129},{130,2},{2,130},{131,3},{3,131},{1... | collective-permute-start | bytes 196616 | tf_op jit(solution)/shard_map/ppermute | solution.py:277
  73.7 22.6 %collective-permute-start.6 = (f32[16,1024]{1,0:T(8,128)S(1)}, f32[16,1024]{1,0:T(8,128)S(1)}, u32[]{:S(2)}, u32[]{:S(2)}) collective-permute-start(f32[16,1024]{1,0:T(8,128)S(1)} %get-tuple-element.39), channel_id=1, source_target_pairs={{0,128},{128,0},{1,129},{129,1},{2,130},{130,2},{3,131},{131,3},{4... | collective-permute-start | bytes 196616 | tf_op jit(solution)/shard_map/ppermute | solution.py:276
  74.2 8.4 %collective-permute-start.9 = (f32[64,128]{1,0:T(8,128)}, f32[64,128]{1,0:T(8,128)S(1)}, u32[]{:S(2)}, u32[]{:S(2)}) collective-permute-start(f32[64,128]{1,0:T(8,128)} %get-tuple-element.28), channel_id=1, source_target_pairs={{0,32},{32,64},{64,96},{96,0},{1,33},{33,65},{65,97},{97,1},{2,34}... | collective-permute-start | bytes 98312 | tf_op jit(solution)/shard_map/ppermute | solution.py:278
  77.3 13.6 %collective-permute-start.10 = (f32[64,128]{1,0:T(8,128)}, f32[64,128]{1,0:T(8,128)S(1)}, u32[]{:S(2)}, u32[]{:S(2)}) collective-permute-start(f32[64,128]{1,0:T(8,128)} %get-tuple-element.29), channel_id=1, source_target_pairs={{1,0},{2,1},{3,2},{4,3},{5,4},{6,5},{7,6},{8,7},{9,8},{10,9},{11,1... | collective-permute-start | bytes 98312 | tf_op jit(solution)/shard_map/ppermute | solution.py:281
  82.6 13.8 %copy-start.14 = (f32[64,128]{1,0:T(8,128)}, f32[64,128]{1,0:T(8,128)S(1)}, u32[]{:S(2)}) copy-start(f32[64,128]{1,0:T(8,128)S(1)} %collective-permute-done.8.hyp_ref) | copy-start | bytes 98308
  82.6 13.8 %collective-permute-start.11 = (f32[64,128]{1,0:T(8,128)}, f32[64,128]{1,0:T(8,128)S(1)}, u32[]{:S(2)}, u32[]{:S(2)}) collective-permute-start(f32[64,128]{1,0:T(8,128)} %get-tuple-element.30), channel_id=1, source_target_pairs={{0,1},{1,2},{2,3},{3,4},{4,5},{5,6},{6,7},{7,8},{8,9},{9,10},{10,1... | collective-permute-start | bytes 98312 | tf_op jit(solution)/shard_map/ppermute | solution.py:280
  82.6 13.8 %copy-start.15 = (f32[64,128]{1,0:T(8,128)}, f32[64,128]{1,0:T(8,128)S(1)}, u32[]{:S(2)}) copy-start(f32[64,128]{1,0:T(8,128)S(1)} %collective-permute-done.9.hym_ref) | copy-start | bytes 98308
  90.9 5.5 %copy-start.16 = (f32[64,128]{1,0:T(8,128)}, f32[64,128]{1,0:T(8,128)S(1)}, u32[]{:S(2)}) copy-start(f32[64,128]{1,0:T(8,128)S(1)} %collective-permute-done.10.hzp_ref) | copy-start | bytes 98308
  96.3 0.6 copy-start.8
  97.0 0.6 copy-start.9
  100.9 1.0 copy-start.2
  (4 other events, 2.4 us)

commit v3 on v2

--- a/solution.py
+++ b/solution.py
@@ -61,26 +61,23 @@
     yhi_ref[...] = _compress(cur, "y_hi")
 
 
-def _emit_send(plist_ref, cur_ref, snd_ref):
-    peers, both, _ = snd_ref.shape
-    slot_cap = both // 8
-    for s in range(peers):
-        parts = []
-        for c in range(slot_cap):
-            plane = plist_ref[s * slot_cap + c]
-            parts.append(cur_ref[pl.ds(pl.multiple_of(plane * 8, 8), 8), :])
-        snd_ref[s] = jnp.concatenate(parts, axis=0).astype(BF16)
-
-
-def _send_kernel(plist_ref, cur_ref, snd_ref):
-    _emit_send(plist_ref, cur_ref, snd_ref)
+def _emit_send(pick_ref, cur, snd_ref):
+    snd_ref[...] = jnp.dot(
+        pick_ref[...], cur.astype(BF16), preferred_element_type=F32
+    ).astype(BF16)
+
+
+def _prep_kernel(pick_ref, cur_ref, snd_ref, zlo_ref, zhi_ref, ylo_ref, yhi_ref):
+    cur = cur_ref[...]
+    _emit_send(pick_ref, cur, snd_ref)
+    _emit_halos(cur, zlo_ref, zhi_ref, ylo_ref, yhi_ref)
 
 
 def _halo_kernel(cur_ref, zlo_ref, zhi_ref, ylo_ref, yhi_ref):
     _emit_halos(cur_ref[...], zlo_ref, zhi_ref, ylo_ref, yhi_ref)
 
 
-def _finish_kernel(last, plist_ref, sel_ref, inc_ref, p_ref, q_ref, w_ref, *refs):
+def _finish_kernel(last, pick_ref, sel_ref, inc_ref, p_ref, q_ref, w_ref, *refs):
     if last:
         cur_ref, g_scr, acc_scr = refs
     else:
@@ -104,7 +101,7 @@
         cur = (p_ref[...] + acc_scr[...]) - q_ref[...]
         cur_ref[...] = cur
         if not last:
-            _emit_send(plist_ref, cur_ref, snd_ref)
+            _emit_send(pick_ref, cur, snd_ref)
 
 
 def _deriv(a1, m1, a2, m2):
@@ -154,21 +151,13 @@
 
 
 def _send_shape(lanes, peers, both):
-    return jax.ShapeDtypeStruct((peers, both, lanes), BF16)
-
-
-def _send(plist, cur, peers, both):
-    shape = _send_shape(cur.shape[1], peers, both)
-    return pl.pallas_call(
-        _send_kernel,
-        out_shape=shape,
-        grid_spec=pltpu.PrefetchScalarGridSpec(
-            num_scalar_prefetch=1,
-            grid=(1,),
-            in_specs=[_full(cur.shape)],
-            out_specs=_full(shape.shape),
-        ),
-    )(plist, cur)
+    return jax.ShapeDtypeStruct((peers * both, lanes), BF16)
+
+
+def _prep(pick, cur, peers, both):
+    halo = jax.ShapeDtypeStruct((cur.shape[0], 128), F32)
+    shapes = [_send_shape(cur.shape[1], peers, both)] + [halo] * 4
+    return pl.pallas_call(_prep_kernel, out_shape=shapes)(pick, cur)
 
 
 def _halos(cur):
@@ -176,7 +165,7 @@
     return pl.pallas_call(_halo_kernel, out_shape=[halo] * 4)(cur)
 
 
-def _finish(last, plist, sel, inc, p, q, tiles, peers, both):
+def _finish(last, pick, sel, inc, p, q, tiles, peers, both):
     rows, lanes = p.shape
     tile_count = tiles.shape[0]
     shapes = [jax.ShapeDtypeStruct((rows, lanes), F32)]
@@ -185,24 +174,22 @@
     outs = pl.pallas_call(
         functools.partial(_finish_kernel, last),
         out_shape=shapes,
-        grid_spec=pltpu.PrefetchScalarGridSpec(
-            num_scalar_prefetch=1,
-            grid=(tile_count,),
-            in_specs=[
-                _full(sel.shape),
-                _full(inc.shape),
-                _full(p.shape),
-                _full(q.shape),
-                pl.BlockSpec((1,) + tiles.shape[1:], lambda t, *_: (t, 0, 0)),
-            ],
-            out_specs=[_full(x.shape) for x in shapes],
-            scratch_shapes=[
-                pltpu.VMEM((tile_count * rows, lanes), BF16),
-                pltpu.VMEM((rows, lanes), F32),
-            ],
-        ),
+        grid=(tile_count,),
+        in_specs=[
+            _full(pick.shape),
+            _full(sel.shape),
+            _full(inc.shape),
+            _full(p.shape),
+            _full(q.shape),
+            pl.BlockSpec((1,) + tiles.shape[1:], lambda t: (t, 0, 0)),
+        ],
+        out_specs=[_full(x.shape) for x in shapes],
+        scratch_shapes=[
+            pltpu.VMEM((tile_count * rows, lanes), BF16),
+            pltpu.VMEM((rows, lanes), F32),
+        ],
         compiler_params=pltpu.CompilerParams(dimension_semantics=("arbitrary",)),
-    )(plist, sel, inc, p, q, tiles)
+    )(pick, sel, inc, p, q, tiles)
     return outs[0], outs[1:]
 
 
@@ -254,6 +241,10 @@
     hit = hit & flat_usable[None, :] & ((r % drive_count) == (col % drive_count))
     sel_big = hit.astype(BF16)
     both = slot_cap * drive_count
+    flat_plane = jnp.repeat(plane_list, drive_count)
+    pr = lax.broadcasted_iota(jnp.int32, (peer_count * both, rows), 0)
+    pc = lax.broadcasted_iota(jnp.int32, (peer_count * both, rows), 1)
+    pick = ((flat_plane[:, None] == pc // drive_count) & (pr % drive_count == pc % drive_count)).astype(BF16)
 
     def spread(a):
         a = a.reshape(width_x, 1, lanes)
@@ -269,20 +260,22 @@
     up_z, down_z = _ring("kz")
 
     cur = populations.reshape(rows, lanes)
-    snd = _send(plane_list, cur, peer_count, both)
+    snd, zlo, zhi, ylo, yhi = _prep(pick, cur, peer_count, both)
     for iteration in range(ITERS):
         last = iteration + 1 == ITERS
-        zlo, zhi, ylo, yhi = _halos(cur)
+        if iteration > 0:
+            zlo, zhi, ylo, yhi = _halos(cur)
         xlo = lax.ppermute(cur[rows - 16:], "kx", up_x)
         xhi = lax.ppermute(cur[:16], "kx", down_x)
         hym = lax.ppermute(yhi, "ky", up_y)
         hyp = lax.ppermute(ylo, "ky", down_y)
         hzm = lax.ppermute(zhi, "kz", up_z)
         hzp = lax.ppermute(zlo, "kz", down_z)
-        incoming = lax.all_to_all(snd, "kz", split_axis=0, concat_axis=0, tiled=True)
+        outgoing = snd.reshape(peer_count, both, lanes)
+        incoming = lax.all_to_all(outgoing, "kz", split_axis=0, concat_axis=0, tiled=True)
         p, q = _drift(cur, xlo, xhi, hyp, hym, hzp, hzm, fx, fy, fz, rate_wide)
         inc = incoming.reshape(peer_count * both, lanes)
-        cur, rest = _finish(last, plane_list, sel_big, inc, p, q, tiles, peer_count, both)
+        cur, rest = _finish(last, pick, sel_big, inc, p, q, tiles, peer_count, both)
         if not last:
             (snd,) = rest
     return cur.reshape(width_x, drive_count, band_count, width_y, width_z)

time: 113 us -> 110 us (0.973)
  waiting for transfers between devices: 27.4 us -> 23.4 us
  Pallas kernels: 31 us -> 27.3 us
  starting transfers between devices: 34.2 us -> 36.2 us
  local copies, waits for them, and re-layouts: 18.6 us -> 20.1 us
    all_to_all x2, waiting for transfers between devices: 13.6 us -> 0.01 us  [per_device(): lax.all_to_all(outgoing, 'kz', split_axis=0, concat_axis=0, tiled=True)]
    ppermute x2, waiting for transfers between devices: 5.44 us -> 11.8 us  [per_device(): hzm = lax.ppermute(zhi, 'kz', up_z)]
    all_to_all x2, starting transfers between devices: 13 us -> 17.8 us  [per_device(): lax.all_to_all(outgoing, 'kz', split_axis=0, concat_axis=0, tiled=True)]
    ppermute x2, waiting for transfers between devices: 8.32 us -> 11.6 us  [per_device(): hzp = lax.ppermute(zlo, 'kz', down_z)]
    ppermute x2, starting transfers between devices: 13.5 us -> 10.4 us  [per_device(): hzp = lax.ppermute(zlo, 'kz', down_z)]
    pallas_call x2 -> x1, Pallas kernels: 5.29 us -> 2.57 us  [_halos(): return pl.pallas_call(_halo_kernel, out_shape=[halo] * 4)(cur)]
    unnamed x47 -> x51, local copies, waits for them, and re-layouts: 4.09 us -> 4.78 us
  transfers between devices with their start and end apart: 14 -> 14, of which waited for: 3 -> 4; matrix products, arithmetic and copies ran while one was open for 8% -> 9% of each run, Pallas kernels for 10% -> 8%
where the time goes in v3:
time: 110 us
  starting transfers between devices  36.2 us (33%)
  Pallas kernels  27.3 us (25%)
  waiting for transfers between devices  23.4 us (21%)
  local copies, waits for them, and re-layouts  20.1 us (18%)
  other arithmetic  2.35 us (2%)
    all_to_all x2, starting transfers between devices, per_device(): lax.all_to_all(outgoing, 'kz', split_axis=0, concat_axis=0, tiled=True)  17.8 us
    pallas_call x2, Pallas kernels, _finish(): pl.pallas_call(functools.partial(_finish_kernel, last), out_shape=shapes,...  15.4 us
    ppermute x2, waiting for transfers between devices, per_device(): hzm = lax.ppermute(zhi, 'kz', up_z)  11.8 us
    ppermute x2, waiting for transfers between devices, per_device(): hzp = lax.ppermute(zlo, 'kz', down_z)  11.6 us
    ppermute x2, starting transfers between devices, per_device(): hzp = lax.ppermute(zlo, 'kz', down_z)  10.4 us
    pallas_call x2, Pallas kernels, _drift(): pl.pallas_call(_drift_kernel, out_shape=[plane, plane], scratch_shapes=[p...  6.51 us
    ppermute x2, starting transfers between devices, per_device(): hym = lax.ppermute(yhi, 'ky', up_y)  4.81 us
    unnamed x51, local copies, waits for them, and re-layouts  4.78 us
  transfers between devices with their start and end apart: 14, of which 4 were waited for; matrix products, arithmetic and copies ran while one was open for 9% of the time, Pallas kernels for 8%

profile of v3, /device:TPU:6, one launch (start us, length us, event | category | flops | bytes accessed | tf_op | source)
XLA Modules:
  0.0 109.7 jit_solution(15434788106167682373)
XLA Ops:
  0.0 0.8 copy.12
  1.1 4.0 %reshape.50.cur_ref = f32[64,1024]{1,0:T(8,128)} reshape(f32[8,8,4,16,16]{4,3,2,1,0:T(8,128)} %param.8) | data formatting | bytes 524288 | tf_op jit(solution)/shard_map/reshape | solution.py:262
  5.1 1.0 fusion.7.pick_ref
  6.1 2.8 %shard_map.82 = (bf16[512,1024]{1,0:T(8,128)(2,1)}, f32[64,128]{1,0:T(8,128)}, f32[64,128]{1,0:T(8,128)}, f32[64,128]{1,0:T(8,128)}, f32[64,128]{1,0:T(8,128)}) custom-call(bf16[512,64]{1,0:T(8,128)(2,1)} %fusion.7.pick_ref, f32[64,1024]{1,0:T(8,128)} %reshape.50.cur_ref), custom_call_target="tpu_custom_call" | custom-call | tf_op jit(solution)/shard_map/pallas_call | solution.py:160
  8.9 11.5 %all-to-all-start = ((bf16[32,16,1024]{2,1,0:T(8,128)(2,1)}), bf16[32,16,1024]{2,1,0:T(8,128)(2,1)S(1)}, u32[]{:S(2)}, u32[]{:S(2)}) async-start(bf16[32,16,1024]{2,1,0:T(8,128)(2,1)} %bitcast.35), calls=%async_computation | async-start | bytes 2097152 | tf_op jit(solution)/shard_map/all_to_all | solution.py:275
  20.4 1.1 fusion.16
  21.5 1.3 %slice.28 = f32[16,1024]{1,0:T(8,128)S(1)} reshape(f32[2,8,4,16,16]{4,3,2,1,0:T(8,128)} %get-tuple-element.36) | data formatting | bytes 131072 | tf_op jit(solution)/shard_map/slice | solution.py:268
  23.0 1.3 %slice.30 = f32[16,1024]{1,0:T(8,128)S(1)} reshape(f32[2,8,4,16,16]{4,3,2,1,0:T(8,128)} %get-tuple-element.35) | data formatting | bytes 131072 | tf_op jit(solution)/shard_map/slice | solution.py:269
  24.9 0.8 collective-permute-start.2
  25.7 2.4 %collective-permute-start.3 = (f32[64,128]{1,0:T(8,128)S(1)}, f32[64,128]{1,0:T(8,128)S(1)}, u32[]{:S(2)}, u32[]{:S(2)}) collective-permute-start(f32[64,128]{1,0:T(8,128)S(1)} %copy-done.22), channel_id=1, source_target_pairs={{0,32},{32,64},{64,96},{96,0},{1,33},{33,65},{65,97},{97,1},{2,34}... | collective-permute-start | bytes 98312 | tf_op jit(solution)/shard_map/ppermute | solution.py:270
  28.1 5.2 %collective-permute-start.4 = (f32[64,128]{1,0:T(8,128)S(1)}, f32[64,128]{1,0:T(8,128)S(1)}, u32[]{:S(2)}, u32[]{:S(2)}) collective-permute-start(f32[64,128]{1,0:T(8,128)S(1)} %copy-done.21), channel_id=1, source_target_pairs={{1,0},{2,1},{3,2},{4,3},{5,4},{6,5},{7,6},{8,7},{9,8},{10,9},{11,1... | collective-permute-start | bytes 98312 | tf_op jit(solution)/shard_map/ppermute | solution.py:273
  33.5 1.2 %fusion.17 = (f32[8,1,4,16,16]{4,3,2,1,0:T(8,128)S(1)}, f32[8,1,4,16,16]{4,3,2,1,0:T(8,128)S(1)}, f32[8,1,4,16,16]{4,3,2,1,0:T(8,128)S(1)}) fusion(f32[8,3,4,16,16]{4,3,2,1,0:T(8,128)} %param.9), kind=kLoop, calls=%fused_computation.48 | loop fusion | bytes 196608 | tf_op jit(solution)/shard_map/slice | solution.py:255
  35.3 0.9 broadcast_bitcast_fusion.2
  36.1 0.9 broadcast_bitcast_fusion
  38.3 1.2 %fusion.3.sel_ref = bf16[256,512]{1,0:T(8,128)(2,1)} fusion(s32[512]{0:T(512)S(1)} %get-tuple-element.42, s32[512]{0:T(512)S(1)} %get-tuple-element.43, s32[256]{0:T(256)S(1)} %get-tuple-element.54, s32[256]{0:T(256)S(1)} %get-tuple-element.55, s32[512]{0:T(512)S(1)} %eq.50, s32[256]{0:T(256)S(1)} %get-tuple-element.51, s32[256]{0:T(256)S(1)} %get-tuple-element.56, ...), kind=kLoop, calls=%fused_computation.10 | loop fusion | flops 2883584 | bytes 278272 | tf_op jit(solution)/shard_map/convert_element_type | solution.py:242
  39.6 2.2 %collective-permute-done.4.hzp_ref = f32[64,128]{1,0:T(8,128)S(1)} collective-permute-done((f32[64,128]{1,0:T(8,128)S(1)}, f32[64,128]{1,0:T(8,128)S(1)}, u32[]{:S(2)}, u32[]{:S(2)}) %collective-permute-start.4) | collective-permute-done | bytes 32800 | tf_op jit(solution)/shard_map/ppermute | solution.py:273
  41.8 5.9 %collective-permute-done.5.hzm_ref = f32[64,128]{1,0:T(8,128)S(1)} collective-permute-done((f32[64,128]{1,0:T(8,128)S(1)}, f32[64,128]{1,0:T(8,128)S(1)}, u32[]{:S(2)}, u32[]{:S(2)}) %collective-permute-start.5) | collective-permute-done | bytes 32800 | tf_op jit(solution)/shard_map/ppermute | solution.py:272
  48.4 3.3 %shard_map.83 = (f32[64,1024]{1,0:T(8,128)}, f32[64,1024]{1,0:T(8,128)}) custom-call(f32[64,1024]{1,0:T(8,128)} %reshape.50.cur_ref, f32[16,1024]{1,0:T(8,128)} %copy-done.5, f32[16,1024]{1,0:T(8,128)} %copy-done.6, f32[64,128]{1,0:T(8,128)} %copy-done.9, f32[64,128]{1,0:T(8,128)} %copy-done.10, f32[64,128]{1,0:T(8,128)} %copy-done.11, ...), custom_call_target="tpu_custom_call" | custom-call | tf_op jit(solution)/shard_map/pallas_call | solution.py:199
  51.6 1.0 copy-done.1
  52.6 8.1 %shard_map.84 = (f32[64,1024]{1,0:T(8,128)}, bf16[512,1024]{1,0:T(8,128)(2,1)}) custom-call(bf16[512,64]{1,0:T(8,128)(2,1)} %fusion.7.pick_ref, bf16[256,512]{1,0:T(8,128)(2,1)} %fusion.3.sel_ref, bf16[512,1024]{1,0:T(8,128)(2,1)} %bitcast.33, f32[64,1024]{1,0:T(8,128)} %get-tuple-element.25.p_ref, f32[64,1024]{1,0:T(8,128)} %get-tuple-element.26.q_ref, ...), custom_call_target="tpu_custom_call" | custom-call | tf_op jit(solution)/shard_map/pallas_call | solution.py:174
  60.7 6.3 %all-to-all-start.1 = ((bf16[32,16,1024]{2,1,0:T(8,128)(2,1)}), bf16[32,16,1024]{2,1,0:T(8,128)(2,1)S(1)}, u32[]{:S(2)}, u32[]{:S(2)}) async-start(bf16[32,16,1024]{2,1,0:T(8,128)(2,1)} %bitcast.36), calls=%async_computation.1 | async-start | bytes 2097152 | tf_op jit(solution)/shard_map/all_to_all | solution.py:275
  67.0 2.6 %shard_map.85 = (f32[64,128]{1,0:T(8,128)}, f32[64,128]{1,0:T(8,128)}, f32[64,128]{1,0:T(8,128)}, f32[64,128]{1,0:T(8,128)}) custom-call(f32[64,1024]{1,0:T(8,128)} %get-tuple-element.28.cur_ref), custom_call_target="tpu_custom_call" | custom-call | tf_op jit(solution)/shard_map/pallas_call | solution.py:165
  69.6 0.9 collective-permute-start.8
  71.0 2.4 %collective-permute-start.9 = (f32[64,128]{1,0:T(8,128)}, f32[64,128]{1,0:T(8,128)S(1)}, u32[]{:S(2)}, u32[]{:S(2)}) collective-permute-start(f32[64,128]{1,0:T(8,128)} %get-tuple-element.30), channel_id=1, source_target_pairs={{0,32},{32,64},{64,96},{96,0},{1,33},{33,65},{65,97},{97,1},{2,34}... | collective-permute-start | bytes 98312 | tf_op jit(solution)/shard_map/ppermute | solution.py:270
  73.4 5.2 %collective-permute-start.10 = (f32[64,128]{1,0:T(8,128)}, f32[64,128]{1,0:T(8,128)S(1)}, u32[]{:S(2)}, u32[]{:S(2)}) collective-permute-start(f32[64,128]{1,0:T(8,128)} %get-tuple-element.31), channel_id=1, source_target_pairs={{1,0},{2,1},{3,2},{4,3},{5,4},{6,5},{7,6},{8,7},{9,8},{10,9},{11,1... | collective-permute-start | bytes 98312 | tf_op jit(solution)/shard_map/ppermute | solution.py:273
  78.6 9.4 %collective-permute-done.10.hzp_ref = f32[64,128]{1,0:T(8,128)S(1)} collective-permute-done((f32[64,128]{1,0:T(8,128)}, f32[64,128]{1,0:T(8,128)S(1)}, u32[]{:S(2)}, u32[]{:S(2)}) %collective-permute-start.10) | collective-permute-done | bytes 32800 | tf_op jit(solution)/shard_map/ppermute | solution.py:273
  88.1 5.8 %collective-permute-done.11.hzm_ref = f32[64,128]{1,0:T(8,128)S(1)} collective-permute-done((f32[64,128]{1,0:T(8,128)}, f32[64,128]{1,0:T(8,128)S(1)}, u32[]{:S(2)}, u32[]{:S(2)}) %collective-permute-start.11) | collective-permute-done | bytes 32800 | tf_op jit(solution)/shard_map/ppermute | solution.py:272
  94.6 0.6 copy-done.8
  95.2 3.3 %shard_map.86 = (f32[64,1024]{1,0:T(8,128)}, f32[64,1024]{1,0:T(8,128)}) custom-call(f32[64,1024]{1,0:T(8,128)} %get-tuple-element.28.cur_ref, f32[16,1024]{1,0:T(8,128)} %copy-done.8, f32[16,1024]{1,0:T(8,128)} %copy-done.7, f32[64,128]{1,0:T(8,128)} %copy-done.12, f32[64,128]{1,0:T(8,128)} %copy-done.14, f32[64,128]{1,0:T(8,128)} %copy-done.15, ...), custom_call_target="tpu_custom_call" | custom-call | tf_op jit(solution)/shard_map/pallas_call | solution.py:199
  98.4 1.0 copy-done.2
  99.4 7.3 %shard_map.87 = f32[64,1024]{1,0:T(8,128)} custom-call(bf16[512,64]{1,0:T(8,128)(2,1)} %fusion.7.pick_ref, bf16[256,512]{1,0:T(8,128)(2,1)} %fusion.3.sel_ref, bf16[512,1024]{1,0:T(8,128)(2,1)} %bitcast.34, f32[64,1024]{1,0:T(8,128)} %get-tuple-element.33.p_ref, f32[64,1024]{1,0:T(8,128)} %get-tuple-element.34.q_ref, bf16[4,1024,1024]{2,1,0:T(8,128)(2,1)} %w_ref.3), custom_call_target="tpu_custom_call" | custom-call | tf_op jit(solution)/shard_map/pallas_call | solution.py:174
  106.7 3.0 %reshape.59 = f32[8,8,4,16,16]{4,3,2,1,0:T(8,128)} reshape(f32[64,1024]{1,0:T(8,128)} %shard_map.87) | data formatting | bytes 524288 | tf_op jit(solution)/shard_map/reshape | solution.py:281
  (91 shorter events, 4.8 us)
Async XLA Ops:
  1.1 19.3 %copy-start = (f32[8,8,4,16,16]{4,3,2,1,0:T(8,128)S(1)}, f32[8,8,4,16,16]{4,3,2,1,0:T(8,128)}, u32[]{:S(2)}) copy-start(f32[8,8,4,16,16]{4,3,2,1,0:T(8,128)} %param.8) | copy-start | bytes 786436
  8.9 42.7 %all-to-all-start = ((bf16[32,16,1024]{2,1,0:T(8,128)(2,1)}), bf16[32,16,1024]{2,1,0:T(8,128)(2,1)S(1)}, u32[]{:S(2)}, u32[]{:S(2)}) async-start(bf16[32,16,1024]{2,1,0:T(8,128)(2,1)} %bitcast.35), calls=%async_computation | async-start | bytes 2097152 | tf_op jit(solution)/shard_map/all_to_all | solution.py:275
  20.4 4.5 %copy-start.23 = (f32[64,128]{1,0:T(8,128)S(1)}, f32[64,128]{1,0:T(8,128)}, u32[]{:S(2)}) copy-start(f32[64,128]{1,0:T(8,128)} %get-tuple-element.21) | copy-start | bytes 98308
  20.4 5.3 %copy-start.22 = (f32[64,128]{1,0:T(8,128)S(1)}, f32[64,128]{1,0:T(8,128)}, u32[]{:S(2)}) copy-start(f32[64,128]{1,0:T(8,128)} %get-tuple-element.22) | copy-start | bytes 98308
  20.4 7.7 %copy-start.21 = (f32[64,128]{1,0:T(8,128)S(1)}, f32[64,128]{1,0:T(8,128)}, u32[]{:S(2)}) copy-start(f32[64,128]{1,0:T(8,128)} %get-tuple-element.23) | copy-start | bytes 98308
  20.4 12.9 %copy-start.4 = (f32[8,4,16,16]{3,2,1,0:T(8,128)S(1)}, f32[8,4,16,16]{3,2,1,0:T(8,128)}, u32[]{:S(2)}) copy-start(f32[8,4,16,16]{3,2,1,0:T(8,128)} %param.10) | copy-start | bytes 98308
  21.5 13.6 %copy-start.19 = (s32[1,1,1,32]{3,2,1,0:T(1,128)S(1)}, s32[1,1,1,32]{3,2,1,0:T(1,128)}, u32[]{:S(2)}) copy-start(s32[1,1,1,32]{3,2,1,0:T(1,128)} %param.15) | copy-start | bytes 388
  22.9 24.8 %collective-permute-start = (f32[16,1024]{1,0:T(8,128)S(1)}, f32[16,1024]{1,0:T(8,128)S(1)}, u32[]{:S(2)}, u32[]{:S(2)}) collective-permute-start(f32[16,1024]{1,0:T(8,128)S(1)} %slice.28), channel_id=1, source_target_pairs={{0,128},{128,0},{1,129},{129,1},{2,130},{130,2},{3,131},{131,3},{4... | collective-permute-start | bytes 196616 | tf_op jit(solution)/shard_map/ppermute | solution.py:268
  24.3 13.0 %copy-start.17 = (s32[1,1,1,32,2]{3,4,2,1,0:T(2,128)S(1)}, s32[1,1,1,32,2]{3,4,2,1,0:T(2,128)}, u32[]{:S(2)}) copy-start(s32[1,1,1,32,2]{3,4,2,1,0:T(2,128)} %param.13) | copy-start | bytes 772
  24.3 13.2 %copy-start.18 = (s32[1,1,1,32,2]{3,4,2,1,0:T(2,128)S(1)}, s32[1,1,1,32,2]{3,4,2,1,0:T(2,128)}, u32[]{:S(2)}) copy-start(s32[1,1,1,32,2]{3,4,2,1,0:T(2,128)} %param.14) | copy-start | bytes 772
  24.3 13.8 %copy-start.20 = (f32[64,128]{1,0:T(8,128)S(1)}, f32[64,128]{1,0:T(8,128)}, u32[]{:S(2)}) copy-start(f32[64,128]{1,0:T(8,128)} %get-tuple-element.24) | copy-start | bytes 98308
  24.3 23.4 %collective-permute-start.1 = (f32[16,1024]{1,0:T(8,128)S(1)}, f32[16,1024]{1,0:T(8,128)S(1)}, u32[]{:S(2)}, u32[]{:S(2)}) collective-permute-start(f32[16,1024]{1,0:T(8,128)S(1)} %slice.30), channel_id=1, source_target_pairs={{128,0},{0,128},{129,1},{1,129},{130,2},{2,130},{131,3},{3,131},{1... | collective-permute-start | bytes 196616 | tf_op jit(solution)/shard_map/ppermute | solution.py:269
  24.9 13.1 %collective-permute-start.2 = (f32[64,128]{1,0:T(8,128)S(1)}, f32[64,128]{1,0:T(8,128)S(1)}, u32[]{:S(2)}, u32[]{:S(2)}) collective-permute-start(f32[64,128]{1,0:T(8,128)S(1)} %copy-done.23), channel_id=1, source_target_pairs={{32,0},{64,32},{96,64},{0,96},{33,1},{65,33},{97,65},{1,97},{34,2}... | collective-permute-start | bytes 98312 | tf_op jit(solution)/shard_map/ppermute | solution.py:271
  25.7 13.9 %collective-permute-start.3 = (f32[64,128]{1,0:T(8,128)S(1)}, f32[64,128]{1,0:T(8,128)S(1)}, u32[]{:S(2)}, u32[]{:S(2)}) collective-permute-start(f32[64,128]{1,0:T(8,128)S(1)} %copy-done.22), channel_id=1, source_target_pairs={{0,32},{32,64},{64,96},{96,0},{1,33},{33,65},{65,97},{97,1},{2,34}... | collective-permute-start | bytes 98312 | tf_op jit(solution)/shard_map/ppermute | solution.py:270
  28.1 13.6 %collective-permute-start.4 = (f32[64,128]{1,0:T(8,128)S(1)}, f32[64,128]{1,0:T(8,128)S(1)}, u32[]{:S(2)}, u32[]{:S(2)}) collective-permute-start(f32[64,128]{1,0:T(8,128)S(1)} %copy-done.21), channel_id=1, source_target_pairs={{1,0},{2,1},{3,2},{4,3},{5,4},{6,5},{7,6},{8,7},{9,8},{10,9},{11,1... | collective-permute-start | bytes 98312 | tf_op jit(solution)/shard_map/ppermute | solution.py:273
  38.0 9.7 %copy-start.9 = (f32[64,128]{1,0:T(8,128)}, f32[64,128]{1,0:T(8,128)S(1)}, u32[]{:S(2)}) copy-start(f32[64,128]{1,0:T(8,128)S(1)} %collective-permute-done.2.hyp_ref) | copy-start | bytes 98308
  38.1 9.6 %collective-permute-start.5 = (f32[64,128]{1,0:T(8,128)S(1)}, f32[64,128]{1,0:T(8,128)S(1)}, u32[]{:S(2)}, u32[]{:S(2)}) collective-permute-start(f32[64,128]{1,0:T(8,128)S(1)} %copy-done.20), channel_id=1, source_target_pairs={{0,1},{1,2},{2,3},{3,4},{4,5},{5,6},{6,7},{7,8},{8,9},{9,10},{10,1... | collective-permute-start | bytes 98312 | tf_op jit(solution)/shard_map/ppermute | solution.py:272
  39.6 8.1 %copy-start.10 = (f32[64,128]{1,0:T(8,128)}, f32[64,128]{1,0:T(8,128)S(1)}, u32[]{:S(2)}) copy-start(f32[64,128]{1,0:T(8,128)S(1)} %collective-permute-done.3.hym_ref) | copy-start | bytes 98308
  41.8 6.0 %copy-start.11 = (f32[64,128]{1,0:T(8,128)}, f32[64,128]{1,0:T(8,128)S(1)}, u32[]{:S(2)}) copy-start(f32[64,128]{1,0:T(8,128)S(1)} %collective-permute-done.4.hzp_ref) | copy-start | bytes 98308
  51.6 1.0 copy-start.1
  60.7 8.9 %copy-start.3 = (f32[64,1024]{1,0:T(8,128)S(1)}, f32[64,1024]{1,0:T(8,128)}, u32[]{:S(2)}) copy-start(f32[64,1024]{1,0:T(8,128)} %get-tuple-element.28.cur_ref) | copy-start | bytes 786436
  60.7 37.7 %all-to-all-start.1 = ((bf16[32,16,1024]{2,1,0:T(8,128)(2,1)}), bf16[32,16,1024]{2,1,0:T(8,128)(2,1)S(1)}, u32[]{:S(2)}, u32[]{:S(2)}) async-start(bf16[32,16,1024]{2,1,0:T(8,128)(2,1)} %bitcast.36), calls=%async_computation.1 | async-start | bytes 2097152 | tf_op jit(solution)/shard_map/all_to_all | solution.py:275
  69.6 9.0 %collective-permute-start.8 = (f32[64,128]{1,0:T(8,128)}, f32[64,128]{1,0:T(8,128)S(1)}, u32[]{:S(2)}, u32[]{:S(2)}) collective-permute-start(f32[64,128]{1,0:T(8,128)} %get-tuple-element.29), channel_id=1, source_target_pairs={{32,0},{64,32},{96,64},{0,96},{33,1},{65,33},{97,65},{1,97},{34,2}... | collective-permute-start | bytes 98312 | tf_op jit(solution)/shard_map/ppermute | solution.py:271
  70.5 23.4 %collective-permute-start.7 = (f32[16,1024]{1,0:T(8,128)S(1)}, f32[16,1024]{1,0:T(8,128)S(1)}, u32[]{:S(2)}, u32[]{:S(2)}) collective-permute-start(f32[16,1024]{1,0:T(8,128)S(1)} %get-tuple-element.40), channel_id=1, source_target_pairs={{128,0},{0,128},{129,1},{1,129},{130,2},{2,130},{131,3},{3,131},{1... | collective-permute-start | bytes 196616 | tf_op jit(solution)/shard_map/ppermute | solution.py:269
  70.5 23.4 %collective-permute-start.6 = (f32[16,1024]{1,0:T(8,128)S(1)}, f32[16,1024]{1,0:T(8,128)S(1)}, u32[]{:S(2)}, u32[]{:S(2)}) collective-permute-start(f32[16,1024]{1,0:T(8,128)S(1)} %get-tuple-element.41), channel_id=1, source_target_pairs={{0,128},{128,0},{1,129},{129,1},{2,130},{130,2},{3,131},{131,3},{4... | collective-permute-start | bytes 196616 | tf_op jit(solution)/shard_map/ppermute | solution.py:268
  71.0 7.6 %collective-permute-start.9 = (f32[64,128]{1,0:T(8,128)}, f32[64,128]{1,0:T(8,128)S(1)}, u32[]{:S(2)}, u32[]{:S(2)}) collective-permute-start(f32[64,128]{1,0:T(8,128)} %get-tuple-element.30), channel_id=1, source_target_pairs={{0,32},{32,64},{64,96},{96,0},{1,33},{33,65},{65,97},{97,1},{2,34}... | collective-permute-start | bytes 98312 | tf_op jit(solution)/shard_map/ppermute | solution.py:270
  73.4 14.6 %collective-permute-start.10 = (f32[64,128]{1,0:T(8,128)}, f32[64,128]{1,0:T(8,128)S(1)}, u32[]{:S(2)}, u32[]{:S(2)}) collective-permute-start(f32[64,128]{1,0:T(8,128)} %get-tuple-element.31), channel_id=1, source_target_pairs={{1,0},{2,1},{3,2},{4,3},{5,4},{6,5},{7,6},{8,7},{9,8},{10,9},{11,1... | collective-permute-start | bytes 98312 | tf_op jit(solution)/shard_map/ppermute | solution.py:273
  78.6 15.3 %copy-start.12 = (f32[64,128]{1,0:T(8,128)}, f32[64,128]{1,0:T(8,128)S(1)}, u32[]{:S(2)}) copy-start(f32[64,128]{1,0:T(8,128)S(1)} %collective-permute-done.8.hyp_ref) | copy-start | bytes 98308
  78.6 15.3 %collective-permute-start.11 = (f32[64,128]{1,0:T(8,128)}, f32[64,128]{1,0:T(8,128)S(1)}, u32[]{:S(2)}, u32[]{:S(2)}) collective-permute-start(f32[64,128]{1,0:T(8,128)} %get-tuple-element.32), channel_id=1, source_target_pairs={{0,1},{1,2},{2,3},{3,4},{4,5},{5,6},{6,7},{7,8},{8,9},{9,10},{10,1... | collective-permute-start | bytes 98312 | tf_op jit(solution)/shard_map/ppermute | solution.py:272
  78.6 15.3 %copy-start.14 = (f32[64,128]{1,0:T(8,128)}, f32[64,128]{1,0:T(8,128)S(1)}, u32[]{:S(2)}) copy-start(f32[64,128]{1,0:T(8,128)S(1)} %collective-permute-done.9.hym_ref) | copy-start | bytes 98308
  88.1 5.9 %copy-start.15 = (f32[64,128]{1,0:T(8,128)}, f32[64,128]{1,0:T(8,128)S(1)}, u32[]{:S(2)}) copy-start(f32[64,128]{1,0:T(8,128)S(1)} %collective-permute-done.10.hzp_ref) | copy-start | bytes 98308
  98.4 1.0 copy-start.2
  (6 other events, 3.8 us)

commit v4 on v3

--- a/solution.py
+++ b/solution.py
@@ -77,19 +77,24 @@
     _emit_halos(cur_ref[...], zlo_ref, zhi_ref, ylo_ref, yhi_ref)
 
 
-def _finish_kernel(last, pick_ref, sel_ref, inc_ref, p_ref, q_ref, w_ref, *refs):
+def _finish_kernel(last, pick_ref, sel_ref, inc_ref, cur_ref, a_ref, q_ref, fz_ref,
+                   hzp_ref, hzm_ref, w_ref, *refs):
     if last:
-        cur_ref, g_scr, acc_scr = refs
+        out_ref, g_scr, acc_scr, p_scr = refs
     else:
-        cur_ref, snd_ref, g_scr, acc_scr = refs
+        out_ref, snd_ref, g_scr, acc_scr, p_scr = refs
     t = pl.program_id(0)
-    rows = p_ref.shape[0]
+    rows, _ = cur_ref.shape
 
     @pl.when(t == 0)
     def _():
         summed = jnp.dot(sel_ref[...], inc_ref[...], preferred_element_type=F32)
         g_scr[...] = summed.astype(BF16)
         acc_scr[...] = jnp.zeros_like(acc_scr)
+        cur = cur_ref[...]
+        dz = _deriv_z(cur, hzp_ref[...], hzm_ref[...])
+        drift = a_ref[...] + fz_ref[...] * dz
+        p_scr[...] = cur - drift
 
     grouped = g_scr[pl.ds(pl.multiple_of(t * rows, rows), rows), :]
     acc_scr[...] += lax.dot_general(
@@ -98,8 +103,8 @@
 
     @pl.when(t == pl.num_programs(0) - 1)
     def _():
-        cur = (p_ref[...] + acc_scr[...]) - q_ref[...]
-        cur_ref[...] = cur
+        cur = (p_scr[...] + acc_scr[...]) - q_ref[...]
+        out_ref[...] = cur
         if not last:
             _emit_send(pick_ref, cur, snd_ref)
 
@@ -108,8 +113,20 @@
     return (8.0 * (a1 - m1) - (a2 - m2)) / 12.0
 
 
-def _drift_kernel(cur_ref, xlo_ref, xhi_ref, hyp_ref, hym_ref, hzp_ref, hzm_ref,
-                  fx_ref, fy_ref, fz_ref, rate_ref, p_ref, q_ref, ext_ref):
+def _deriv_z(cur, hzp, hzm):
+    rows, lanes = cur.shape
+    z = lax.broadcasted_iota(jnp.int32, (rows, lanes), 1) & 15
+    ezp = _expand(hzp, "z_hi", lanes)
+    ezm = _expand(hzm, "z_lo", lanes)
+    zp1 = jnp.where(z == 15, pltpu.roll(ezp, 1, 1), pltpu.roll(cur, lanes - 1, 1))
+    zp2 = jnp.where(z >= 14, ezp, pltpu.roll(cur, lanes - 2, 1))
+    zm1 = jnp.where(z == 0, pltpu.roll(ezm, lanes - 1, 1), pltpu.roll(cur, 1, 1))
+    zm2 = jnp.where(z <= 1, ezm, pltpu.roll(cur, 2, 1))
+    return _deriv(zp1, zm1, zp2, zm2)
+
+
+def _drift_kernel(cur_ref, xlo_ref, xhi_ref, hyp_ref, hym_ref,
+                  fx_ref, fy_ref, rate_ref, a_ref, q_ref, ext_ref):
     rows, lanes = cur_ref.shape
     cur = cur_ref[...]
     ext_ref[0:16, :] = xlo_ref[...]
@@ -119,9 +136,7 @@
                 ext_ref[32:32 + rows, :], ext_ref[0:rows, :])
 
     k = lax.broadcasted_iota(jnp.int32, (rows, lanes), 1)
-    z = k & 15
     y = (k >> 4) & 15
-
     eyp = _expand(hyp_ref[...], "y_hi", lanes)
     eym = _expand(hym_ref[...], "y_lo", lanes)
     yp1 = jnp.where(y == 15, pltpu.roll(eyp, 16, 1), pltpu.roll(cur, lanes - 16, 1))
@@ -130,18 +145,8 @@
     ym2 = jnp.where(y <= 1, eym, pltpu.roll(cur, 32, 1))
     dy = _deriv(yp1, ym1, yp2, ym2)
 
-    ezp = _expand(hzp_ref[...], "z_hi", lanes)
-    ezm = _expand(hzm_ref[...], "z_lo", lanes)
-    zp1 = jnp.where(z == 15, pltpu.roll(ezp, 1, 1), pltpu.roll(cur, lanes - 1, 1))
-    zp2 = jnp.where(z >= 14, ezp, pltpu.roll(cur, lanes - 2, 1))
-    zm1 = jnp.where(z == 0, pltpu.roll(ezm, lanes - 1, 1), pltpu.roll(cur, 1, 1))
-    zm2 = jnp.where(z <= 1, ezm, pltpu.roll(cur, 2, 1))
-    dz = _deriv(zp1, zm1, zp2, zm2)
-
     drift = fx_ref[...] * dx
-    drift = drift + fy_ref[...] * dy
-    drift = drift + fz_ref[...] * dz
-    p_ref[...] = cur - drift
+    a_ref[...] = drift + fy_ref[...] * dy
     q_ref[...] = rate_ref[...] * cur
 
 
@@ -165,42 +170,38 @@
     return pl.pallas_call(_halo_kernel, out_shape=[halo] * 4)(cur)
 
 
-def _finish(last, pick, sel, inc, p, q, tiles, peers, both):
-    rows, lanes = p.shape
+def _finish(last, pick, sel, inc, cur, a, q, fz, hzp, hzm, tiles, peers, both):
+    rows, lanes = cur.shape
     tile_count = tiles.shape[0]
     shapes = [jax.ShapeDtypeStruct((rows, lanes), F32)]
     if not last:
         shapes.append(_send_shape(lanes, peers, both))
+    small = (pick, sel, inc, cur, a, q, fz, hzp, hzm)
     outs = pl.pallas_call(
         functools.partial(_finish_kernel, last),
         out_shape=shapes,
         grid=(tile_count,),
-        in_specs=[
-            _full(pick.shape),
-            _full(sel.shape),
-            _full(inc.shape),
-            _full(p.shape),
-            _full(q.shape),
-            pl.BlockSpec((1,) + tiles.shape[1:], lambda t: (t, 0, 0)),
-        ],
+        in_specs=[_full(x.shape) for x in small]
+        + [pl.BlockSpec((1,) + tiles.shape[1:], lambda t: (t, 0, 0))],
         out_specs=[_full(x.shape) for x in shapes],
         scratch_shapes=[
             pltpu.VMEM((tile_count * rows, lanes), BF16),
             pltpu.VMEM((rows, lanes), F32),
+            pltpu.VMEM((rows, lanes), F32),
         ],
         compiler_params=pltpu.CompilerParams(dimension_semantics=("arbitrary",)),
-    )(pick, sel, inc, p, q, tiles)
+    )(*small, tiles)
     return outs[0], outs[1:]
 
 
-def _drift(cur, xlo, xhi, hyp, hym, hzp, hzm, fx, fy, fz, rate):
+def _drift(cur, xlo, xhi, hyp, hym, fx, fy, rate):
     rows, lanes = cur.shape
     plane = jax.ShapeDtypeStruct((rows, lanes), F32)
     return pl.pallas_call(
         _drift_kernel,
         out_shape=[plane, plane],
         scratch_shapes=[pltpu.VMEM((rows + 32, lanes), F32)],
-    )(cur, xlo, xhi, hyp, hym, hzp, hzm, fx, fy, fz, rate)
+    )(cur, xlo, xhi, hyp, hym, fx, fy, rate)
 
 
 def _ring(axis):
@@ -273,9 +274,11 @@
         hzp = lax.ppermute(zlo, "kz", down_z)
         outgoing = snd.reshape(peer_count, both, lanes)
         incoming = lax.all_to_all(outgoing, "kz", split_axis=0, concat_axis=0, tiled=True)
-        p, q = _drift(cur, xlo, xhi, hyp, hym, hzp, hzm, fx, fy, fz, rate_wide)
+        a, q = _drift(cur, xlo, xhi, hyp, hym, fx, fy, rate_wide)
         inc = incoming.reshape(peer_count * both, lanes)
-        cur, rest = _finish(last, pick, sel_big, inc, p, q, tiles, peer_count, both)
+        cur, rest = _finish(
+            last, pick, sel_big, inc, cur, a, q, fz, hzp, hzm, tiles, peer_count, both
+        )
         if not last:
             (snd,) = rest
     return cur.reshape(width_x, drive_count, band_count, width_y, width_z)

time: 110 us -> 104 us (0.945)
  waiting for transfers between devices: 23.4 us -> 16.6 us
    ppermute x2, waiting for transfers between devices: 11.6 us -> 4.97 us  [per_device(): hzp = lax.ppermute(zlo, 'kz', down_z)]
    pallas_call x2, Pallas kernels: 15.4 us -> 16.8 us  [_finish(): pl.pallas_call(functools.partial(_finish_kernel, last), out_shape=shapes,...]
    pallas_call x2, Pallas kernels: 6.51 us -> 5.26 us  [_drift(): pl.pallas_call(_drift_kernel, out_shape=[plane, plane], scratch_shapes=[p...]
    ppermute x2, waiting for transfers between devices: 11.8 us -> 10.5 us  [per_device(): hzm = lax.ppermute(zhi, 'kz', up_z)]
    reshape x2 -> x3, local copies, waits for them, and re-layouts: 1.71 us -> 2.3 us  [spread(): jnp.broadcast_to(a, (width_x, drive_count, lanes)).reshape(rows, lanes)]
  transfers between devices with their start and end apart: 14 -> 14, of which waited for: 4 -> 5; matrix products, arithmetic and copies ran while one was open for 9% -> 10% of each run, Pallas kernels for 8% -> 8%
where the time goes in v4:
time: 104 us; the launch traced here: 103 us
  starting transfers between devices  35.9 us (35%)
  Pallas kernels  27.5 us (26%)
  local copies, waits for them, and re-layouts  20.7 us (20%)
  waiting for transfers between devices  16.6 us (16%)
  other arithmetic  2.35 us (2%)
    all_to_all x2, starting transfers between devices, per_device(): lax.all_to_all(outgoing, 'kz', split_axis=0, concat_axis=0, tiled=True)  17.5 us
    pallas_call x2, Pallas kernels, _finish(): pl.pallas_call(functools.partial(_finish_kernel, last), out_shape=shapes,...  16.8 us
    ppermute x2, waiting for transfers between devices, per_device(): hzm = lax.ppermute(zhi, 'kz', up_z)  10.5 us
    ppermute x2, starting transfers between devices, per_device(): hzp = lax.ppermute(zlo, 'kz', down_z)  10.4 us
    pallas_call x2, Pallas kernels, _drift(): pl.pallas_call(_drift_kernel, out_shape=[plane, plane], scratch_shapes=[p...  5.26 us
    ppermute x2, waiting for transfers between devices, per_device(): hzp = lax.ppermute(zlo, 'kz', down_z)  4.97 us
    unnamed x51, local copies, waits for them, and re-layouts  4.82 us
    ppermute x2, starting transfers between devices, per_device(): hym = lax.ppermute(yhi, 'ky', up_y)  4.82 us
  transfers between devices with their start and end apart: 14, of which 5 were waited for; matrix products, arithmetic and copies ran while one was open for 10% of the time, Pallas kernels for 8%

profile of v4, /device:TPU:6, one launch (start us, length us, event | category | flops | bytes accessed | tf_op | source)
XLA Modules:
  0.0 103.4 jit_solution(12241501075140087063)
XLA Ops:
  0.0 0.8 copy.12
  1.1 4.0 %reshape.50.cur_ref = f32[64,1024]{1,0:T(8,128)} reshape(f32[8,8,4,16,16]{4,3,2,1,0:T(8,128)} %param.8) | data formatting | bytes 524288 | tf_op jit(solution)/shard_map/reshape | solution.py:263
  5.1 1.0 fusion.7.pick_ref
  6.1 2.8 %shard_map.82 = (bf16[512,1024]{1,0:T(8,128)(2,1)}, f32[64,128]{1,0:T(8,128)}, f32[64,128]{1,0:T(8,128)}, f32[64,128]{1,0:T(8,128)}, f32[64,128]{1,0:T(8,128)}) custom-call(bf16[512,64]{1,0:T(8,128)(2,1)} %fusion.7.pick_ref, f32[64,1024]{1,0:T(8,128)} %reshape.50.cur_ref), custom_call_target="tpu_custom_call" | custom-call | tf_op jit(solution)/shard_map/pallas_call | solution.py:165
  8.9 11.5 %all-to-all-start = ((bf16[32,16,1024]{2,1,0:T(8,128)(2,1)}), bf16[32,16,1024]{2,1,0:T(8,128)(2,1)S(1)}, u32[]{:S(2)}, u32[]{:S(2)}) async-start(bf16[32,16,1024]{2,1,0:T(8,128)(2,1)} %bitcast.35), calls=%async_computation | async-start | bytes 2097152 | tf_op jit(solution)/shard_map/all_to_all | solution.py:276
  20.5 1.1 %fusion.16 = (f32[2,8,4,16,16]{4,3,2,1,0:T(8,128)}, f32[2,8,4,16,16]{4,3,2,1,0:T(8,128)}) fusion(f32[8,8,4,16,16]{4,3,2,1,0:T(8,128)S(1)} %copy-done), kind=kLoop, calls=%fused_computation.47 | loop fusion | bytes 262144 | tf_op jit(solution)/shard_map/slice | solution.py:270
  21.6 1.3 %slice.28 = f32[16,1024]{1,0:T(8,128)S(1)} reshape(f32[2,8,4,16,16]{4,3,2,1,0:T(8,128)} %get-tuple-element.36) | data formatting | bytes 131072 | tf_op jit(solution)/shard_map/slice | solution.py:269
  23.0 1.3 %slice.30 = f32[16,1024]{1,0:T(8,128)S(1)} reshape(f32[2,8,4,16,16]{4,3,2,1,0:T(8,128)} %get-tuple-element.35) | data formatting | bytes 131072 | tf_op jit(solution)/shard_map/slice | solution.py:270
  24.9 0.8 collective-permute-start.2
  25.7 2.4 %collective-permute-start.3 = (f32[64,128]{1,0:T(8,128)S(1)}, f32[64,128]{1,0:T(8,128)S(1)}, u32[]{:S(2)}, u32[]{:S(2)}) collective-permute-start(f32[64,128]{1,0:T(8,128)S(1)} %copy-done.22), channel_id=1, source_target_pairs={{0,32},{32,64},{64,96},{96,0},{1,33},{33,65},{65,97},{97,1},{2,34}... | collective-permute-start | bytes 98312 | tf_op jit(solution)/shard_map/ppermute | solution.py:271
  28.1 5.2 %collective-permute-start.4 = (f32[64,128]{1,0:T(8,128)S(1)}, f32[64,128]{1,0:T(8,128)S(1)}, u32[]{:S(2)}, u32[]{:S(2)}) collective-permute-start(f32[64,128]{1,0:T(8,128)S(1)} %copy-done.21), channel_id=1, source_target_pairs={{1,0},{2,1},{3,2},{4,3},{5,4},{6,5},{7,6},{8,7},{9,8},{10,9},{11,1... | collective-permute-start | bytes 98312 | tf_op jit(solution)/shard_map/ppermute | solution.py:274
  33.5 1.2 %fusion.17 = (f32[8,1,4,16,16]{4,3,2,1,0:T(8,128)S(1)}, f32[8,1,4,16,16]{4,3,2,1,0:T(8,128)S(1)}, f32[8,1,4,16,16]{4,3,2,1,0:T(8,128)S(1)}) fusion(f32[8,3,4,16,16]{4,3,2,1,0:T(8,128)} %param.9), kind=kLoop, calls=%fused_computation.48 | loop fusion | bytes 196608 | tf_op jit(solution)/shard_map/slice | solution.py:256
  35.3 0.7 broadcast_bitcast_fusion.3.fx_ref
  36.0 0.7 broadcast_bitcast_fusion.fz_ref
  36.7 0.8 broadcast_bitcast_fusion.1
  38.9 1.2 %fusion.3.sel_ref = bf16[256,512]{1,0:T(8,128)(2,1)} fusion(s32[512]{0:T(512)S(1)} %get-tuple-element.42, s32[512]{0:T(512)S(1)} %get-tuple-element.43, s32[256]{0:T(256)S(1)} %get-tuple-element.54, s32[256]{0:T(256)S(1)} %get-tuple-element.55, s32[512]{0:T(512)S(1)} %eq.50, s32[256]{0:T(256)S(1)} %get-tuple-element.51, s32[256]{0:T(256)S(1)} %get-tuple-element.56, ...), kind=kLoop, calls=%fused_computation.10 | loop fusion | flops 2883584 | bytes 278272 | tf_op jit(solution)/shard_map/convert_element_type | solution.py:243
  40.9 2.6 %shard_map.83 = (f32[64,1024]{1,0:T(8,128)}, f32[64,1024]{1,0:T(8,128)}) custom-call(f32[64,1024]{1,0:T(8,128)} %reshape.50.cur_ref, f32[16,1024]{1,0:T(8,128)} %copy-done.5, f32[16,1024]{1,0:T(8,128)} %copy-done.6, f32[64,128]{1,0:T(8,128)} %copy-done.13, f32[64,128]{1,0:T(8,128)} %copy-done.14, f32[64,1024]{1,0:T(8,128)} %broadcast_bitcast_fusion.3.fx_ref, ...), custom_call_target="tpu_custom_call" | custom-call | tf_op jit(solution)/shard_map/pallas_call | solution.py:200
  43.5 4.2 %collective-permute-done.5.hzm_ref = f32[64,128]{1,0:T(8,128)S(1)} collective-permute-done((f32[64,128]{1,0:T(8,128)S(1)}, f32[64,128]{1,0:T(8,128)S(1)}, u32[]{:S(2)}, u32[]{:S(2)}) %collective-permute-start.5) | collective-permute-done | bytes 32800 | tf_op jit(solution)/shard_map/ppermute | solution.py:273
  47.7 0.8 all-to-all-done
  48.5 1.0 copy-done.1
  49.5 8.8 %shard_map.84 = (f32[64,1024]{1,0:T(8,128)}, bf16[512,1024]{1,0:T(8,128)(2,1)}) custom-call(bf16[512,64]{1,0:T(8,128)(2,1)} %fusion.7.pick_ref, bf16[256,512]{1,0:T(8,128)(2,1)} %fusion.3.sel_ref, bf16[512,1024]{1,0:T(8,128)(2,1)} %bitcast.33, f32[64,1024]{1,0:T(8,128)} %reshape.50.cur_ref, f32[64,1024]{1,0:T(8,128)} %get-tuple-element.23.a_ref, ...), custom_call_target="tpu_custom_call" | custom-call | tf_op jit(solution)/shard_map/pallas_call | solution.py:180
  58.3 6.0 %all-to-all-start.1 = ((bf16[32,16,1024]{2,1,0:T(8,128)(2,1)}), bf16[32,16,1024]{2,1,0:T(8,128)(2,1)S(1)}, u32[]{:S(2)}, u32[]{:S(2)}) async-start(bf16[32,16,1024]{2,1,0:T(8,128)(2,1)} %bitcast.36), calls=%async_computation.1 | async-start | bytes 2097152 | tf_op jit(solution)/shard_map/all_to_all | solution.py:276
  64.3 2.6 %shard_map.85 = (f32[64,128]{1,0:T(8,128)}, f32[64,128]{1,0:T(8,128)}, f32[64,128]{1,0:T(8,128)}, f32[64,128]{1,0:T(8,128)}) custom-call(f32[64,1024]{1,0:T(8,128)} %get-tuple-element.28.cur_ref), custom_call_target="tpu_custom_call" | custom-call | tf_op jit(solution)/shard_map/pallas_call | solution.py:170
  67.5 0.8 collective-permute-start.8
  68.3 2.4 %collective-permute-start.9 = (f32[64,128]{1,0:T(8,128)}, f32[64,128]{1,0:T(8,128)S(1)}, u32[]{:S(2)}, u32[]{:S(2)}) collective-permute-start(f32[64,128]{1,0:T(8,128)} %get-tuple-element.30), channel_id=1, source_target_pairs={{0,32},{32,64},{64,96},{96,0},{1,33},{33,65},{65,97},{97,1},{2,34}... | collective-permute-start | bytes 98312 | tf_op jit(solution)/shard_map/ppermute | solution.py:271
  70.7 5.2 %collective-permute-start.10 = (f32[64,128]{1,0:T(8,128)}, f32[64,128]{1,0:T(8,128)S(1)}, u32[]{:S(2)}, u32[]{:S(2)}) collective-permute-start(f32[64,128]{1,0:T(8,128)} %get-tuple-element.33), channel_id=1, source_target_pairs={{1,0},{2,1},{3,2},{4,3},{5,4},{6,5},{7,6},{8,7},{9,8},{10,9},{11,1... | collective-permute-start | bytes 98312 | tf_op jit(solution)/shard_map/ppermute | solution.py:274
  76.6 0.6 copy-done.8
  77.2 2.6 %shard_map.86 = (f32[64,1024]{1,0:T(8,128)}, f32[64,1024]{1,0:T(8,128)}) custom-call(f32[64,1024]{1,0:T(8,128)} %get-tuple-element.28.cur_ref, f32[16,1024]{1,0:T(8,128)} %copy-done.8, f32[16,1024]{1,0:T(8,128)} %copy-done.7, f32[64,128]{1,0:T(8,128)} %copy-done.15, f32[64,128]{1,0:T(8,128)} %copy-done.16, f32[64,1024]{1,0:T(8,128)} %broadcast_bitcast_fusion.3.fx_ref, ...), custom_call_target="tpu_custom_call" | custom-call | tf_op jit(solution)/shard_map/pallas_call | solution.py:200
  79.9 5.0 %collective-permute-done.10.hzp_ref = f32[64,128]{1,0:T(8,128)S(1)} collective-permute-done((f32[64,128]{1,0:T(8,128)}, f32[64,128]{1,0:T(8,128)S(1)}, u32[]{:S(2)}, u32[]{:S(2)}) %collective-permute-start.10) | collective-permute-done | bytes 32800 | tf_op jit(solution)/shard_map/ppermute | solution.py:274
  84.8 6.3 %collective-permute-done.11.hzm_ref = f32[64,128]{1,0:T(8,128)S(1)} collective-permute-done((f32[64,128]{1,0:T(8,128)}, f32[64,128]{1,0:T(8,128)S(1)}, u32[]{:S(2)}, u32[]{:S(2)}) %collective-permute-start.11) | collective-permute-done | bytes 32800 | tf_op jit(solution)/shard_map/ppermute | solution.py:273
  92.4 8.0 %shard_map.87 = f32[64,1024]{1,0:T(8,128)} custom-call(bf16[512,64]{1,0:T(8,128)(2,1)} %fusion.7.pick_ref, bf16[256,512]{1,0:T(8,128)(2,1)} %fusion.3.sel_ref, bf16[512,1024]{1,0:T(8,128)(2,1)} %bitcast.34, f32[64,1024]{1,0:T(8,128)} %get-tuple-element.28.cur_ref, f32[64,1024]{1,0:T(8,128)} %get-tuple-element.31.a_ref, f32[64,1024]{1,0:T(8,128)} %get-tuple-element.32.q_ref, ...), custom_call_target="tpu_custom_call" | custom-call | tf_op jit(solution)/shard_map/pallas_call | solution.py:180
  100.4 3.0 %reshape.59 = f32[8,8,4,16,16]{4,3,2,1,0:T(8,128)} reshape(f32[64,1024]{1,0:T(8,128)} %shard_map.87) | data formatting | bytes 524288 | tf_op jit(solution)/shard_map/reshape | solution.py:284
  (92 shorter events, 6.1 us)
Async XLA Ops:
  1.1 19.3 %copy-start = (f32[8,8,4,16,16]{4,3,2,1,0:T(8,128)S(1)}, f32[8,8,4,16,16]{4,3,2,1,0:T(8,128)}, u32[]{:S(2)}) copy-start(f32[8,8,4,16,16]{4,3,2,1,0:T(8,128)} %param.8) | copy-start | bytes 786436
  8.9 39.6 %all-to-all-start = ((bf16[32,16,1024]{2,1,0:T(8,128)(2,1)}), bf16[32,16,1024]{2,1,0:T(8,128)(2,1)S(1)}, u32[]{:S(2)}, u32[]{:S(2)}) async-start(bf16[32,16,1024]{2,1,0:T(8,128)(2,1)} %bitcast.35), calls=%async_computation | async-start | bytes 2097152 | tf_op jit(solution)/shard_map/all_to_all | solution.py:276
  20.4 4.5 %copy-start.23 = (f32[64,128]{1,0:T(8,128)S(1)}, f32[64,128]{1,0:T(8,128)}, u32[]{:S(2)}) copy-start(f32[64,128]{1,0:T(8,128)} %get-tuple-element.21) | copy-start | bytes 98308
  20.4 5.3 %copy-start.22 = (f32[64,128]{1,0:T(8,128)S(1)}, f32[64,128]{1,0:T(8,128)}, u32[]{:S(2)}) copy-start(f32[64,128]{1,0:T(8,128)} %get-tuple-element.22) | copy-start | bytes 98308
  20.5 7.7 %copy-start.21 = (f32[64,128]{1,0:T(8,128)S(1)}, f32[64,128]{1,0:T(8,128)}, u32[]{:S(2)}) copy-start(f32[64,128]{1,0:T(8,128)} %get-tuple-element.25) | copy-start | bytes 98308
  20.5 12.9 %copy-start.4 = (f32[8,4,16,16]{3,2,1,0:T(8,128)S(1)}, f32[8,4,16,16]{3,2,1,0:T(8,128)}, u32[]{:S(2)}) copy-start(f32[8,4,16,16]{3,2,1,0:T(8,128)} %param.10) | copy-start | bytes 98308
  21.6 13.6 %copy-start.19 = (s32[1,1,1,32]{3,2,1,0:T(1,128)S(1)}, s32[1,1,1,32]{3,2,1,0:T(1,128)}, u32[]{:S(2)}) copy-start(s32[1,1,1,32]{3,2,1,0:T(1,128)} %param.15) | copy-start | bytes 388
  22.9 17.3 %collective-permute-start = (f32[16,1024]{1,0:T(8,128)S(1)}, f32[16,1024]{1,0:T(8,128)S(1)}, u32[]{:S(2)}, u32[]{:S(2)}) collective-permute-start(f32[16,1024]{1,0:T(8,128)S(1)} %slice.28), channel_id=1, source_target_pairs={{0,128},{128,0},{1,129},{129,1},{2,130},{130,2},{3,131},{131,3},{4... | collective-permute-start | bytes 196616 | tf_op jit(solution)/shard_map/ppermute | solution.py:269
  24.3 13.6 %copy-start.17 = (s32[1,1,1,32,2]{3,4,2,1,0:T(2,128)S(1)}, s32[1,1,1,32,2]{3,4,2,1,0:T(2,128)}, u32[]{:S(2)}) copy-start(s32[1,1,1,32,2]{3,4,2,1,0:T(2,128)} %param.13) | copy-start | bytes 772
  24.3 13.8 %copy-start.18 = (s32[1,1,1,32,2]{3,4,2,1,0:T(2,128)S(1)}, s32[1,1,1,32,2]{3,4,2,1,0:T(2,128)}, u32[]{:S(2)}) copy-start(s32[1,1,1,32,2]{3,4,2,1,0:T(2,128)} %param.14) | copy-start | bytes 772
  24.3 14.3 %copy-start.20 = (f32[64,128]{1,0:T(8,128)S(1)}, f32[64,128]{1,0:T(8,128)}, u32[]{:S(2)}) copy-start(f32[64,128]{1,0:T(8,128)} %get-tuple-element.26) | copy-start | bytes 98308
  24.3 15.9 %collective-permute-start.1 = (f32[16,1024]{1,0:T(8,128)S(1)}, f32[16,1024]{1,0:T(8,128)S(1)}, u32[]{:S(2)}, u32[]{:S(2)}) collective-permute-start(f32[16,1024]{1,0:T(8,128)S(1)} %slice.30), channel_id=1, source_target_pairs={{128,0},{0,128},{129,1},{1,129},{130,2},{2,130},{131,3},{3,131},{1... | collective-permute-start | bytes 196616 | tf_op jit(solution)/shard_map/ppermute | solution.py:270
  24.9 13.7 %collective-permute-start.2 = (f32[64,128]{1,0:T(8,128)S(1)}, f32[64,128]{1,0:T(8,128)S(1)}, u32[]{:S(2)}, u32[]{:S(2)}) collective-permute-start(f32[64,128]{1,0:T(8,128)S(1)} %copy-done.23), channel_id=1, source_target_pairs={{32,0},{64,32},{96,64},{0,96},{33,1},{65,33},{97,65},{1,97},{34,2}... | collective-permute-start | bytes 98312 | tf_op jit(solution)/shard_map/ppermute | solution.py:272
  25.7 14.4 %collective-permute-start.3 = (f32[64,128]{1,0:T(8,128)S(1)}, f32[64,128]{1,0:T(8,128)S(1)}, u32[]{:S(2)}, u32[]{:S(2)}) collective-permute-start(f32[64,128]{1,0:T(8,128)S(1)} %copy-done.22), channel_id=1, source_target_pairs={{0,32},{32,64},{64,96},{96,0},{1,33},{33,65},{65,97},{97,1},{2,34}... | collective-permute-start | bytes 98312 | tf_op jit(solution)/shard_map/ppermute | solution.py:271
  28.1 15.3 %collective-permute-start.4 = (f32[64,128]{1,0:T(8,128)S(1)}, f32[64,128]{1,0:T(8,128)S(1)}, u32[]{:S(2)}, u32[]{:S(2)}) collective-permute-start(f32[64,128]{1,0:T(8,128)S(1)} %copy-done.21), channel_id=1, source_target_pairs={{1,0},{2,1},{3,2},{4,3},{5,4},{6,5},{7,6},{8,7},{9,8},{10,9},{11,1... | collective-permute-start | bytes 98312 | tf_op jit(solution)/shard_map/ppermute | solution.py:274
  38.6 1.6 %copy-start.13 = (f32[64,128]{1,0:T(8,128)}, f32[64,128]{1,0:T(8,128)S(1)}, u32[]{:S(2)}) copy-start(f32[64,128]{1,0:T(8,128)S(1)} %collective-permute-done.2.hyp_ref) | copy-start | bytes 98308
  38.7 9.1 %collective-permute-start.5 = (f32[64,128]{1,0:T(8,128)S(1)}, f32[64,128]{1,0:T(8,128)S(1)}, u32[]{:S(2)}, u32[]{:S(2)}) collective-permute-start(f32[64,128]{1,0:T(8,128)S(1)} %copy-done.20), channel_id=1, source_target_pairs={{0,1},{1,2},{2,3},{3,4},{4,5},{5,6},{6,7},{7,8},{8,9},{9,10},{10,1... | collective-permute-start | bytes 98312 | tf_op jit(solution)/shard_map/ppermute | solution.py:273
  40.2 0.6 copy-start.5
  40.2 0.6 copy-start.6
  43.5 5.0 %copy-start.9 = (f32[64,128]{1,0:T(8,128)}, f32[64,128]{1,0:T(8,128)S(1)}, u32[]{:S(2)}) copy-start(f32[64,128]{1,0:T(8,128)S(1)} %collective-permute-done.4.hzp_ref) | copy-start | bytes 98308
  47.7 0.8 copy-start.10
  48.5 1.0 copy-start.1
  58.3 8.6 %copy-start.3 = (f32[64,1024]{1,0:T(8,128)S(1)}, f32[64,1024]{1,0:T(8,128)}, u32[]{:S(2)}) copy-start(f32[64,1024]{1,0:T(8,128)} %get-tuple-element.28.cur_ref) | copy-start | bytes 786436
  58.3 33.2 %all-to-all-start.1 = ((bf16[32,16,1024]{2,1,0:T(8,128)(2,1)}), bf16[32,16,1024]{2,1,0:T(8,128)(2,1)S(1)}, u32[]{:S(2)}, u32[]{:S(2)}) async-start(bf16[32,16,1024]{2,1,0:T(8,128)(2,1)} %bitcast.36), calls=%async_computation.1 | async-start | bytes 2097152 | tf_op jit(solution)/shard_map/all_to_all | solution.py:276
  66.9 9.1 %collective-permute-start.7 = (f32[16,1024]{1,0:T(8,128)S(1)}, f32[16,1024]{1,0:T(8,128)S(1)}, u32[]{:S(2)}, u32[]{:S(2)}) collective-permute-start(f32[16,1024]{1,0:T(8,128)S(1)} %get-tuple-element.40), channel_id=1, source_target_pairs={{128,0},{0,128},{129,1},{1,129},{130,2},{2,130},{131,3},{3,131},{1... | collective-permute-start | bytes 196616 | tf_op jit(solution)/shard_map/ppermute | solution.py:270
  67.0 9.0 %collective-permute-start.6 = (f32[16,1024]{1,0:T(8,128)S(1)}, f32[16,1024]{1,0:T(8,128)S(1)}, u32[]{:S(2)}, u32[]{:S(2)}) collective-permute-start(f32[16,1024]{1,0:T(8,128)S(1)} %get-tuple-element.41), channel_id=1, source_target_pairs={{0,128},{128,0},{1,129},{129,1},{2,130},{130,2},{3,131},{131,3},{4... | collective-permute-start | bytes 196616 | tf_op jit(solution)/shard_map/ppermute | solution.py:269
  67.5 8.4 %collective-permute-start.8 = (f32[64,128]{1,0:T(8,128)}, f32[64,128]{1,0:T(8,128)S(1)}, u32[]{:S(2)}, u32[]{:S(2)}) collective-permute-start(f32[64,128]{1,0:T(8,128)} %get-tuple-element.29), channel_id=1, source_target_pairs={{32,0},{64,32},{96,64},{0,96},{33,1},{65,33},{97,65},{1,97},{34,2}... | collective-permute-start | bytes 98312 | tf_op jit(solution)/shard_map/ppermute | solution.py:272
  68.3 7.6 %collective-permute-start.9 = (f32[64,128]{1,0:T(8,128)}, f32[64,128]{1,0:T(8,128)S(1)}, u32[]{:S(2)}, u32[]{:S(2)}) collective-permute-start(f32[64,128]{1,0:T(8,128)} %get-tuple-element.30), channel_id=1, source_target_pairs={{0,32},{32,64},{64,96},{96,0},{1,33},{33,65},{65,97},{97,1},{2,34}... | collective-permute-start | bytes 98312 | tf_op jit(solution)/shard_map/ppermute | solution.py:271
  70.7 14.1 %collective-permute-start.10 = (f32[64,128]{1,0:T(8,128)}, f32[64,128]{1,0:T(8,128)S(1)}, u32[]{:S(2)}, u32[]{:S(2)}) collective-permute-start(f32[64,128]{1,0:T(8,128)} %get-tuple-element.33), channel_id=1, source_target_pairs={{1,0},{2,1},{3,2},{4,3},{5,4},{6,5},{7,6},{8,7},{9,8},{10,9},{11,1... | collective-permute-start | bytes 98312 | tf_op jit(solution)/shard_map/ppermute | solution.py:274
  75.9 15.2 %collective-permute-start.11 = (f32[64,128]{1,0:T(8,128)}, f32[64,128]{1,0:T(8,128)S(1)}, u32[]{:S(2)}, u32[]{:S(2)}) collective-permute-start(f32[64,128]{1,0:T(8,128)} %get-tuple-element.34), channel_id=1, source_target_pairs={{0,1},{1,2},{2,3},{3,4},{4,5},{5,6},{6,7},{7,8},{8,9},{9,10},{10,1... | collective-permute-start | bytes 98312 | tf_op jit(solution)/shard_map/ppermute | solution.py:273
  84.8 6.6 %copy-start.11 = (f32[64,128]{1,0:T(8,128)}, f32[64,128]{1,0:T(8,128)S(1)}, u32[]{:S(2)}) copy-start(f32[64,128]{1,0:T(8,128)S(1)} %collective-permute-done.10.hzp_ref) | copy-start | bytes 98308
  91.4 1.0 copy-start.2
  (6 other events, 3.7 us)

commit v5 on v4

--- a/solution.py
+++ b/solution.py
@@ -78,35 +78,35 @@
 
 
 def _finish_kernel(last, pick_ref, sel_ref, inc_ref, cur_ref, a_ref, q_ref, fz_ref,
-                   hzp_ref, hzm_ref, w_ref, *refs):
+                   hzp_ref, hzm_ref, w_hbm, *refs):
     if last:
-        out_ref, g_scr, acc_scr, p_scr = refs
+        out_ref, w_buf, sems = refs
     else:
-        out_ref, snd_ref, g_scr, acc_scr, p_scr = refs
-    t = pl.program_id(0)
-    rows, _ = cur_ref.shape
-
-    @pl.when(t == 0)
-    def _():
-        summed = jnp.dot(sel_ref[...], inc_ref[...], preferred_element_type=F32)
-        g_scr[...] = summed.astype(BF16)
-        acc_scr[...] = jnp.zeros_like(acc_scr)
-        cur = cur_ref[...]
-        dz = _deriv_z(cur, hzp_ref[...], hzm_ref[...])
-        drift = a_ref[...] + fz_ref[...] * dz
-        p_scr[...] = cur - drift
-
-    grouped = g_scr[pl.ds(pl.multiple_of(t * rows, rows), rows), :]
-    acc_scr[...] += lax.dot_general(
-        grouped, w_ref[0], (((1,), (1,)), ((), ())), preferred_element_type=F32
-    )
-
-    @pl.when(t == pl.num_programs(0) - 1)
-    def _():
-        cur = (p_scr[...] + acc_scr[...]) - q_ref[...]
-        out_ref[...] = cur
-        if not last:
-            _emit_send(pick_ref, cur, snd_ref)
+        out_ref, snd_ref, w_buf, sems = refs
+    rows = cur_ref.shape[0]
+    tile_count = w_hbm.shape[0]
+    copies = [
+        pltpu.make_async_copy(w_hbm.at[t], w_buf.at[t], sems.at[t]) for t in range(tile_count)
+    ]
+    for copy in copies:
+        copy.start()
+    grouped = jnp.dot(sel_ref[...], inc_ref[...], preferred_element_type=F32).astype(BF16)
+    cur = cur_ref[...]
+    dz = _deriv_z(cur, hzp_ref[...], hzm_ref[...])
+    drift = a_ref[...] + fz_ref[...] * dz
+    p = cur - drift
+    coll = None
+    for t in range(tile_count):
+        copies[t].wait()
+        part = lax.dot_general(
+            grouped[t * rows:(t + 1) * rows], w_buf[t], (((1,), (1,)), ((), ())),
+            preferred_element_type=F32,
+        )
+        coll = part if coll is None else coll + part
+    cur = (p + coll) - q_ref[...]
+    out_ref[...] = cur
+    if not last:
+        _emit_send(pick_ref, cur, snd_ref)
 
 
 def _deriv(a1, m1, a2, m2):
@@ -150,11 +150,6 @@
     q_ref[...] = rate_ref[...] * cur
 
 
-def _full(shape):
-    zeros = (0,) * len(shape)
-    return pl.BlockSpec(shape, lambda *_: zeros)
-
-
 def _send_shape(lanes, peers, both):
     return jax.ShapeDtypeStruct((peers * both, lanes), BF16)
 
@@ -172,24 +167,21 @@
 
 def _finish(last, pick, sel, inc, cur, a, q, fz, hzp, hzm, tiles, peers, both):
     rows, lanes = cur.shape
-    tile_count = tiles.shape[0]
     shapes = [jax.ShapeDtypeStruct((rows, lanes), F32)]
     if not last:
         shapes.append(_send_shape(lanes, peers, both))
     small = (pick, sel, inc, cur, a, q, fz, hzp, hzm)
+    vmem = pl.BlockSpec(memory_space=pltpu.VMEM)
     outs = pl.pallas_call(
         functools.partial(_finish_kernel, last),
         out_shape=shapes,
-        grid=(tile_count,),
-        in_specs=[_full(x.shape) for x in small]
-        + [pl.BlockSpec((1,) + tiles.shape[1:], lambda t: (t, 0, 0))],
-        out_specs=[_full(x.shape) for x in shapes],
+        in_specs=[vmem] * len(small) + [pl.BlockSpec(memory_space=pl.ANY)],
+        out_specs=[vmem] * len(shapes),
         scratch_shapes=[
-            pltpu.VMEM((tile_count * rows, lanes), BF16),
-            pltpu.VMEM((rows, lanes), F32),
-            pltpu.VMEM((rows, lanes), F32),
+            pltpu.VMEM(tiles.shape, tiles.dtype),
+            pltpu.SemaphoreType.DMA((tiles.shape[0],)),
         ],
-        compiler_params=pltpu.CompilerParams(dimension_semantics=("arbitrary",)),
+        compiler_params=pltpu.CompilerParams(vmem_limit_bytes=40 * 1024 * 1024),
     )(*small, tiles)
     return outs[0], outs[1:]
 

time: 104 us -> 106 us (1.019)
  local copies, waits for them, and re-layouts: 20.7 us -> 28.4 us
  Pallas kernels: 27.5 us -> 20.5 us
  waiting for transfers between devices: 16.6 us -> 18 us
    unnamed x51 -> x53, local copies, waits for them, and re-layouts: 4.82 us -> 14.1 us
    pallas_call x2, Pallas kernels: 16.8 us -> 9.82 us  [_finish(): pl.pallas_call(functools.partial(_finish_kernel, last), out_shape=shapes,...]
    ppermute x2, waiting for transfers between devices: 10.5 us -> 11.9 us  [per_device(): hzm = lax.ppermute(zhi, 'kz', up_z)]
  transfers between devices with their start and end apart: 14 -> 14, of which waited for: 5 -> 5; matrix products, arithmetic and copies ran while one was open for 10% -> 8% of each run, Pallas kernels for 8% -> 7%
where the time goes in v5:
time: 106 us; the launch traced here: 105 us
  starting transfers between devices  35.9 us (34%)
  local copies, waits for them, and re-layouts  28.4 us (27%)
  Pallas kernels  20.5 us (19%)
  waiting for transfers between devices  18 us (17%)
  other arithmetic  1.71 us (2%)
    all_to_all x2, starting transfers between devices, per_device(): lax.all_to_all(outgoing, 'kz', split_axis=0, concat_axis=0, tiled=True)  17.5 us
    unnamed x53, local copies, waits for them, and re-layouts  14.1 us
    ppermute x2, waiting for transfers between devices, per_device(): hzm = lax.ppermute(zhi, 'kz', up_z)  11.9 us
    ppermute x2, starting transfers between devices, per_device(): hzp = lax.ppermute(zlo, 'kz', down_z)  10.4 us
    pallas_call x2, Pallas kernels, _finish(): pl.pallas_call(functools.partial(_finish_kernel, last), out_shape=shapes,...  9.82 us
    pallas_call x2, Pallas kernels, _drift(): pl.pallas_call(_drift_kernel, out_shape=[plane, plane], scratch_shapes=[p...  5.27 us
    ppermute x2, waiting for transfers between devices, per_device(): hzp = lax.ppermute(zlo, 'kz', down_z)  5 us
    ppermute x2, starting transfers between devices, per_device(): hym = lax.ppermute(yhi, 'ky', up_y)  4.81 us
  transfers between devices with their start and end apart: 14, of which 5 were waited for; matrix products, arithmetic and copies ran while one was open for 8% of the time, Pallas kernels for 7%

profile of v5, /device:TPU:6, one launch (start us, length us, event | category | flops | bytes accessed | tf_op | source)
XLA Modules:
  0.0 104.8 jit_solution(13593419336815289122)
XLA Ops:
  1.1 4.0 %reshape.50.cur_ref = f32[64,1024]{1,0:T(8,128)} reshape(f32[8,8,4,16,16]{4,3,2,1,0:T(8,128)} %param.8) | data formatting | bytes 524288 | tf_op jit(solution)/shard_map/reshape | solution.py:255
  5.1 1.0 fusion.7.pick_ref
  6.1 2.8 %shard_map.82 = (bf16[512,1024]{1,0:T(8,128)(2,1)}, f32[64,128]{1,0:T(8,128)}, f32[64,128]{1,0:T(8,128)}, f32[64,128]{1,0:T(8,128)}, f32[64,128]{1,0:T(8,128)}) custom-call(bf16[512,64]{1,0:T(8,128)(2,1)} %fusion.7.pick_ref, f32[64,1024]{1,0:T(8,128)} %reshape.50.cur_ref), custom_call_target="tpu_custom_call" | custom-call | tf_op jit(solution)/shard_map/pallas_call | solution.py:160
  8.9 11.5 %all-to-all-start = ((bf16[32,16,1024]{2,1,0:T(8,128)(2,1)}), bf16[32,16,1024]{2,1,0:T(8,128)(2,1)S(1)}, u32[]{:S(2)}, u32[]{:S(2)}) async-start(bf16[32,16,1024]{2,1,0:T(8,128)(2,1)} %bitcast.35), calls=%async_computation | async-start | bytes 2097152 | tf_op jit(solution)/shard_map/all_to_all | solution.py:268
  20.4 1.1 %fusion.16 = (f32[2,8,4,16,16]{4,3,2,1,0:T(8,128)}, f32[2,8,4,16,16]{4,3,2,1,0:T(8,128)}) fusion(f32[8,8,4,16,16]{4,3,2,1,0:T(8,128)S(1)} %copy-done.11), kind=kLoop, calls=%fused_computation.47 | loop fusion | bytes 262144 | tf_op jit(solution)/shard_map/slice | solution.py:262
  21.5 1.3 %slice.28 = f32[16,1024]{1,0:T(8,128)S(1)} reshape(f32[2,8,4,16,16]{4,3,2,1,0:T(8,128)} %get-tuple-element.36) | data formatting | bytes 131072 | tf_op jit(solution)/shard_map/slice | solution.py:261
  23.0 1.3 %slice.30 = f32[16,1024]{1,0:T(8,128)S(1)} reshape(f32[2,8,4,16,16]{4,3,2,1,0:T(8,128)} %get-tuple-element.35) | data formatting | bytes 131072 | tf_op jit(solution)/shard_map/slice | solution.py:262
  24.9 0.8 collective-permute-start.2
  25.7 2.4 %collective-permute-start.3 = (f32[64,128]{1,0:T(8,128)}, f32[64,128]{1,0:T(8,128)S(1)}, u32[]{:S(2)}, u32[]{:S(2)}) collective-permute-start(f32[64,128]{1,0:T(8,128)} %get-tuple-element.22), channel_id=1, source_target_pairs={{0,32},{32,64},{64,96},{96,0},{1,33},{33,65},{65,97},{97,1},{2,34}... | collective-permute-start | bytes 98312 | tf_op jit(solution)/shard_map/ppermute | solution.py:263
  28.1 5.2 %collective-permute-start.4 = (f32[64,128]{1,0:T(8,128)}, f32[64,128]{1,0:T(8,128)S(1)}, u32[]{:S(2)}, u32[]{:S(2)}) collective-permute-start(f32[64,128]{1,0:T(8,128)} %get-tuple-element.25), channel_id=1, source_target_pairs={{1,0},{2,1},{3,2},{4,3},{5,4},{6,5},{7,6},{8,7},{9,8},{10,9},{11,1... | collective-permute-start | bytes 98312 | tf_op jit(solution)/shard_map/ppermute | solution.py:266
  33.5 1.2 %fusion.17 = (f32[8,1,4,16,16]{4,3,2,1,0:T(8,128)S(1)}, f32[8,1,4,16,16]{4,3,2,1,0:T(8,128)S(1)}, f32[8,1,4,16,16]{4,3,2,1,0:T(8,128)S(1)}) fusion(f32[8,3,4,16,16]{4,3,2,1,0:T(8,128)} %param.9), kind=kLoop, calls=%fused_computation.48 | loop fusion | bytes 196608 | tf_op jit(solution)/shard_map/slice | solution.py:248
  36.0 0.9 broadcast_bitcast_fusion.1
  39.5 2.6 %shard_map.83 = (f32[64,1024]{1,0:T(8,128)}, f32[64,1024]{1,0:T(8,128)}) custom-call(f32[64,1024]{1,0:T(8,128)} %reshape.50.cur_ref, f32[16,1024]{1,0:T(8,128)} %copy-done.13, f32[16,1024]{1,0:T(8,128)} %copy-done.14, f32[64,128]{1,0:T(8,128)} %copy-done.17, f32[64,128]{1,0:T(8,128)} %copy-done.18, f32[64,1024]{1,0:T(8,128)} %broadcast_bitcast_fusion.3.fx_ref, ...), custom_call_target="tpu_custom_call" | custom-call | tf_op jit(solution)/shard_map/pallas_call | solution.py:192
  42.1 5.6 %collective-permute-done.5.hzm_ref = f32[64,128]{1,0:T(8,128)S(1)} collective-permute-done((f32[64,128]{1,0:T(8,128)S(1)}, f32[64,128]{1,0:T(8,128)S(1)}, u32[]{:S(2)}, u32[]{:S(2)}) %collective-permute-start.5) | collective-permute-done | bytes 32800 | tf_op jit(solution)/shard_map/ppermute | solution.py:265
  47.7 0.8 all-to-all-done
  48.5 3.4 %copy-done = bf16[4,1024,1024]{2,1,0:T(8,128)(2,1)S(1)} copy-done((bf16[4,1024,1024]{2,1,0:T(8,128)(2,1)S(1)}, bf16[4,1024,1024]{2,1,0:T(8,128)(2,1)}, u32[]{:S(2)}) %copy-start) | copy-done | bytes 8388632
  51.9 0.9 copy-done.9
  52.9 0.9 copy-done.10
  53.8 5.5 %shard_map.84 = (f32[64,1024]{1,0:T(8,128)S(1)}, bf16[512,1024]{1,0:T(8,128)(2,1)}) custom-call(bf16[512,64]{1,0:T(8,128)(2,1)S(1)} %copy-done.6, bf16[256,512]{1,0:T(8,128)(2,1)S(1)} %fusion.3.sel_ref, bf16[512,1024]{1,0:T(8,128)(2,1)S(1)} %bitcast.33, f32[64,1024]{1,0:T(8,128)S(1)} %copy-done.2, f32[64,1024]{1,0:T(8,128)S(1)} %copy-done.9, ...), custom_call_target="tpu_custom_call" | custom-call | tf_op jit(solution)/shard_map/pallas_call | solution.py:175
  60.0 6.0 %all-to-all-start.1 = ((bf16[32,16,1024]{2,1,0:T(8,128)(2,1)}), bf16[32,16,1024]{2,1,0:T(8,128)(2,1)S(1)}, u32[]{:S(2)}, u32[]{:S(2)}) async-start(bf16[32,16,1024]{2,1,0:T(8,128)(2,1)} %bitcast.7), calls=%async_computation.1 | async-start | bytes 2097152 | tf_op jit(solution)/shard_map/all_to_all | solution.py:268
  66.1 2.6 %shard_map.85 = (f32[64,128]{1,0:T(8,128)}, f32[64,128]{1,0:T(8,128)}, f32[64,128]{1,0:T(8,128)}, f32[64,128]{1,0:T(8,128)}) custom-call(f32[64,1024]{1,0:T(8,128)} %copy-done.3), custom_call_target="tpu_custom_call" | custom-call | tf_op jit(solution)/shard_map/pallas_call | solution.py:165
  69.3 0.8 collective-permute-start.8
  70.1 2.4 %collective-permute-start.9 = (f32[64,128]{1,0:T(8,128)}, f32[64,128]{1,0:T(8,128)S(1)}, u32[]{:S(2)}, u32[]{:S(2)}) collective-permute-start(f32[64,128]{1,0:T(8,128)} %get-tuple-element.30), channel_id=1, source_target_pairs={{0,32},{32,64},{64,96},{96,0},{1,33},{33,65},{65,97},{97,1},{2,34}... | collective-permute-start | bytes 98312 | tf_op jit(solution)/shard_map/ppermute | solution.py:263
  72.5 5.2 %collective-permute-start.10 = (f32[64,128]{1,0:T(8,128)}, f32[64,128]{1,0:T(8,128)S(1)}, u32[]{:S(2)}, u32[]{:S(2)}) collective-permute-start(f32[64,128]{1,0:T(8,128)} %get-tuple-element.33), channel_id=1, source_target_pairs={{1,0},{2,1},{3,2},{4,3},{5,4},{6,5},{7,6},{8,7},{9,8},{10,9},{11,1... | collective-permute-start | bytes 98312 | tf_op jit(solution)/shard_map/ppermute | solution.py:266
  79.0 2.6 %shard_map.86 = (f32[64,1024]{1,0:T(8,128)}, f32[64,1024]{1,0:T(8,128)}) custom-call(f32[64,1024]{1,0:T(8,128)} %copy-done.3, f32[16,1024]{1,0:T(8,128)} %copy-done.16, f32[16,1024]{1,0:T(8,128)} %copy-done.15, f32[64,128]{1,0:T(8,128)} %copy-done.19, f32[64,128]{1,0:T(8,128)} %copy-done.20, f32[64,1024]{1,0:T(8,128)} %broadcast_bitcast_fusion.3.fx_ref, ...), custom_call_target="tpu_custom_call" | custom-call | tf_op jit(solution)/shard_map/pallas_call | solution.py:192
  81.6 5.0 %collective-permute-done.10.hzp_ref = f32[64,128]{1,0:T(8,128)S(1)} collective-permute-done((f32[64,128]{1,0:T(8,128)}, f32[64,128]{1,0:T(8,128)S(1)}, u32[]{:S(2)}, u32[]{:S(2)}) %collective-permute-start.10) | collective-permute-done | bytes 32800 | tf_op jit(solution)/shard_map/ppermute | solution.py:266
  86.6 6.3 %collective-permute-done.11.hzm_ref = f32[64,128]{1,0:T(8,128)S(1)} collective-permute-done((f32[64,128]{1,0:T(8,128)}, f32[64,128]{1,0:T(8,128)S(1)}, u32[]{:S(2)}, u32[]{:S(2)}) %collective-permute-start.11) | collective-permute-done | bytes 32800 | tf_op jit(solution)/shard_map/ppermute | solution.py:265
  93.2 3.4 %copy-done.1 = bf16[4,1024,1024]{2,1,0:T(8,128)(2,1)S(1)} copy-done((bf16[4,1024,1024]{2,1,0:T(8,128)(2,1)S(1)}, bf16[4,1024,1024]{2,1,0:T(8,128)(2,1)}, u32[]{:S(2)}) %copy-start.1) | copy-done | bytes 8388632
  96.6 0.9 copy-done.7
  97.5 0.9 copy-done.8
  98.5 4.3 %shard_map.87 = f32[64,1024]{1,0:T(8,128)S(1)} custom-call(bf16[512,64]{1,0:T(8,128)(2,1)S(1)} %copy-done.6, bf16[256,512]{1,0:T(8,128)(2,1)S(1)} %fusion.3.sel_ref, bf16[512,1024]{1,0:T(8,128)(2,1)S(1)} %bitcast.34, f32[64,1024]{1,0:T(8,128)S(1)} %copy-done.5, f32[64,1024]{1,0:T(8,128)S(1)} %copy-done.7, f32[64,1024]{1,0:T(8,128)S(1)} %copy-done.8, ...), custom_call_target="tpu_custom_call" | custom-call | tf_op jit(solution)/shard_map/pallas_call | solution.py:175
  102.8 2.0 %reshape.59 = f32[8,8,4,16,16]{4,3,2,1,0:T(8,128)} reshape(f32[64,1024]{1,0:T(8,128)S(1)} %shard_map.87) | data formatting | bytes 524288 | tf_op jit(solution)/shard_map/reshape | solution.py:276
  (94 shorter events, 8.5 us)
Async XLA Ops:
  1.1 19.3 %copy-start.11 = (f32[8,8,4,16,16]{4,3,2,1,0:T(8,128)S(1)}, f32[8,8,4,16,16]{4,3,2,1,0:T(8,128)}, u32[]{:S(2)}) copy-start(f32[8,8,4,16,16]{4,3,2,1,0:T(8,128)} %param.8) | copy-start | bytes 786436
  8.9 39.6 %all-to-all-start = ((bf16[32,16,1024]{2,1,0:T(8,128)(2,1)}), bf16[32,16,1024]{2,1,0:T(8,128)(2,1)S(1)}, u32[]{:S(2)}, u32[]{:S(2)}) async-start(bf16[32,16,1024]{2,1,0:T(8,128)(2,1)} %bitcast.35), calls=%async_computation | async-start | bytes 2097152 | tf_op jit(solution)/shard_map/all_to_all | solution.py:268
  20.4 12.9 %copy-start.12 = (f32[8,4,16,16]{3,2,1,0:T(8,128)S(1)}, f32[8,4,16,16]{3,2,1,0:T(8,128)}, u32[]{:S(2)}) copy-start(f32[8,4,16,16]{3,2,1,0:T(8,128)} %param.10) | copy-start | bytes 98308
  21.5 13.7 %copy-start.23 = (s32[1,1,1,32]{3,2,1,0:T(1,128)S(1)}, s32[1,1,1,32]{3,2,1,0:T(1,128)}, u32[]{:S(2)}) copy-start(s32[1,1,1,32]{3,2,1,0:T(1,128)} %param.15) | copy-start | bytes 388
  22.9 16.0 %collective-permute-start = (f32[16,1024]{1,0:T(8,128)S(1)}, f32[16,1024]{1,0:T(8,128)S(1)}, u32[]{:S(2)}, u32[]{:S(2)}) collective-permute-start(f32[16,1024]{1,0:T(8,128)S(1)} %slice.28), channel_id=1, source_target_pairs={{0,128},{128,0},{1,129},{129,1},{2,130},{130,2},{3,131},{131,3},{4... | collective-permute-start | bytes 196616 | tf_op jit(solution)/shard_map/ppermute | solution.py:261
  24.3 12.9 %copy-start.21 = (s32[1,1,1,32,2]{3,4,2,1,0:T(2,128)S(1)}, s32[1,1,1,32,2]{3,4,2,1,0:T(2,128)}, u32[]{:S(2)}) copy-start(s32[1,1,1,32,2]{3,4,2,1,0:T(2,128)} %param.13) | copy-start | bytes 772
  24.3 13.1 %copy-start.22 = (s32[1,1,1,32,2]{3,4,2,1,0:T(2,128)S(1)}, s32[1,1,1,32,2]{3,4,2,1,0:T(2,128)}, u32[]{:S(2)}) copy-start(s32[1,1,1,32,2]{3,4,2,1,0:T(2,128)} %param.14) | copy-start | bytes 772
  24.3 13.7 %copy-start.24 = (f32[64,128]{1,0:T(8,128)S(1)}, f32[64,128]{1,0:T(8,128)}, u32[]{:S(2)}) copy-start(f32[64,128]{1,0:T(8,128)} %get-tuple-element.26) | copy-start | bytes 98308
  24.3 14.6 %collective-permute-start.1 = (f32[16,1024]{1,0:T(8,128)S(1)}, f32[16,1024]{1,0:T(8,128)S(1)}, u32[]{:S(2)}, u32[]{:S(2)}) collective-permute-start(f32[16,1024]{1,0:T(8,128)S(1)} %slice.30), channel_id=1, source_target_pairs={{128,0},{0,128},{129,1},{1,129},{130,2},{2,130},{131,3},{3,131},{1... | collective-permute-start | bytes 196616 | tf_op jit(solution)/shard_map/ppermute | solution.py:262
  24.9 13.1 %collective-permute-start.2 = (f32[64,128]{1,0:T(8,128)}, f32[64,128]{1,0:T(8,128)S(1)}, u32[]{:S(2)}, u32[]{:S(2)}) collective-permute-start(f32[64,128]{1,0:T(8,128)} %get-tuple-element.21), channel_id=1, source_target_pairs={{32,0},{64,32},{96,64},{0,96},{33,1},{65,33},{97,65},{1,97},{34,2}... | collective-permute-start | bytes 98312 | tf_op jit(solution)/shard_map/ppermute | solution.py:264
  25.7 13.1 %collective-permute-start.3 = (f32[64,128]{1,0:T(8,128)}, f32[64,128]{1,0:T(8,128)S(1)}, u32[]{:S(2)}, u32[]{:S(2)}) collective-permute-start(f32[64,128]{1,0:T(8,128)} %get-tuple-element.22), channel_id=1, source_target_pairs={{0,32},{32,64},{64,96},{96,0},{1,33},{33,65},{65,97},{97,1},{2,34}... | collective-permute-start | bytes 98312 | tf_op jit(solution)/shard_map/ppermute | solution.py:263
  28.1 14.0 %collective-permute-start.4 = (f32[64,128]{1,0:T(8,128)}, f32[64,128]{1,0:T(8,128)S(1)}, u32[]{:S(2)}, u32[]{:S(2)}) collective-permute-start(f32[64,128]{1,0:T(8,128)} %get-tuple-element.25), channel_id=1, source_target_pairs={{1,0},{2,1},{3,2},{4,3},{5,4},{6,5},{7,6},{8,7},{9,8},{10,9},{11,1... | collective-permute-start | bytes 98312 | tf_op jit(solution)/shard_map/ppermute | solution.py:266
  34.7 13.9 %copy-start.2 = (f32[64,1024]{1,0:T(8,128)S(1)}, f32[64,1024]{1,0:T(8,128)}, u32[]{:S(2)}) copy-start(f32[64,1024]{1,0:T(8,128)} %reshape.50.cur_ref) | copy-start | bytes 786436
  34.7 13.8 %copy-start.6 = (bf16[512,64]{1,0:T(8,128)(2,1)S(1)}, bf16[512,64]{1,0:T(8,128)(2,1)}, u32[]{:S(2)}) copy-start(bf16[512,64]{1,0:T(8,128)(2,1)} %fusion.7.pick_ref) | copy-start | bytes 196612
  37.9 0.9 copy-start.17
  38.0 9.7 %collective-permute-start.5 = (f32[64,128]{1,0:T(8,128)S(1)}, f32[64,128]{1,0:T(8,128)S(1)}, u32[]{:S(2)}, u32[]{:S(2)}) collective-permute-start(f32[64,128]{1,0:T(8,128)S(1)} %copy-done.24), channel_id=1, source_target_pairs={{0,1},{1,2},{2,3},{3,4},{4,5},{5,6},{6,7},{7,8},{8,9},{9,10},{10,1... | collective-permute-start | bytes 98312 | tf_op jit(solution)/shard_map/ppermute | solution.py:265
  48.5 3.4 %copy-start = (bf16[4,1024,1024]{2,1,0:T(8,128)(2,1)S(1)}, bf16[4,1024,1024]{2,1,0:T(8,128)(2,1)}, u32[]{:S(2)}) copy-start(bf16[4,1024,1024]{2,1,0:T(8,128)(2,1)} %w_hbm.3) | copy-start | bytes 25165828
  51.9 0.9 copy-start.9
  52.8 0.9 copy-start.10
  59.3 0.7 copy-start.3
  60.0 8.6 %copy-start.4 = (f32[64,1024]{1,0:T(8,128)S(1)}, f32[64,1024]{1,0:T(8,128)}, u32[]{:S(2)}) copy-start(f32[64,1024]{1,0:T(8,128)} %copy-done.3) | copy-start | bytes 786436
  60.0 33.2 %copy-start.5 = (f32[64,1024]{1,0:T(8,128)S(1)}, f32[64,1024]{1,0:T(8,128)}, u32[]{:S(2)}) copy-start(f32[64,1024]{1,0:T(8,128)} %copy-done.3) | copy-start | bytes 786436
  60.0 33.2 %all-to-all-start.1 = ((bf16[32,16,1024]{2,1,0:T(8,128)(2,1)}), bf16[32,16,1024]{2,1,0:T(8,128)(2,1)S(1)}, u32[]{:S(2)}, u32[]{:S(2)}) async-start(bf16[32,16,1024]{2,1,0:T(8,128)(2,1)} %bitcast.7), calls=%async_computation.1 | async-start | bytes 2097152 | tf_op jit(solution)/shard_map/all_to_all | solution.py:268
  68.7 9.1 %collective-permute-start.7 = (f32[16,1024]{1,0:T(8,128)S(1)}, f32[16,1024]{1,0:T(8,128)S(1)}, u32[]{:S(2)}, u32[]{:S(2)}) collective-permute-start(f32[16,1024]{1,0:T(8,128)S(1)} %get-tuple-element.40), channel_id=1, source_target_pairs={{128,0},{0,128},{129,1},{1,129},{130,2},{2,130},{131,3},{3,131},{1... | collective-permute-start | bytes 196616 | tf_op jit(solution)/shard_map/ppermute | solution.py:262
  68.8 9.0 %collective-permute-start.6 = (f32[16,1024]{1,0:T(8,128)S(1)}, f32[16,1024]{1,0:T(8,128)S(1)}, u32[]{:S(2)}, u32[]{:S(2)}) collective-permute-start(f32[16,1024]{1,0:T(8,128)S(1)} %get-tuple-element.41), channel_id=1, source_target_pairs={{0,128},{128,0},{1,129},{129,1},{2,130},{130,2},{3,131},{131,3},{4... | collective-permute-start | bytes 196616 | tf_op jit(solution)/shard_map/ppermute | solution.py:261
  69.3 8.4 %collective-permute-start.8 = (f32[64,128]{1,0:T(8,128)}, f32[64,128]{1,0:T(8,128)S(1)}, u32[]{:S(2)}, u32[]{:S(2)}) collective-permute-start(f32[64,128]{1,0:T(8,128)} %get-tuple-element.29), channel_id=1, source_target_pairs={{32,0},{64,32},{96,64},{0,96},{33,1},{65,33},{97,65},{1,97},{34,2}... | collective-permute-start | bytes 98312 | tf_op jit(solution)/shard_map/ppermute | solution.py:264
  70.1 7.6 %collective-permute-start.9 = (f32[64,128]{1,0:T(8,128)}, f32[64,128]{1,0:T(8,128)S(1)}, u32[]{:S(2)}, u32[]{:S(2)}) collective-permute-start(f32[64,128]{1,0:T(8,128)} %get-tuple-element.30), channel_id=1, source_target_pairs={{0,32},{32,64},{64,96},{96,0},{1,33},{33,65},{65,97},{97,1},{2,34}... | collective-permute-start | bytes 98312 | tf_op jit(solution)/shard_map/ppermute | solution.py:263
  72.5 14.1 %collective-permute-start.10 = (f32[64,128]{1,0:T(8,128)}, f32[64,128]{1,0:T(8,128)S(1)}, u32[]{:S(2)}, u32[]{:S(2)}) collective-permute-start(f32[64,128]{1,0:T(8,128)} %get-tuple-element.33), channel_id=1, source_target_pairs={{1,0},{2,1},{3,2},{4,3},{5,4},{6,5},{7,6},{8,7},{9,8},{10,9},{11,1... | collective-permute-start | bytes 98312 | tf_op jit(solution)/shard_map/ppermute | solution.py:266
  77.7 15.2 %collective-permute-start.11 = (f32[64,128]{1,0:T(8,128)}, f32[64,128]{1,0:T(8,128)S(1)}, u32[]{:S(2)}, u32[]{:S(2)}) collective-permute-start(f32[64,128]{1,0:T(8,128)} %get-tuple-element.34), channel_id=1, source_target_pairs={{0,1},{1,2},{2,3},{3,4},{4,5},{5,6},{6,7},{7,8},{8,9},{9,10},{10,1... | collective-permute-start | bytes 98312 | tf_op jit(solution)/shard_map/ppermute | solution.py:265
  93.2 3.4 %copy-start.1 = (bf16[4,1024,1024]{2,1,0:T(8,128)(2,1)S(1)}, bf16[4,1024,1024]{2,1,0:T(8,128)(2,1)}, u32[]{:S(2)}) copy-start(bf16[4,1024,1024]{2,1,0:T(8,128)(2,1)} %w_hbm.3) | copy-start | bytes 25165828
  96.6 0.9 copy-start.7
  97.5 0.9 copy-start.8
  (7 other events, 4.3 us)

commit v6 on v4

--- a/solution.py
+++ b/solution.py
@@ -67,10 +67,10 @@
     ).astype(BF16)
 
 
-def _prep_kernel(pick_ref, cur_ref, snd_ref, zlo_ref, zhi_ref, ylo_ref, yhi_ref):
-    cur = cur_ref[...]
-    _emit_send(pick_ref, cur, snd_ref)
-    _emit_halos(cur, zlo_ref, zhi_ref, ylo_ref, yhi_ref)
+def _send_kernel(pick_ref, rnd_ref, snd_ref):
+    snd_ref[...] = jnp.dot(
+        pick_ref[...], rnd_ref[...], preferred_element_type=F32
+    ).astype(BF16)
 
 
 def _halo_kernel(cur_ref, zlo_ref, zhi_ref, ylo_ref, yhi_ref):
@@ -159,10 +159,9 @@
     return jax.ShapeDtypeStruct((peers * both, lanes), BF16)
 
 
-def _prep(pick, cur, peers, both):
-    halo = jax.ShapeDtypeStruct((cur.shape[0], 128), F32)
-    shapes = [_send_shape(cur.shape[1], peers, both)] + [halo] * 4
-    return pl.pallas_call(_prep_kernel, out_shape=shapes)(pick, cur)
+def _send(pick, rnd, peers, both):
+    shape = _send_shape(rnd.shape[1], peers, both)
+    return pl.pallas_call(_send_kernel, out_shape=shape)(pick, rnd)
 
 
 def _halos(cur):
@@ -260,12 +259,12 @@
     up_y, down_y = _ring("ky")
     up_z, down_z = _ring("kz")
 
-    cur = populations.reshape(rows, lanes)
-    snd, zlo, zhi, ylo, yhi = _prep(pick, cur, peer_count, both)
+    snd = _send(pick, populations.astype(BF16).reshape(rows, lanes), peer_count, both)
+    _, later = lax.optimization_barrier((snd, populations))
+    cur = later.reshape(rows, lanes)
     for iteration in range(ITERS):
         last = iteration + 1 == ITERS
-        if iteration > 0:
-            zlo, zhi, ylo, yhi = _halos(cur)
+        zlo, zhi, ylo, yhi = _halos(cur)
         xlo = lax.ppermute(cur[rows - 16:], "kx", up_x)
         xhi = lax.ppermute(cur[:16], "kx", down_x)
         hym = lax.ppermute(yhi, "ky", up_y)

time: 104 us -> 106 us (1.019)
  waiting for transfers between devices: 16.6 us -> 14.2 us
  Pallas kernels: 27.5 us -> 29.5 us
  other arithmetic: 2.35 us -> 4.09 us
    ppermute x2, waiting for transfers between devices: 10.5 us -> 6.74 us  [per_device(): hzm = lax.ppermute(zhi, 'kz', up_z)]
    pallas_call x1 -> x2, Pallas kernels: 2.57 us -> 5.13 us  [_halos(): return pl.pallas_call(_halo_kernel, out_shape=[halo] * 4)(cur)]
    convert_element_type x0 -> x1, other arithmetic: none -> 1.8 us  [per_device(): populations.astype(BF16).reshape(rows, lanes)]
    ppermute x2, waiting for transfers between devices: 4.97 us -> 6.15 us  [per_device(): hzp = lax.ppermute(zlo, 'kz', down_z)]
    all_to_all x2, starting transfers between devices: 17.5 us -> 18.6 us  [per_device(): lax.all_to_all(outgoing, 'kz', split_axis=0, concat_axis=0, tiled=True)]
    reshape x1 -> x2, local copies, waits for them, and re-layouts: 3.99 us -> 4.71 us  [the longest x1 2.46 us: per_device(): populations.astype(BF16).reshape(rows, lanes)]
    unnamed x51 -> x45, local copies, waits for them, and re-layouts: 4.82 us -> 4.77 us
  transfers between devices with their start and end apart: 14 -> 14, of which waited for: 5 -> 5; matrix products, arithmetic and copies ran while one was open for 10% -> 11% of each run, Pallas kernels for 8% -> 10%
where the time goes in v6:
time: 106 us; the launch traced here: 105 us
  starting transfers between devices  36.9 us (35%)
  Pallas kernels  29.5 us (28%)
  local copies, waits for them, and re-layouts  20.3 us (19%)
  waiting for transfers between devices  14.2 us (13%)
  other arithmetic  4.09 us (4%)
    all_to_all x2, starting transfers between devices, per_device(): lax.all_to_all(outgoing, 'kz', split_axis=0, concat_axis=0, tiled=True)  18.6 us
    pallas_call x2, Pallas kernels, _finish(): pl.pallas_call(functools.partial(_finish_kernel, last), out_shape=shapes,...  16.8 us
    ppermute x2, starting transfers between devices, per_device(): hzp = lax.ppermute(zlo, 'kz', down_z)  10.4 us
    ppermute x2, waiting for transfers between devices, per_device(): hzm = lax.ppermute(zhi, 'kz', up_z)  6.74 us
    ppermute x2, waiting for transfers between devices, per_device(): hzp = lax.ppermute(zlo, 'kz', down_z)  6.15 us
    ppermute x2, starting transfers between devices, per_device(): hym = lax.ppermute(yhi, 'ky', up_y)  5.64 us
    pallas_call x2, Pallas kernels, _drift(): pl.pallas_call(_drift_kernel, out_shape=[plane, plane], scratch_shapes=[p...  5.25 us
    pallas_call x2, Pallas kernels, _halos(): return pl.pallas_call(_halo_kernel, out_shape=[halo] * 4)(cur)  5.13 us
  transfers between devices with their start and end apart: 14, of which 5 were waited for; matrix products, arithmetic and copies ran while one was open for 11% of the time, Pallas kernels for 10%

profile of v6, /device:TPU:6, one launch (start us, length us, event | category | flops | bytes accessed | tf_op | source)
XLA Modules:
  0.0 105.4 jit_solution(9056109762797575168)
XLA Ops:
  0.0 0.8 copy.12
  1.1 1.8 %convert_element_type.11 = bf16[8,8,4,16,16]{4,3,2,1,0:T(8,128)(2,1)S(1)} convert(f32[8,8,4,16,16]{4,3,2,1,0:T(8,128)} %param.8) | non-fusion elementwise | flops 65536 | bytes 393216 | tf_op jit(solution)/shard_map/convert_element_type | solution.py:262
  2.9 2.5 %reshape.53.rnd_ref = bf16[64,1024]{1,0:T(8,128)(2,1)} reshape(bf16[8,8,4,16,16]{4,3,2,1,0:T(8,128)(2,1)S(1)} %convert_element_type.11) | data formatting | bytes 262144 | tf_op jit(solution)/shard_map/reshape | solution.py:262
  5.4 1.0 fusion.7.pick_ref
  6.3 2.3 %shard_map.82 = bf16[512,1024]{1,0:T(8,128)(2,1)} custom-call(bf16[512,64]{1,0:T(8,128)(2,1)} %fusion.7.pick_ref, bf16[64,1024]{1,0:T(8,128)(2,1)} %reshape.53.rnd_ref), custom_call_target="tpu_custom_call" | custom-call | tf_op jit(solution)/shard_map/pallas_call | solution.py:164
  8.7 11.5 %all-to-all-start = ((bf16[32,16,1024]{2,1,0:T(8,128)(2,1)}), bf16[32,16,1024]{2,1,0:T(8,128)(2,1)S(1)}, u32[]{:S(2)}, u32[]{:S(2)}) async-start(bf16[32,16,1024]{2,1,0:T(8,128)(2,1)} %bitcast.35), calls=%async_computation | async-start | bytes 2097152 | tf_op jit(solution)/shard_map/all_to_all | solution.py:275
  20.2 2.3 %reshape.56.cur_ref = f32[64,1024]{1,0:T(8,128)} reshape(f32[8,8,4,16,16]{4,3,2,1,0:T(8,128)S(1)} %copy-done) | data formatting | bytes 524288 | tf_op jit(solution)/shard_map/reshape | solution.py:264
  22.4 2.6 %shard_map.83 = (f32[64,128]{1,0:T(8,128)}, f32[64,128]{1,0:T(8,128)}, f32[64,128]{1,0:T(8,128)}, f32[64,128]{1,0:T(8,128)}) custom-call(f32[64,1024]{1,0:T(8,128)} %reshape.56.cur_ref), custom_call_target="tpu_custom_call" | custom-call | tf_op jit(solution)/shard_map/pallas_call | solution.py:169
  25.0 0.8 collective-permute-start.2
  25.8 2.4 %collective-permute-start.3 = (f32[64,128]{1,0:T(8,128)}, f32[64,128]{1,0:T(8,128)S(1)}, u32[]{:S(2)}, u32[]{:S(2)}) collective-permute-start(f32[64,128]{1,0:T(8,128)} %get-tuple-element.22), channel_id=1, source_target_pairs={{0,32},{32,64},{64,96},{96,0},{1,33},{33,65},{65,97},{97,1},{2,34}... | collective-permute-start | bytes 98312 | tf_op jit(solution)/shard_map/ppermute | solution.py:270
  28.3 5.2 %collective-permute-start.4 = (f32[64,128]{1,0:T(8,128)}, f32[64,128]{1,0:T(8,128)S(1)}, u32[]{:S(2)}, u32[]{:S(2)}) collective-permute-start(f32[64,128]{1,0:T(8,128)} %get-tuple-element.25), channel_id=1, source_target_pairs={{1,0},{2,1},{3,2},{4,3},{5,4},{6,5},{7,6},{8,7},{9,8},{10,9},{11,1... | collective-permute-start | bytes 98312 | tf_op jit(solution)/shard_map/ppermute | solution.py:273
  33.5 1.1 %fusion.16 = (f32[2,8,4,16,16]{4,3,2,1,0:T(8,128)}, f32[2,8,4,16,16]{4,3,2,1,0:T(8,128)}) fusion(f32[8,8,4,16,16]{4,3,2,1,0:T(8,128)S(1)} %copy-done), kind=kLoop, calls=%fused_computation.47 | loop fusion | bytes 262144 | tf_op jit(solution)/shard_map/slice | solution.py:269
  34.5 1.3 %slice.28 = f32[16,1024]{1,0:T(8,128)S(1)} reshape(f32[2,8,4,16,16]{4,3,2,1,0:T(8,128)} %get-tuple-element.36) | data formatting | bytes 131072 | tf_op jit(solution)/shard_map/slice | solution.py:268
  36.2 1.2 %fusion.17 = (f32[8,1,4,16,16]{4,3,2,1,0:T(8,128)S(1)}, f32[8,1,4,16,16]{4,3,2,1,0:T(8,128)S(1)}, f32[8,1,4,16,16]{4,3,2,1,0:T(8,128)S(1)}) fusion(f32[8,3,4,16,16]{4,3,2,1,0:T(8,128)} %param.9), kind=kLoop, calls=%fused_computation.48 | loop fusion | bytes 196608 | tf_op jit(solution)/shard_map/slice | solution.py:255
  37.9 0.7 broadcast_bitcast_fusion.3.fx_ref
  39.4 0.9 broadcast_bitcast_fusion.1
  41.6 0.8 collective-permute-start.1
  42.3 1.2 %fusion.3.sel_ref = bf16[256,512]{1,0:T(8,128)(2,1)} fusion(s32[512]{0:T(512)S(1)} %get-tuple-element.42, s32[512]{0:T(512)S(1)} %get-tuple-element.43, s32[256]{0:T(256)S(1)} %get-tuple-element.54, s32[256]{0:T(256)S(1)} %get-tuple-element.55, s32[512]{0:T(512)S(1)} %eq.50, s32[256]{0:T(256)S(1)} %get-tuple-element.51, s32[256]{0:T(256)S(1)} %get-tuple-element.56, ...), kind=kLoop, calls=%fused_computation.10 | loop fusion | flops 2883584 | bytes 278272 | tf_op jit(solution)/shard_map/convert_element_type | solution.py:242
  44.2 2.6 %shard_map.84 = (f32[64,1024]{1,0:T(8,128)}, f32[64,1024]{1,0:T(8,128)}) custom-call(f32[64,1024]{1,0:T(8,128)} %reshape.56.cur_ref, f32[16,1024]{1,0:T(8,128)} %copy-done.6, f32[16,1024]{1,0:T(8,128)} %copy-done.9, f32[64,128]{1,0:T(8,128)} %copy-done.14, f32[64,128]{1,0:T(8,128)} %copy-done.15, f32[64,1024]{1,0:T(8,128)} %broadcast_bitcast_fusion.3.fx_ref, ...), custom_call_target="tpu_custom_call" | custom-call | tf_op jit(solution)/shard_map/pallas_call | solution.py:199
  47.5 0.8 all-to-all-done
  48.3 1.0 copy-done.1
  49.2 8.8 %shard_map.85 = (f32[64,1024]{1,0:T(8,128)}, bf16[512,1024]{1,0:T(8,128)(2,1)}) custom-call(bf16[512,64]{1,0:T(8,128)(2,1)} %fusion.7.pick_ref, bf16[256,512]{1,0:T(8,128)(2,1)} %fusion.3.sel_ref, bf16[512,1024]{1,0:T(8,128)(2,1)} %bitcast.36, f32[64,1024]{1,0:T(8,128)} %reshape.56.cur_ref, f32[64,1024]{1,0:T(8,128)} %get-tuple-element.23.a_ref, ...), custom_call_target="tpu_custom_call" | custom-call | tf_op jit(solution)/shard_map/pallas_call | solution.py:179
  58.0 7.1 %all-to-all-start.1 = ((bf16[32,16,1024]{2,1,0:T(8,128)(2,1)}), bf16[32,16,1024]{2,1,0:T(8,128)(2,1)S(1)}, u32[]{:S(2)}, u32[]{:S(2)}) async-start(bf16[32,16,1024]{2,1,0:T(8,128)(2,1)} %bitcast.38), calls=%async_computation.1 | async-start | bytes 2097152 | tf_op jit(solution)/shard_map/all_to_all | solution.py:275
  65.1 2.6 %shard_map.86 = (f32[64,128]{1,0:T(8,128)}, f32[64,128]{1,0:T(8,128)}, f32[64,128]{1,0:T(8,128)}, f32[64,128]{1,0:T(8,128)}) custom-call(f32[64,1024]{1,0:T(8,128)} %get-tuple-element.28.cur_ref), custom_call_target="tpu_custom_call" | custom-call | tf_op jit(solution)/shard_map/pallas_call | solution.py:169
  68.3 3.2 %collective-permute-start.9 = (f32[64,128]{1,0:T(8,128)}, f32[64,128]{1,0:T(8,128)S(1)}, u32[]{:S(2)}, u32[]{:S(2)}) collective-permute-start(f32[64,128]{1,0:T(8,128)} %get-tuple-element.30), channel_id=1, source_target_pairs={{0,32},{32,64},{64,96},{96,0},{1,33},{33,65},{65,97},{97,1},{2,34}... | collective-permute-start | bytes 98312 | tf_op jit(solution)/shard_map/ppermute | solution.py:270
  71.5 5.2 %collective-permute-start.10 = (f32[64,128]{1,0:T(8,128)}, f32[64,128]{1,0:T(8,128)S(1)}, u32[]{:S(2)}, u32[]{:S(2)}) collective-permute-start(f32[64,128]{1,0:T(8,128)} %get-tuple-element.33), channel_id=1, source_target_pairs={{1,0},{2,1},{3,2},{4,3},{5,4},{6,5},{7,6},{8,7},{9,8},{10,9},{11,1... | collective-permute-start | bytes 98312 | tf_op jit(solution)/shard_map/ppermute | solution.py:273
  78.0 2.6 %shard_map.87 = (f32[64,1024]{1,0:T(8,128)}, f32[64,1024]{1,0:T(8,128)}) custom-call(f32[64,1024]{1,0:T(8,128)} %get-tuple-element.28.cur_ref, f32[16,1024]{1,0:T(8,128)} %copy-done.8, f32[16,1024]{1,0:T(8,128)} %copy-done.7, f32[64,128]{1,0:T(8,128)} %copy-done.16, f32[64,128]{1,0:T(8,128)} %copy-done.17, f32[64,1024]{1,0:T(8,128)} %broadcast_bitcast_fusion.3.fx_ref, ...), custom_call_target="tpu_custom_call" | custom-call | tf_op jit(solution)/shard_map/pallas_call | solution.py:199
  80.7 6.1 %collective-permute-done.10.hzp_ref = f32[64,128]{1,0:T(8,128)S(1)} collective-permute-done((f32[64,128]{1,0:T(8,128)}, f32[64,128]{1,0:T(8,128)S(1)}, u32[]{:S(2)}, u32[]{:S(2)}) %collective-permute-start.10) | collective-permute-done | bytes 32800 | tf_op jit(solution)/shard_map/ppermute | solution.py:273
  86.8 6.0 %collective-permute-done.11.hzm_ref = f32[64,128]{1,0:T(8,128)S(1)} collective-permute-done((f32[64,128]{1,0:T(8,128)}, f32[64,128]{1,0:T(8,128)S(1)}, u32[]{:S(2)}, u32[]{:S(2)}) %collective-permute-start.11) | collective-permute-done | bytes 32800 | tf_op jit(solution)/shard_map/ppermute | solution.py:272
  93.5 0.9 copy-done.2
  94.4 8.0 %shard_map.88 = f32[64,1024]{1,0:T(8,128)} custom-call(bf16[512,64]{1,0:T(8,128)(2,1)} %fusion.7.pick_ref, bf16[256,512]{1,0:T(8,128)(2,1)} %fusion.3.sel_ref, bf16[512,1024]{1,0:T(8,128)(2,1)} %bitcast.37, f32[64,1024]{1,0:T(8,128)} %get-tuple-element.28.cur_ref, f32[64,1024]{1,0:T(8,128)} %get-tuple-element.31.a_ref, f32[64,1024]{1,0:T(8,128)} %get-tuple-element.32.q_ref, ...), custom_call_target="tpu_custom_call" | custom-call | tf_op jit(solution)/shard_map/pallas_call | solution.py:179
  102.4 3.0 %reshape.63 = f32[8,8,4,16,16]{4,3,2,1,0:T(8,128)} reshape(f32[64,1024]{1,0:T(8,128)} %shard_map.88) | data formatting | bytes 524288 | tf_op jit(solution)/shard_map/reshape | solution.py:283
  (89 shorter events, 6.9 us)
Async XLA Ops:
  2.9 17.3 %copy-start = (f32[8,8,4,16,16]{4,3,2,1,0:T(8,128)S(1)}, f32[8,8,4,16,16]{4,3,2,1,0:T(8,128)}, u32[]{:S(2)}) copy-start(f32[8,8,4,16,16]{4,3,2,1,0:T(8,128)} %param.8) | copy-start | bytes 786436
  8.7 39.6 %all-to-all-start = ((bf16[32,16,1024]{2,1,0:T(8,128)(2,1)}), bf16[32,16,1024]{2,1,0:T(8,128)(2,1)S(1)}, u32[]{:S(2)}, u32[]{:S(2)}) async-start(bf16[32,16,1024]{2,1,0:T(8,128)(2,1)} %bitcast.35), calls=%async_computation | async-start | bytes 2097152 | tf_op jit(solution)/shard_map/all_to_all | solution.py:275
  20.2 15.8 %copy-start.5 = (f32[8,4,16,16]{3,2,1,0:T(8,128)S(1)}, f32[8,4,16,16]{3,2,1,0:T(8,128)}, u32[]{:S(2)}) copy-start(f32[8,4,16,16]{3,2,1,0:T(8,128)} %param.10) | copy-start | bytes 98308
  25.0 16.5 %collective-permute-start.2 = (f32[64,128]{1,0:T(8,128)}, f32[64,128]{1,0:T(8,128)S(1)}, u32[]{:S(2)}, u32[]{:S(2)}) collective-permute-start(f32[64,128]{1,0:T(8,128)} %get-tuple-element.21), channel_id=1, source_target_pairs={{32,0},{64,32},{96,64},{0,96},{33,1},{65,33},{97,65},{1,97},{34,2}... | collective-permute-start | bytes 98312 | tf_op jit(solution)/shard_map/ppermute | solution.py:271
  25.8 17.7 %collective-permute-start.3 = (f32[64,128]{1,0:T(8,128)}, f32[64,128]{1,0:T(8,128)S(1)}, u32[]{:S(2)}, u32[]{:S(2)}) collective-permute-start(f32[64,128]{1,0:T(8,128)} %get-tuple-element.22), channel_id=1, source_target_pairs={{0,32},{32,64},{64,96},{96,0},{1,33},{33,65},{65,97},{97,1},{2,34}... | collective-permute-start | bytes 98312 | tf_op jit(solution)/shard_map/ppermute | solution.py:270
  28.3 18.5 %collective-permute-start.4 = (f32[64,128]{1,0:T(8,128)}, f32[64,128]{1,0:T(8,128)S(1)}, u32[]{:S(2)}, u32[]{:S(2)}) collective-permute-start(f32[64,128]{1,0:T(8,128)} %get-tuple-element.25), channel_id=1, source_target_pairs={{1,0},{2,1},{3,2},{4,3},{5,4},{6,5},{7,6},{8,7},{9,8},{10,9},{11,1... | collective-permute-start | bytes 98312 | tf_op jit(solution)/shard_map/ppermute | solution.py:273
  33.5 14.0 %collective-permute-start.5 = (f32[64,128]{1,0:T(8,128)}, f32[64,128]{1,0:T(8,128)S(1)}, u32[]{:S(2)}, u32[]{:S(2)}) collective-permute-start(f32[64,128]{1,0:T(8,128)} %get-tuple-element.26), channel_id=1, source_target_pairs={{0,1},{1,2},{2,3},{3,4},{4,5},{5,6},{6,7},{7,8},{8,9},{9,10},{10,1... | collective-permute-start | bytes 98312 | tf_op jit(solution)/shard_map/ppermute | solution.py:272
  34.5 3.3 %copy-start.20 = (s32[1,1,1,32]{3,2,1,0:T(1,128)S(1)}, s32[1,1,1,32]{3,2,1,0:T(1,128)}, u32[]{:S(2)}) copy-start(s32[1,1,1,32]{3,2,1,0:T(1,128)} %param.15) | copy-start | bytes 388
  35.9 4.7 %copy-start.18 = (s32[1,1,1,32,2]{3,4,2,1,0:T(2,128)S(1)}, s32[1,1,1,32,2]{3,4,2,1,0:T(2,128)}, u32[]{:S(2)}) copy-start(s32[1,1,1,32,2]{3,4,2,1,0:T(2,128)} %param.13) | copy-start | bytes 772
  35.9 4.9 %copy-start.19 = (s32[1,1,1,32,2]{3,4,2,1,0:T(2,128)S(1)}, s32[1,1,1,32,2]{3,4,2,1,0:T(2,128)}, u32[]{:S(2)}) copy-start(s32[1,1,1,32,2]{3,4,2,1,0:T(2,128)} %param.14) | copy-start | bytes 772
  35.9 5.4 %copy-start.4 = (f32[2,8,4,16,16]{4,3,2,1,0:T(8,128)S(1)}, f32[2,8,4,16,16]{4,3,2,1,0:T(8,128)}, u32[]{:S(2)}) copy-start(f32[2,8,4,16,16]{4,3,2,1,0:T(8,128)} %get-tuple-element.35) | copy-start | bytes 196612
  35.9 7.6 %collective-permute-start = (f32[16,1024]{1,0:T(8,128)S(1)}, f32[16,1024]{1,0:T(8,128)S(1)}, u32[]{:S(2)}, u32[]{:S(2)}) collective-permute-start(f32[16,1024]{1,0:T(8,128)S(1)} %slice.28), channel_id=1, source_target_pairs={{0,128},{128,0},{1,129},{129,1},{2,130},{130,2},{3,131},{131,3},{4... | collective-permute-start | bytes 196616 | tf_op jit(solution)/shard_map/ppermute | solution.py:268
  41.5 2.0 %copy-start.14 = (f32[64,128]{1,0:T(8,128)}, f32[64,128]{1,0:T(8,128)S(1)}, u32[]{:S(2)}) copy-start(f32[64,128]{1,0:T(8,128)S(1)} %collective-permute-done.2.hyp_ref) | copy-start | bytes 98308
  41.6 2.0 %collective-permute-start.1 = (f32[16,1024]{1,0:T(8,128)S(1)}, f32[16,1024]{1,0:T(8,128)S(1)}, u32[]{:S(2)}, u32[]{:S(2)}) collective-permute-start(f32[16,1024]{1,0:T(8,128)S(1)} %slice.30), channel_id=1, source_target_pairs={{128,0},{0,128},{129,1},{1,129},{130,2},{2,130},{131,3},{3,131},{1... | collective-permute-start | bytes 196616 | tf_op jit(solution)/shard_map/ppermute | solution.py:269
  43.5 0.6 copy-start.6
  43.5 0.6 copy-start.9
  46.8 1.5 %copy-start.10 = (f32[64,128]{1,0:T(8,128)}, f32[64,128]{1,0:T(8,128)S(1)}, u32[]{:S(2)}) copy-start(f32[64,128]{1,0:T(8,128)S(1)} %collective-permute-done.4.hzp_ref) | copy-start | bytes 98308
  47.5 0.8 copy-start.11
  48.2 1.0 copy-start.1
  58.0 9.7 %copy-start.3 = (f32[64,1024]{1,0:T(8,128)S(1)}, f32[64,1024]{1,0:T(8,128)}, u32[]{:S(2)}) copy-start(f32[64,1024]{1,0:T(8,128)} %get-tuple-element.28.cur_ref) | copy-start | bytes 786436
  58.0 35.4 %all-to-all-start.1 = ((bf16[32,16,1024]{2,1,0:T(8,128)(2,1)}), bf16[32,16,1024]{2,1,0:T(8,128)(2,1)S(1)}, u32[]{:S(2)}, u32[]{:S(2)}) async-start(bf16[32,16,1024]{2,1,0:T(8,128)(2,1)} %bitcast.38), calls=%async_computation.1 | async-start | bytes 2097152 | tf_op jit(solution)/shard_map/all_to_all | solution.py:275
  67.7 9.1 %collective-permute-start.7 = (f32[16,1024]{1,0:T(8,128)S(1)}, f32[16,1024]{1,0:T(8,128)S(1)}, u32[]{:S(2)}, u32[]{:S(2)}) collective-permute-start(f32[16,1024]{1,0:T(8,128)S(1)} %get-tuple-element.40), channel_id=1, source_target_pairs={{128,0},{0,128},{129,1},{1,129},{130,2},{2,130},{131,3},{3,131},{1... | collective-permute-start | bytes 196616 | tf_op jit(solution)/shard_map/ppermute | solution.py:269
  67.8 9.0 %collective-permute-start.6 = (f32[16,1024]{1,0:T(8,128)S(1)}, f32[16,1024]{1,0:T(8,128)S(1)}, u32[]{:S(2)}, u32[]{:S(2)}) collective-permute-start(f32[16,1024]{1,0:T(8,128)S(1)} %get-tuple-element.41), channel_id=1, source_target_pairs={{0,128},{128,0},{1,129},{129,1},{2,130},{130,2},{3,131},{131,3},{4... | collective-permute-start | bytes 196616 | tf_op jit(solution)/shard_map/ppermute | solution.py:268
  68.3 8.4 %collective-permute-start.8 = (f32[64,128]{1,0:T(8,128)}, f32[64,128]{1,0:T(8,128)S(1)}, u32[]{:S(2)}, u32[]{:S(2)}) collective-permute-start(f32[64,128]{1,0:T(8,128)} %get-tuple-element.29), channel_id=1, source_target_pairs={{32,0},{64,32},{96,64},{0,96},{33,1},{65,33},{97,65},{1,97},{34,2}... | collective-permute-start | bytes 98312 | tf_op jit(solution)/shard_map/ppermute | solution.py:271
  68.3 8.4 %collective-permute-start.9 = (f32[64,128]{1,0:T(8,128)}, f32[64,128]{1,0:T(8,128)S(1)}, u32[]{:S(2)}, u32[]{:S(2)}) collective-permute-start(f32[64,128]{1,0:T(8,128)} %get-tuple-element.30), channel_id=1, source_target_pairs={{0,32},{32,64},{64,96},{96,0},{1,33},{33,65},{65,97},{97,1},{2,34}... | collective-permute-start | bytes 98312 | tf_op jit(solution)/shard_map/ppermute | solution.py:270
  71.5 15.3 %collective-permute-start.10 = (f32[64,128]{1,0:T(8,128)}, f32[64,128]{1,0:T(8,128)S(1)}, u32[]{:S(2)}, u32[]{:S(2)}) collective-permute-start(f32[64,128]{1,0:T(8,128)} %get-tuple-element.33), channel_id=1, source_target_pairs={{1,0},{2,1},{3,2},{4,3},{5,4},{6,5},{7,6},{8,7},{9,8},{10,9},{11,1... | collective-permute-start | bytes 98312 | tf_op jit(solution)/shard_map/ppermute | solution.py:273
  76.7 16.1 %collective-permute-start.11 = (f32[64,128]{1,0:T(8,128)}, f32[64,128]{1,0:T(8,128)S(1)}, u32[]{:S(2)}, u32[]{:S(2)}) collective-permute-start(f32[64,128]{1,0:T(8,128)} %get-tuple-element.34), channel_id=1, source_target_pairs={{0,1},{1,2},{2,3},{3,4},{4,5},{5,6},{6,7},{7,8},{8,9},{9,10},{10,1... | collective-permute-start | bytes 98312 | tf_op jit(solution)/shard_map/ppermute | solution.py:272
  76.8 0.6 copy-start.7
  77.4 0.6 copy-start.8
  86.8 6.6 %copy-start.12 = (f32[64,128]{1,0:T(8,128)}, f32[64,128]{1,0:T(8,128)S(1)}, u32[]{:S(2)}) copy-start(f32[64,128]{1,0:T(8,128)S(1)} %collective-permute-done.10.hzp_ref) | copy-start | bytes 98308
  92.9 0.6 copy-start.13
  93.4 1.0 copy-start.2
  (3 other events, 1.8 us)

commit v7 on v4

--- a/solution.py
+++ b/solution.py
@@ -84,9 +84,11 @@
     else:
         out_ref, snd_ref, g_scr, acc_scr, p_scr = refs
     t = pl.program_id(0)
+    h = pl.program_id(1)
     rows, _ = cur_ref.shape
-
-    @pl.when(t == 0)
+    width = w_ref.shape[1]
+
+    @pl.when((t == 0) & (h == 0))
     def _():
         summed = jnp.dot(sel_ref[...], inc_ref[...], preferred_element_type=F32)
         g_scr[...] = summed.astype(BF16)
@@ -97,11 +99,12 @@
         p_scr[...] = cur - drift
 
     grouped = g_scr[pl.ds(pl.multiple_of(t * rows, rows), rows), :]
-    acc_scr[...] += lax.dot_general(
+    cols = pl.ds(pl.multiple_of(h * width, width), width)
+    acc_scr[:, cols] += lax.dot_general(
         grouped, w_ref[0], (((1,), (1,)), ((), ())), preferred_element_type=F32
     )
 
-    @pl.when(t == pl.num_programs(0) - 1)
+    @pl.when((t == pl.num_programs(0) - 1) & (h == pl.num_programs(1) - 1))
     def _():
         cur = (p_scr[...] + acc_scr[...]) - q_ref[...]
         out_ref[...] = cur
@@ -177,19 +180,21 @@
     if not last:
         shapes.append(_send_shape(lanes, peers, both))
     small = (pick, sel, inc, cur, a, q, fz, hzp, hzm)
+    halves = 2
+    block = (1, tiles.shape[1] // halves, tiles.shape[2])
     outs = pl.pallas_call(
         functools.partial(_finish_kernel, last),
         out_shape=shapes,
-        grid=(tile_count,),
+        grid=(tile_count, halves),
         in_specs=[_full(x.shape) for x in small]
-        + [pl.BlockSpec((1,) + tiles.shape[1:], lambda t: (t, 0, 0))],
+        + [pl.BlockSpec(block, lambda t, h: (t, h, 0))],
         out_specs=[_full(x.shape) for x in shapes],
         scratch_shapes=[
             pltpu.VMEM((tile_count * rows, lanes), BF16),
             pltpu.VMEM((rows, lanes), F32),
             pltpu.VMEM((rows, lanes), F32),
         ],
-        compiler_params=pltpu.CompilerParams(dimension_semantics=("arbitrary",)),
+        compiler_params=pltpu.CompilerParams(dimension_semantics=("arbitrary", "arbitrary")),
     )(*small, tiles)
     return outs[0], outs[1:]
 

time: 104 us -> 108 us (1.038)
  Pallas kernels: 27.5 us -> 31.2 us
    pallas_call x2, Pallas kernels: 16.8 us -> 20.5 us  [_finish(): pl.pallas_call(functools.partial(_finish_kernel, last), out_shape=shapes,...]
  transfers between devices with their start and end apart: 14 -> 14, of which waited for: 5 -> 5; matrix products, arithmetic and copies ran while one was open for 10% -> 9% of each run, Pallas kernels for 8% -> 7%
where the time goes in v7:
time: 108 us; the launch traced here: 107 us
  starting transfers between devices  35.9 us (33%)
  Pallas kernels  31.2 us (29%)
  local copies, waits for them, and re-layouts  20.7 us (19%)
  waiting for transfers between devices  16.6 us (15%)
  other arithmetic  2.35 us (2%)
    pallas_call x2, Pallas kernels, _finish(): pl.pallas_call(functools.partial(_finish_kernel, last), out_shape=shapes,...  20.5 us
    all_to_all x2, starting transfers between devices, per_device(): lax.all_to_all(outgoing, 'kz', split_axis=0, concat_axis=0, tiled=True)  17.5 us
    ppermute x2, waiting for transfers between devices, per_device(): hzm = lax.ppermute(zhi, 'kz', up_z)  10.5 us
    ppermute x2, starting transfers between devices, per_device(): hzp = lax.ppermute(zlo, 'kz', down_z)  10.4 us
    pallas_call x2, Pallas kernels, _drift(): pl.pallas_call(_drift_kernel, out_shape=[plane, plane], scratch_shapes=[p...  5.26 us
    ppermute x2, waiting for transfers between devices, per_device(): hzp = lax.ppermute(zlo, 'kz', down_z)  4.97 us
    unnamed x51, local copies, waits for them, and re-layouts  4.82 us
    ppermute x2, starting transfers between devices, per_device(): hym = lax.ppermute(yhi, 'ky', up_y)  4.82 us
  transfers between devices with their start and end apart: 14, of which 5 were waited for; matrix products, arithmetic and copies ran while one was open for 9% of the time, Pallas kernels for 7%

profile of v7, /device:TPU:6, one launch (start us, length us, event | category | flops | bytes accessed | tf_op | source)
XLA Modules:
  0.0 107.1 jit_solution(9034895545583317299)
XLA Ops:
  0.0 0.8 copy.12
  1.1 4.0 %reshape.50.cur_ref = f32[64,1024]{1,0:T(8,128)} reshape(f32[8,8,4,16,16]{4,3,2,1,0:T(8,128)} %param.8) | data formatting | bytes 524288 | tf_op jit(solution)/shard_map/reshape | solution.py:268
  5.1 1.0 fusion.7.pick_ref
  6.1 2.8 %shard_map.82 = (bf16[512,1024]{1,0:T(8,128)(2,1)}, f32[64,128]{1,0:T(8,128)}, f32[64,128]{1,0:T(8,128)}, f32[64,128]{1,0:T(8,128)}, f32[64,128]{1,0:T(8,128)}) custom-call(bf16[512,64]{1,0:T(8,128)(2,1)} %fusion.7.pick_ref, f32[64,1024]{1,0:T(8,128)} %reshape.50.cur_ref), custom_call_target="tpu_custom_call" | custom-call | tf_op jit(solution)/shard_map/pallas_call | solution.py:168
  8.9 11.5 %all-to-all-start = ((bf16[32,16,1024]{2,1,0:T(8,128)(2,1)}), bf16[32,16,1024]{2,1,0:T(8,128)(2,1)S(1)}, u32[]{:S(2)}, u32[]{:S(2)}) async-start(bf16[32,16,1024]{2,1,0:T(8,128)(2,1)} %bitcast.35), calls=%async_computation | async-start | bytes 2097152 | tf_op jit(solution)/shard_map/all_to_all | solution.py:281
  20.5 1.1 %fusion.16 = (f32[2,8,4,16,16]{4,3,2,1,0:T(8,128)}, f32[2,8,4,16,16]{4,3,2,1,0:T(8,128)}) fusion(f32[8,8,4,16,16]{4,3,2,1,0:T(8,128)S(1)} %copy-done), kind=kLoop, calls=%fused_computation.47 | loop fusion | bytes 262144 | tf_op jit(solution)/shard_map/slice | solution.py:275
  21.6 1.3 %slice.28 = f32[16,1024]{1,0:T(8,128)S(1)} reshape(f32[2,8,4,16,16]{4,3,2,1,0:T(8,128)} %get-tuple-element.36) | data formatting | bytes 131072 | tf_op jit(solution)/shard_map/slice | solution.py:274
  23.0 1.3 %slice.30 = f32[16,1024]{1,0:T(8,128)S(1)} reshape(f32[2,8,4,16,16]{4,3,2,1,0:T(8,128)} %get-tuple-element.35) | data formatting | bytes 131072 | tf_op jit(solution)/shard_map/slice | solution.py:275
  24.9 0.8 collective-permute-start.2
  25.7 2.4 %collective-permute-start.3 = (f32[64,128]{1,0:T(8,128)S(1)}, f32[64,128]{1,0:T(8,128)S(1)}, u32[]{:S(2)}, u32[]{:S(2)}) collective-permute-start(f32[64,128]{1,0:T(8,128)S(1)} %copy-done.22), channel_id=1, source_target_pairs={{0,32},{32,64},{64,96},{96,0},{1,33},{33,65},{65,97},{97,1},{2,34}... | collective-permute-start | bytes 98312 | tf_op jit(solution)/shard_map/ppermute | solution.py:276
  28.1 5.2 %collective-permute-start.4 = (f32[64,128]{1,0:T(8,128)S(1)}, f32[64,128]{1,0:T(8,128)S(1)}, u32[]{:S(2)}, u32[]{:S(2)}) collective-permute-start(f32[64,128]{1,0:T(8,128)S(1)} %copy-done.21), channel_id=1, source_target_pairs={{1,0},{2,1},{3,2},{4,3},{5,4},{6,5},{7,6},{8,7},{9,8},{10,9},{11,1... | collective-permute-start | bytes 98312 | tf_op jit(solution)/shard_map/ppermute | solution.py:279
  33.5 1.2 %fusion.17 = (f32[8,1,4,16,16]{4,3,2,1,0:T(8,128)S(1)}, f32[8,1,4,16,16]{4,3,2,1,0:T(8,128)S(1)}, f32[8,1,4,16,16]{4,3,2,1,0:T(8,128)S(1)}) fusion(f32[8,3,4,16,16]{4,3,2,1,0:T(8,128)} %param.9), kind=kLoop, calls=%fused_computation.48 | loop fusion | bytes 196608 | tf_op jit(solution)/shard_map/slice | solution.py:261
  35.3 0.7 broadcast_bitcast_fusion.3.fx_ref
  36.0 0.7 broadcast_bitcast_fusion.fz_ref
  36.7 0.8 broadcast_bitcast_fusion.1
  38.9 1.2 %fusion.3.sel_ref = bf16[256,512]{1,0:T(8,128)(2,1)} fusion(s32[512]{0:T(512)S(1)} %get-tuple-element.42, s32[512]{0:T(512)S(1)} %get-tuple-element.43, s32[256]{0:T(256)S(1)} %get-tuple-element.54, s32[256]{0:T(256)S(1)} %get-tuple-element.55, s32[512]{0:T(512)S(1)} %eq.50, s32[256]{0:T(256)S(1)} %get-tuple-element.51, s32[256]{0:T(256)S(1)} %get-tuple-element.56, ...), kind=kLoop, calls=%fused_computation.10 | loop fusion | flops 2883584 | bytes 278272 | tf_op jit(solution)/shard_map/convert_element_type | solution.py:248
  40.9 2.6 %shard_map.83 = (f32[64,1024]{1,0:T(8,128)}, f32[64,1024]{1,0:T(8,128)}) custom-call(f32[64,1024]{1,0:T(8,128)} %reshape.50.cur_ref, f32[16,1024]{1,0:T(8,128)} %copy-done.5, f32[16,1024]{1,0:T(8,128)} %copy-done.6, f32[64,128]{1,0:T(8,128)} %copy-done.13, f32[64,128]{1,0:T(8,128)} %copy-done.14, f32[64,1024]{1,0:T(8,128)} %broadcast_bitcast_fusion.3.fx_ref, ...), custom_call_target="tpu_custom_call" | custom-call | tf_op jit(solution)/shard_map/pallas_call | solution.py:205
  43.5 4.2 %collective-permute-done.5.hzm_ref = f32[64,128]{1,0:T(8,128)S(1)} collective-permute-done((f32[64,128]{1,0:T(8,128)S(1)}, f32[64,128]{1,0:T(8,128)S(1)}, u32[]{:S(2)}, u32[]{:S(2)}) %collective-permute-start.5) | collective-permute-done | bytes 32800 | tf_op jit(solution)/shard_map/ppermute | solution.py:278
  47.7 0.8 all-to-all-done
  48.5 1.0 copy-done.1
  49.5 10.6 %shard_map.84 = (f32[64,1024]{1,0:T(8,128)}, bf16[512,1024]{1,0:T(8,128)(2,1)}) custom-call(bf16[512,64]{1,0:T(8,128)(2,1)} %fusion.7.pick_ref, bf16[256,512]{1,0:T(8,128)(2,1)} %fusion.3.sel_ref, bf16[512,1024]{1,0:T(8,128)(2,1)} %bitcast.33, f32[64,1024]{1,0:T(8,128)} %reshape.50.cur_ref, f32[64,1024]{1,0:T(8,128)} %get-tuple-element.23.a_ref, ...), custom_call_target="tpu_custom_call" | custom-call | tf_op jit(solution)/shard_map/pallas_call | solution.py:185
  60.1 6.0 %all-to-all-start.1 = ((bf16[32,16,1024]{2,1,0:T(8,128)(2,1)}), bf16[32,16,1024]{2,1,0:T(8,128)(2,1)S(1)}, u32[]{:S(2)}, u32[]{:S(2)}) async-start(bf16[32,16,1024]{2,1,0:T(8,128)(2,1)} %bitcast.36), calls=%async_computation.1 | async-start | bytes 2097152 | tf_op jit(solution)/shard_map/all_to_all | solution.py:281
  66.2 2.6 %shard_map.85 = (f32[64,128]{1,0:T(8,128)}, f32[64,128]{1,0:T(8,128)}, f32[64,128]{1,0:T(8,128)}, f32[64,128]{1,0:T(8,128)}) custom-call(f32[64,1024]{1,0:T(8,128)} %get-tuple-element.28.cur_ref), custom_call_target="tpu_custom_call" | custom-call | tf_op jit(solution)/shard_map/pallas_call | solution.py:173
  69.3 0.8 collective-permute-start.8
  70.2 2.4 %collective-permute-start.9 = (f32[64,128]{1,0:T(8,128)}, f32[64,128]{1,0:T(8,128)S(1)}, u32[]{:S(2)}, u32[]{:S(2)}) collective-permute-start(f32[64,128]{1,0:T(8,128)} %get-tuple-element.30), channel_id=1, source_target_pairs={{0,32},{32,64},{64,96},{96,0},{1,33},{33,65},{65,97},{97,1},{2,34}... | collective-permute-start | bytes 98312 | tf_op jit(solution)/shard_map/ppermute | solution.py:276
  72.6 5.2 %collective-permute-start.10 = (f32[64,128]{1,0:T(8,128)}, f32[64,128]{1,0:T(8,128)S(1)}, u32[]{:S(2)}, u32[]{:S(2)}) collective-permute-start(f32[64,128]{1,0:T(8,128)} %get-tuple-element.33), channel_id=1, source_target_pairs={{1,0},{2,1},{3,2},{4,3},{5,4},{6,5},{7,6},{8,7},{9,8},{10,9},{11,1... | collective-permute-start | bytes 98312 | tf_op jit(solution)/shard_map/ppermute | solution.py:279
  78.5 0.6 copy-done.8
  79.1 2.6 %shard_map.86 = (f32[64,1024]{1,0:T(8,128)}, f32[64,1024]{1,0:T(8,128)}) custom-call(f32[64,1024]{1,0:T(8,128)} %get-tuple-element.28.cur_ref, f32[16,1024]{1,0:T(8,128)} %copy-done.8, f32[16,1024]{1,0:T(8,128)} %copy-done.7, f32[64,128]{1,0:T(8,128)} %copy-done.15, f32[64,128]{1,0:T(8,128)} %copy-done.16, f32[64,1024]{1,0:T(8,128)} %broadcast_bitcast_fusion.3.fx_ref, ...), custom_call_target="tpu_custom_call" | custom-call | tf_op jit(solution)/shard_map/pallas_call | solution.py:205
  81.7 5.0 %collective-permute-done.10.hzp_ref = f32[64,128]{1,0:T(8,128)S(1)} collective-permute-done((f32[64,128]{1,0:T(8,128)}, f32[64,128]{1,0:T(8,128)S(1)}, u32[]{:S(2)}, u32[]{:S(2)}) %collective-permute-start.10) | collective-permute-done | bytes 32800 | tf_op jit(solution)/shard_map/ppermute | solution.py:279
  86.7 6.3 %collective-permute-done.11.hzm_ref = f32[64,128]{1,0:T(8,128)S(1)} collective-permute-done((f32[64,128]{1,0:T(8,128)}, f32[64,128]{1,0:T(8,128)S(1)}, u32[]{:S(2)}, u32[]{:S(2)}) %collective-permute-start.11) | collective-permute-done | bytes 32800 | tf_op jit(solution)/shard_map/ppermute | solution.py:278
  94.2 9.9 %shard_map.87 = f32[64,1024]{1,0:T(8,128)} custom-call(bf16[512,64]{1,0:T(8,128)(2,1)} %fusion.7.pick_ref, bf16[256,512]{1,0:T(8,128)(2,1)} %fusion.3.sel_ref, bf16[512,1024]{1,0:T(8,128)(2,1)} %bitcast.34, f32[64,1024]{1,0:T(8,128)} %get-tuple-element.28.cur_ref, f32[64,1024]{1,0:T(8,128)} %get-tuple-element.31.a_ref, f32[64,1024]{1,0:T(8,128)} %get-tuple-element.32.q_ref, ...), custom_call_target="tpu_custom_call" | custom-call | tf_op jit(solution)/shard_map/pallas_call | solution.py:185
  104.1 3.0 %reshape.59 = f32[8,8,4,16,16]{4,3,2,1,0:T(8,128)} reshape(f32[64,1024]{1,0:T(8,128)} %shard_map.87) | data formatting | bytes 524288 | tf_op jit(solution)/shard_map/reshape | solution.py:289
  (92 shorter events, 6.1 us)
Async XLA Ops:
  1.1 19.3 %copy-start = (f32[8,8,4,16,16]{4,3,2,1,0:T(8,128)S(1)}, f32[8,8,4,16,16]{4,3,2,1,0:T(8,128)}, u32[]{:S(2)}) copy-start(f32[8,8,4,16,16]{4,3,2,1,0:T(8,128)} %param.8) | copy-start | bytes 786436
  8.9 39.6 %all-to-all-start = ((bf16[32,16,1024]{2,1,0:T(8,128)(2,1)}), bf16[32,16,1024]{2,1,0:T(8,128)(2,1)S(1)}, u32[]{:S(2)}, u32[]{:S(2)}) async-start(bf16[32,16,1024]{2,1,0:T(8,128)(2,1)} %bitcast.35), calls=%async_computation | async-start | bytes 2097152 | tf_op jit(solution)/shard_map/all_to_all | solution.py:281
  20.4 4.5 %copy-start.23 = (f32[64,128]{1,0:T(8,128)S(1)}, f32[64,128]{1,0:T(8,128)}, u32[]{:S(2)}) copy-start(f32[64,128]{1,0:T(8,128)} %get-tuple-element.21) | copy-start | bytes 98308
  20.4 5.3 %copy-start.22 = (f32[64,128]{1,0:T(8,128)S(1)}, f32[64,128]{1,0:T(8,128)}, u32[]{:S(2)}) copy-start(f32[64,128]{1,0:T(8,128)} %get-tuple-element.22) | copy-start | bytes 98308
  20.5 7.7 %copy-start.21 = (f32[64,128]{1,0:T(8,128)S(1)}, f32[64,128]{1,0:T(8,128)}, u32[]{:S(2)}) copy-start(f32[64,128]{1,0:T(8,128)} %get-tuple-element.25) | copy-start | bytes 98308
  20.5 12.9 %copy-start.4 = (f32[8,4,16,16]{3,2,1,0:T(8,128)S(1)}, f32[8,4,16,16]{3,2,1,0:T(8,128)}, u32[]{:S(2)}) copy-start(f32[8,4,16,16]{3,2,1,0:T(8,128)} %param.10) | copy-start | bytes 98308
  21.6 13.6 %copy-start.19 = (s32[1,1,1,32]{3,2,1,0:T(1,128)S(1)}, s32[1,1,1,32]{3,2,1,0:T(1,128)}, u32[]{:S(2)}) copy-start(s32[1,1,1,32]{3,2,1,0:T(1,128)} %param.15) | copy-start | bytes 388
  22.9 17.3 %collective-permute-start = (f32[16,1024]{1,0:T(8,128)S(1)}, f32[16,1024]{1,0:T(8,128)S(1)}, u32[]{:S(2)}, u32[]{:S(2)}) collective-permute-start(f32[16,1024]{1,0:T(8,128)S(1)} %slice.28), channel_id=1, source_target_pairs={{0,128},{128,0},{1,129},{129,1},{2,130},{130,2},{3,131},{131,3},{4... | collective-permute-start | bytes 196616 | tf_op jit(solution)/shard_map/ppermute | solution.py:274
  24.3 13.6 %copy-start.17 = (s32[1,1,1,32,2]{3,4,2,1,0:T(2,128)S(1)}, s32[1,1,1,32,2]{3,4,2,1,0:T(2,128)}, u32[]{:S(2)}) copy-start(s32[1,1,1,32,2]{3,4,2,1,0:T(2,128)} %param.13) | copy-start | bytes 772
  24.3 13.8 %copy-start.18 = (s32[1,1,1,32,2]{3,4,2,1,0:T(2,128)S(1)}, s32[1,1,1,32,2]{3,4,2,1,0:T(2,128)}, u32[]{:S(2)}) copy-start(s32[1,1,1,32,2]{3,4,2,1,0:T(2,128)} %param.14) | copy-start | bytes 772
  24.3 14.3 %copy-start.20 = (f32[64,128]{1,0:T(8,128)S(1)}, f32[64,128]{1,0:T(8,128)}, u32[]{:S(2)}) copy-start(f32[64,128]{1,0:T(8,128)} %get-tuple-element.26) | copy-start | bytes 98308
  24.3 15.9 %collective-permute-start.1 = (f32[16,1024]{1,0:T(8,128)S(1)}, f32[16,1024]{1,0:T(8,128)S(1)}, u32[]{:S(2)}, u32[]{:S(2)}) collective-permute-start(f32[16,1024]{1,0:T(8,128)S(1)} %slice.30), channel_id=1, source_target_pairs={{128,0},{0,128},{129,1},{1,129},{130,2},{2,130},{131,3},{3,131},{1... | collective-permute-start | bytes 196616 | tf_op jit(solution)/shard_map/ppermute | solution.py:275
  24.9 13.7 %collective-permute-start.2 = (f32[64,128]{1,0:T(8,128)S(1)}, f32[64,128]{1,0:T(8,128)S(1)}, u32[]{:S(2)}, u32[]{:S(2)}) collective-permute-start(f32[64,128]{1,0:T(8,128)S(1)} %copy-done.23), channel_id=1, source_target_pairs={{32,0},{64,32},{96,64},{0,96},{33,1},{65,33},{97,65},{1,97},{34,2}... | collective-permute-start | bytes 98312 | tf_op jit(solution)/shard_map/ppermute | solution.py:277
  25.7 14.4 %collective-permute-start.3 = (f32[64,128]{1,0:T(8,128)S(1)}, f32[64,128]{1,0:T(8,128)S(1)}, u32[]{:S(2)}, u32[]{:S(2)}) collective-permute-start(f32[64,128]{1,0:T(8,128)S(1)} %copy-done.22), channel_id=1, source_target_pairs={{0,32},{32,64},{64,96},{96,0},{1,33},{33,65},{65,97},{97,1},{2,34}... | collective-permute-start | bytes 98312 | tf_op jit(solution)/shard_map/ppermute | solution.py:276
  28.1 15.3 %collective-permute-start.4 = (f32[64,128]{1,0:T(8,128)S(1)}, f32[64,128]{1,0:T(8,128)S(1)}, u32[]{:S(2)}, u32[]{:S(2)}) collective-permute-start(f32[64,128]{1,0:T(8,128)S(1)} %copy-done.21), channel_id=1, source_target_pairs={{1,0},{2,1},{3,2},{4,3},{5,4},{6,5},{7,6},{8,7},{9,8},{10,9},{11,1... | collective-permute-start | bytes 98312 | tf_op jit(solution)/shard_map/ppermute | solution.py:279
  38.6 1.6 %copy-start.13 = (f32[64,128]{1,0:T(8,128)}, f32[64,128]{1,0:T(8,128)S(1)}, u32[]{:S(2)}) copy-start(f32[64,128]{1,0:T(8,128)S(1)} %collective-permute-done.2.hyp_ref) | copy-start | bytes 98308
  38.7 9.1 %collective-permute-start.5 = (f32[64,128]{1,0:T(8,128)S(1)}, f32[64,128]{1,0:T(8,128)S(1)}, u32[]{:S(2)}, u32[]{:S(2)}) collective-permute-start(f32[64,128]{1,0:T(8,128)S(1)} %copy-done.20), channel_id=1, source_target_pairs={{0,1},{1,2},{2,3},{3,4},{4,5},{5,6},{6,7},{7,8},{8,9},{9,10},{10,1... | collective-permute-start | bytes 98312 | tf_op jit(solution)/shard_map/ppermute | solution.py:278
  40.2 0.6 copy-start.5
  40.2 0.6 copy-start.6
  43.5 5.0 %copy-start.9 = (f32[64,128]{1,0:T(8,128)}, f32[64,128]{1,0:T(8,128)S(1)}, u32[]{:S(2)}) copy-start(f32[64,128]{1,0:T(8,128)S(1)} %collective-permute-done.4.hzp_ref) | copy-start | bytes 98308
  47.7 0.8 copy-start.10
  48.5 1.0 copy-start.1
  60.1 8.6 %copy-start.3 = (f32[64,1024]{1,0:T(8,128)S(1)}, f32[64,1024]{1,0:T(8,128)}, u32[]{:S(2)}) copy-start(f32[64,1024]{1,0:T(8,128)} %get-tuple-element.28.cur_ref) | copy-start | bytes 786436
  60.1 33.2 %all-to-all-start.1 = ((bf16[32,16,1024]{2,1,0:T(8,128)(2,1)}), bf16[32,16,1024]{2,1,0:T(8,128)(2,1)S(1)}, u32[]{:S(2)}, u32[]{:S(2)}) async-start(bf16[32,16,1024]{2,1,0:T(8,128)(2,1)} %bitcast.36), calls=%async_computation.1 | async-start | bytes 2097152 | tf_op jit(solution)/shard_map/all_to_all | solution.py:281
  68.7 9.1 %collective-permute-start.7 = (f32[16,1024]{1,0:T(8,128)S(1)}, f32[16,1024]{1,0:T(8,128)S(1)}, u32[]{:S(2)}, u32[]{:S(2)}) collective-permute-start(f32[16,1024]{1,0:T(8,128)S(1)} %get-tuple-element.40), channel_id=1, source_target_pairs={{128,0},{0,128},{129,1},{1,129},{130,2},{2,130},{131,3},{3,131},{1... | collective-permute-start | bytes 196616 | tf_op jit(solution)/shard_map/ppermute | solution.py:275
  68.8 9.0 %collective-permute-start.6 = (f32[16,1024]{1,0:T(8,128)S(1)}, f32[16,1024]{1,0:T(8,128)S(1)}, u32[]{:S(2)}, u32[]{:S(2)}) collective-permute-start(f32[16,1024]{1,0:T(8,128)S(1)} %get-tuple-element.41), channel_id=1, source_target_pairs={{0,128},{128,0},{1,129},{129,1},{2,130},{130,2},{3,131},{131,3},{4... | collective-permute-start | bytes 196616 | tf_op jit(solution)/shard_map/ppermute | solution.py:274
  69.3 8.4 %collective-permute-start.8 = (f32[64,128]{1,0:T(8,128)}, f32[64,128]{1,0:T(8,128)S(1)}, u32[]{:S(2)}, u32[]{:S(2)}) collective-permute-start(f32[64,128]{1,0:T(8,128)} %get-tuple-element.29), channel_id=1, source_target_pairs={{32,0},{64,32},{96,64},{0,96},{33,1},{65,33},{97,65},{1,97},{34,2}... | collective-permute-start | bytes 98312 | tf_op jit(solution)/shard_map/ppermute | solution.py:277
  70.2 7.6 %collective-permute-start.9 = (f32[64,128]{1,0:T(8,128)}, f32[64,128]{1,0:T(8,128)S(1)}, u32[]{:S(2)}, u32[]{:S(2)}) collective-permute-start(f32[64,128]{1,0:T(8,128)} %get-tuple-element.30), channel_id=1, source_target_pairs={{0,32},{32,64},{64,96},{96,0},{1,33},{33,65},{65,97},{97,1},{2,34}... | collective-permute-start | bytes 98312 | tf_op jit(solution)/shard_map/ppermute | solution.py:276
  72.6 14.1 %collective-permute-start.10 = (f32[64,128]{1,0:T(8,128)}, f32[64,128]{1,0:T(8,128)S(1)}, u32[]{:S(2)}, u32[]{:S(2)}) collective-permute-start(f32[64,128]{1,0:T(8,128)} %get-tuple-element.33), channel_id=1, source_target_pairs={{1,0},{2,1},{3,2},{4,3},{5,4},{6,5},{7,6},{8,7},{9,8},{10,9},{11,1... | collective-permute-start | bytes 98312 | tf_op jit(solution)/shard_map/ppermute | solution.py:279
  77.8 15.2 %collective-permute-start.11 = (f32[64,128]{1,0:T(8,128)}, f32[64,128]{1,0:T(8,128)S(1)}, u32[]{:S(2)}, u32[]{:S(2)}) collective-permute-start(f32[64,128]{1,0:T(8,128)} %get-tuple-element.34), channel_id=1, source_target_pairs={{0,1},{1,2},{2,3},{3,4},{4,5},{5,6},{6,7},{7,8},{8,9},{9,10},{10,1... | collective-permute-start | bytes 98312 | tf_op jit(solution)/shard_map/ppermute | solution.py:278
  86.7 6.6 %copy-start.11 = (f32[64,128]{1,0:T(8,128)}, f32[64,128]{1,0:T(8,128)S(1)}, u32[]{:S(2)}) copy-start(f32[64,128]{1,0:T(8,128)S(1)} %collective-permute-done.10.hzp_ref) | copy-start | bytes 98308
  93.3 1.0 copy-start.2
  (6 other events, 3.7 us)

commit v8 on v4

--- a/solution.py
+++ b/solution.py
@@ -67,10 +67,8 @@
     ).astype(BF16)
 
 
-def _prep_kernel(pick_ref, cur_ref, snd_ref, zlo_ref, zhi_ref, ylo_ref, yhi_ref):
-    cur = cur_ref[...]
-    _emit_send(pick_ref, cur, snd_ref)
-    _emit_halos(cur, zlo_ref, zhi_ref, ylo_ref, yhi_ref)
+def _send_kernel(pick_ref, cur_ref, snd_ref):
+    _emit_send(pick_ref, cur_ref[...], snd_ref)
 
 
 def _halo_kernel(cur_ref, zlo_ref, zhi_ref, ylo_ref, yhi_ref):
@@ -159,10 +157,9 @@
     return jax.ShapeDtypeStruct((peers * both, lanes), BF16)
 
 
-def _prep(pick, cur, peers, both):
-    halo = jax.ShapeDtypeStruct((cur.shape[0], 128), F32)
-    shapes = [_send_shape(cur.shape[1], peers, both)] + [halo] * 4
-    return pl.pallas_call(_prep_kernel, out_shape=shapes)(pick, cur)
+def _send(pick, cur, peers, both):
+    shape = _send_shape(cur.shape[1], peers, both)
+    return pl.pallas_call(_send_kernel, out_shape=shape)(pick, cur)
 
 
 def _halos(cur):
@@ -261,11 +258,11 @@
     up_z, down_z = _ring("kz")
 
     cur = populations.reshape(rows, lanes)
-    snd, zlo, zhi, ylo, yhi = _prep(pick, cur, peer_count, both)
+    snd = _send(pick, cur, peer_count, both)
+    _, cur_late = lax.optimization_barrier((snd, cur))
     for iteration in range(ITERS):
         last = iteration + 1 == ITERS
-        if iteration > 0:
-            zlo, zhi, ylo, yhi = _halos(cur)
+        zlo, zhi, ylo, yhi = _halos(cur_late if iteration == 0 else cur)
         xlo = lax.ppermute(cur[rows - 16:], "kx", up_x)
         xhi = lax.ppermute(cur[:16], "kx", down_x)
         hym = lax.ppermute(yhi, "ky", up_y)

time: 104 us -> 104 us (level)
  Pallas kernels: 27.5 us -> 29.6 us
  local copies, waits for them, and re-layouts: 20.7 us -> 19.4 us
  waiting for transfers between devices: 16.6 us -> 15.3 us
    pallas_call x1 -> x2, Pallas kernels: 2.57 us -> 5.14 us  [_halos(): return pl.pallas_call(_halo_kernel, out_shape=[halo] * 4)(cur)]
    ppermute x2, waiting for transfers between devices: 10.5 us -> 9.28 us  [per_device(): hzm = lax.ppermute(zhi, 'kz', up_z)]
    slice x3, local copies, waits for them, and re-layouts: 2.4 us -> 1.35 us  [per_device(): xhi = lax.ppermute(cur[:16], 'kx', down_x)]
    unnamed x51 -> x45, local copies, waits for them, and re-layouts: 4.82 us -> 4.76 us
  transfers between devices with their start and end apart: 14 -> 14, of which waited for: 5 -> 5; matrix products, arithmetic and copies ran while one was open for 10% -> 9% of each run, Pallas kernels for 8% -> 10%
where the time goes in v8:
time: 104 us; the launch traced here: 103 us
  starting transfers between devices  36 us (35%)
  Pallas kernels  29.6 us (28%)
  local copies, waits for them, and re-layouts  19.4 us (19%)
  waiting for transfers between devices  15.3 us (15%)
  other arithmetic  2.29 us (2%)
    all_to_all x2, starting transfers between devices, per_device(): lax.all_to_all(outgoing, 'kz', split_axis=0, concat_axis=0, tiled=True)  17.7 us
    pallas_call x2, Pallas kernels, _finish(): pl.pallas_call(functools.partial(_finish_kernel, last), out_shape=shapes,...  16.8 us
    ppermute x2, starting transfers between devices, per_device(): hzp = lax.ppermute(zlo, 'kz', down_z)  10.4 us
    ppermute x2, waiting for transfers between devices, per_device(): hzm = lax.ppermute(zhi, 'kz', up_z)  9.28 us
    pallas_call x2, Pallas kernels, _drift(): pl.pallas_call(_drift_kernel, out_shape=[plane, plane], scratch_shapes=[p...  5.25 us
    pallas_call x2, Pallas kernels, _halos(): return pl.pallas_call(_halo_kernel, out_shape=[halo] * 4)(cur)  5.14 us
    ppermute x2, waiting for transfers between devices, per_device(): hzp = lax.ppermute(zlo, 'kz', down_z)  5.01 us
    ppermute x2, starting transfers between devices, per_device(): hym = lax.ppermute(yhi, 'ky', up_y)  4.82 us
  transfers between devices with their start and end apart: 14, of which 5 were waited for; matrix products, arithmetic and copies ran while one was open for 9% of the time, Pallas kernels for 10%

profile of v8, /device:TPU:6, one launch (start us, length us, event | category | flops | bytes accessed | tf_op | source)
XLA Modules:
  0.0 102.9 jit_solution(3146442444076013410)
XLA Ops:
  0.0 0.8 copy.12
  1.1 3.8 %reshape.50.cur_ref = f32[64,1024]{1,0:T(8,128)} reshape(f32[8,8,4,16,16]{4,3,2,1,0:T(8,128)} %param.8) | data formatting | bytes 524288 | tf_op jit(solution)/shard_map/reshape | solution.py:260
  4.9 1.0 fusion.7.pick_ref
  5.9 2.4 %shard_map.82 = bf16[512,1024]{1,0:T(8,128)(2,1)} custom-call(bf16[512,64]{1,0:T(8,128)(2,1)} %fusion.7.pick_ref, f32[64,1024]{1,0:T(8,128)} %reshape.50.cur_ref), custom_call_target="tpu_custom_call" | custom-call | tf_op jit(solution)/shard_map/pallas_call | solution.py:162
  8.3 11.6 %all-to-all-start = ((bf16[32,16,1024]{2,1,0:T(8,128)(2,1)}), bf16[32,16,1024]{2,1,0:T(8,128)(2,1)S(1)}, u32[]{:S(2)}, u32[]{:S(2)}) async-start(bf16[32,16,1024]{2,1,0:T(8,128)(2,1)} %bitcast.33), calls=%async_computation | async-start | bytes 2097152 | tf_op jit(solution)/shard_map/all_to_all | solution.py:273
  19.9 2.6 %shard_map.83 = (f32[64,128]{1,0:T(8,128)}, f32[64,128]{1,0:T(8,128)}, f32[64,128]{1,0:T(8,128)}, f32[64,128]{1,0:T(8,128)}) custom-call(f32[64,1024]{1,0:T(8,128)} %reshape.50.cur_ref), custom_call_target="tpu_custom_call" | custom-call | tf_op jit(solution)/shard_map/pallas_call | solution.py:167
  22.5 0.8 collective-permute-start.2
  23.3 2.4 %collective-permute-start.3 = (f32[64,128]{1,0:T(8,128)}, f32[64,128]{1,0:T(8,128)S(1)}, u32[]{:S(2)}, u32[]{:S(2)}) collective-permute-start(f32[64,128]{1,0:T(8,128)} %get-tuple-element.22), channel_id=1, source_target_pairs={{0,32},{32,64},{64,96},{96,0},{1,33},{33,65},{65,97},{97,1},{2,34}... | collective-permute-start | bytes 98312 | tf_op jit(solution)/shard_map/ppermute | solution.py:268
  25.7 5.2 %collective-permute-start.4 = (f32[64,128]{1,0:T(8,128)}, f32[64,128]{1,0:T(8,128)S(1)}, u32[]{:S(2)}, u32[]{:S(2)}) collective-permute-start(f32[64,128]{1,0:T(8,128)} %get-tuple-element.25), channel_id=1, source_target_pairs={{1,0},{2,1},{3,2},{4,3},{5,4},{6,5},{7,6},{8,7},{9,8},{10,9},{11,1... | collective-permute-start | bytes 98312 | tf_op jit(solution)/shard_map/ppermute | solution.py:271
  31.0 1.1 %fusion.16 = (f32[2,8,4,16,16]{4,3,2,1,0:T(8,128)}, f32[2,8,4,16,16]{4,3,2,1,0:T(8,128)}) fusion(f32[8,8,4,16,16]{4,3,2,1,0:T(8,128)S(1)} %copy-done), kind=kLoop, calls=%fused_computation.47 | loop fusion | bytes 262144 | tf_op jit(solution)/shard_map/slice | solution.py:267
  32.0 1.3 %slice.28 = f32[16,1024]{1,0:T(8,128)S(1)} reshape(f32[2,8,4,16,16]{4,3,2,1,0:T(8,128)} %get-tuple-element.36) | data formatting | bytes 131072 | tf_op jit(solution)/shard_map/slice | solution.py:266
  33.6 1.2 %fusion.17 = (f32[8,1,4,16,16]{4,3,2,1,0:T(8,128)S(1)}, f32[8,1,4,16,16]{4,3,2,1,0:T(8,128)S(1)}, f32[8,1,4,16,16]{4,3,2,1,0:T(8,128)S(1)}) fusion(f32[8,3,4,16,16]{4,3,2,1,0:T(8,128)} %param.9), kind=kLoop, calls=%fused_computation.48 | loop fusion | bytes 196608 | tf_op jit(solution)/shard_map/slice | solution.py:253
  35.4 0.7 broadcast_bitcast_fusion.3.fx_ref
  36.1 0.7 broadcast_bitcast_fusion.fz_ref
  36.8 0.9 broadcast_bitcast_fusion.1
  39.1 0.8 collective-permute-start.1
  39.8 1.2 %fusion.3.sel_ref = bf16[256,512]{1,0:T(8,128)(2,1)} fusion(s32[512]{0:T(512)S(1)} %get-tuple-element.42, s32[512]{0:T(512)S(1)} %get-tuple-element.43, s32[256]{0:T(256)S(1)} %get-tuple-element.54, s32[256]{0:T(256)S(1)} %get-tuple-element.55, s32[512]{0:T(512)S(1)} %eq.50, s32[256]{0:T(256)S(1)} %get-tuple-element.51, s32[256]{0:T(256)S(1)} %get-tuple-element.56, ...), kind=kLoop, calls=%fused_computation.10 | loop fusion | flops 2883584 | bytes 278272 | tf_op jit(solution)/shard_map/convert_element_type | solution.py:240
  41.7 2.6 %shard_map.84 = (f32[64,1024]{1,0:T(8,128)}, f32[64,1024]{1,0:T(8,128)}) custom-call(f32[64,1024]{1,0:T(8,128)} %reshape.50.cur_ref, f32[16,1024]{1,0:T(8,128)} %copy-done.6, f32[16,1024]{1,0:T(8,128)} %copy-done.9, f32[64,128]{1,0:T(8,128)} %copy-done.14, f32[64,128]{1,0:T(8,128)} %copy-done.15, f32[64,1024]{1,0:T(8,128)} %broadcast_bitcast_fusion.3.fx_ref, ...), custom_call_target="tpu_custom_call" | custom-call | tf_op jit(solution)/shard_map/pallas_call | solution.py:197
  44.3 2.9 %collective-permute-done.5.hzm_ref = f32[64,128]{1,0:T(8,128)S(1)} collective-permute-done((f32[64,128]{1,0:T(8,128)}, f32[64,128]{1,0:T(8,128)S(1)}, u32[]{:S(2)}, u32[]{:S(2)}) %collective-permute-start.5) | collective-permute-done | bytes 32800 | tf_op jit(solution)/shard_map/ppermute | solution.py:270
  47.2 0.8 all-to-all-done
  48.0 1.0 copy-done.1
  49.0 8.8 %shard_map.85 = (f32[64,1024]{1,0:T(8,128)}, bf16[512,1024]{1,0:T(8,128)(2,1)}) custom-call(bf16[512,64]{1,0:T(8,128)(2,1)} %fusion.7.pick_ref, bf16[256,512]{1,0:T(8,128)(2,1)} %fusion.3.sel_ref, bf16[512,1024]{1,0:T(8,128)(2,1)} %bitcast.34, f32[64,1024]{1,0:T(8,128)} %reshape.50.cur_ref, f32[64,1024]{1,0:T(8,128)} %get-tuple-element.23.a_ref, ...), custom_call_target="tpu_custom_call" | custom-call | tf_op jit(solution)/shard_map/pallas_call | solution.py:177
  57.8 6.0 %all-to-all-start.1 = ((bf16[32,16,1024]{2,1,0:T(8,128)(2,1)}), bf16[32,16,1024]{2,1,0:T(8,128)(2,1)S(1)}, u32[]{:S(2)}, u32[]{:S(2)}) async-start(bf16[32,16,1024]{2,1,0:T(8,128)(2,1)} %bitcast.36), calls=%async_computation.1 | async-start | bytes 2097152 | tf_op jit(solution)/shard_map/all_to_all | solution.py:273
  63.8 2.6 %shard_map.86 = (f32[64,128]{1,0:T(8,128)}, f32[64,128]{1,0:T(8,128)}, f32[64,128]{1,0:T(8,128)}, f32[64,128]{1,0:T(8,128)}) custom-call(f32[64,1024]{1,0:T(8,128)} %get-tuple-element.28.cur_ref), custom_call_target="tpu_custom_call" | custom-call | tf_op jit(solution)/shard_map/pallas_call | solution.py:167
  67.0 0.8 collective-permute-start.8
  67.8 2.4 %collective-permute-start.9 = (f32[64,128]{1,0:T(8,128)}, f32[64,128]{1,0:T(8,128)S(1)}, u32[]{:S(2)}, u32[]{:S(2)}) collective-permute-start(f32[64,128]{1,0:T(8,128)} %get-tuple-element.30), channel_id=1, source_target_pairs={{0,32},{32,64},{64,96},{96,0},{1,33},{33,65},{65,97},{97,1},{2,34}... | collective-permute-start | bytes 98312 | tf_op jit(solution)/shard_map/ppermute | solution.py:268
  70.2 5.2 %collective-permute-start.10 = (f32[64,128]{1,0:T(8,128)}, f32[64,128]{1,0:T(8,128)S(1)}, u32[]{:S(2)}, u32[]{:S(2)}) collective-permute-start(f32[64,128]{1,0:T(8,128)} %get-tuple-element.33), channel_id=1, source_target_pairs={{1,0},{2,1},{3,2},{4,3},{5,4},{6,5},{7,6},{8,7},{9,8},{10,9},{11,1... | collective-permute-start | bytes 98312 | tf_op jit(solution)/shard_map/ppermute | solution.py:271
  76.7 2.6 %shard_map.87 = (f32[64,1024]{1,0:T(8,128)}, f32[64,1024]{1,0:T(8,128)}) custom-call(f32[64,1024]{1,0:T(8,128)} %get-tuple-element.28.cur_ref, f32[16,1024]{1,0:T(8,128)} %copy-done.8, f32[16,1024]{1,0:T(8,128)} %copy-done.7, f32[64,128]{1,0:T(8,128)} %copy-done.16, f32[64,128]{1,0:T(8,128)} %copy-done.17, f32[64,1024]{1,0:T(8,128)} %broadcast_bitcast_fusion.3.fx_ref, ...), custom_call_target="tpu_custom_call" | custom-call | tf_op jit(solution)/shard_map/pallas_call | solution.py:197
  79.3 5.0 %collective-permute-done.10.hzp_ref = f32[64,128]{1,0:T(8,128)S(1)} collective-permute-done((f32[64,128]{1,0:T(8,128)}, f32[64,128]{1,0:T(8,128)S(1)}, u32[]{:S(2)}, u32[]{:S(2)}) %collective-permute-start.10) | collective-permute-done | bytes 32800 | tf_op jit(solution)/shard_map/ppermute | solution.py:271
  84.4 6.3 %collective-permute-done.11.hzm_ref = f32[64,128]{1,0:T(8,128)S(1)} collective-permute-done((f32[64,128]{1,0:T(8,128)}, f32[64,128]{1,0:T(8,128)S(1)}, u32[]{:S(2)}, u32[]{:S(2)}) %collective-permute-start.11) | collective-permute-done | bytes 32800 | tf_op jit(solution)/shard_map/ppermute | solution.py:270
  91.9 8.0 %shard_map.88 = f32[64,1024]{1,0:T(8,128)} custom-call(bf16[512,64]{1,0:T(8,128)(2,1)} %fusion.7.pick_ref, bf16[256,512]{1,0:T(8,128)(2,1)} %fusion.3.sel_ref, bf16[512,1024]{1,0:T(8,128)(2,1)} %bitcast.35, f32[64,1024]{1,0:T(8,128)} %get-tuple-element.28.cur_ref, f32[64,1024]{1,0:T(8,128)} %get-tuple-element.31.a_ref, f32[64,1024]{1,0:T(8,128)} %get-tuple-element.32.q_ref, ...), custom_call_target="tpu_custom_call" | custom-call | tf_op jit(solution)/shard_map/pallas_call | solution.py:177
  99.9 3.0 %reshape.59 = f32[8,8,4,16,16]{4,3,2,1,0:T(8,128)} reshape(f32[64,1024]{1,0:T(8,128)} %shard_map.88) | data formatting | bytes 524288 | tf_op jit(solution)/shard_map/reshape | solution.py:281
  (87 shorter events, 6.1 us)
Async XLA Ops:
  4.9 26.0 %copy-start = (f32[8,8,4,16,16]{4,3,2,1,0:T(8,128)S(1)}, f32[8,8,4,16,16]{4,3,2,1,0:T(8,128)}, u32[]{:S(2)}) copy-start(f32[8,8,4,16,16]{4,3,2,1,0:T(8,128)} %param.8) | copy-start | bytes 786436
  8.3 25.2 %copy-start.5 = (f32[8,4,16,16]{3,2,1,0:T(8,128)S(1)}, f32[8,4,16,16]{3,2,1,0:T(8,128)}, u32[]{:S(2)}) copy-start(f32[8,4,16,16]{3,2,1,0:T(8,128)} %param.10) | copy-start | bytes 98308
  8.3 39.7 %all-to-all-start = ((bf16[32,16,1024]{2,1,0:T(8,128)(2,1)}), bf16[32,16,1024]{2,1,0:T(8,128)(2,1)S(1)}, u32[]{:S(2)}, u32[]{:S(2)}) async-start(bf16[32,16,1024]{2,1,0:T(8,128)(2,1)} %bitcast.33), calls=%async_computation | async-start | bytes 2097152 | tf_op jit(solution)/shard_map/all_to_all | solution.py:273
  22.5 16.5 %collective-permute-start.2 = (f32[64,128]{1,0:T(8,128)}, f32[64,128]{1,0:T(8,128)S(1)}, u32[]{:S(2)}, u32[]{:S(2)}) collective-permute-start(f32[64,128]{1,0:T(8,128)} %get-tuple-element.21), channel_id=1, source_target_pairs={{32,0},{64,32},{96,64},{0,96},{33,1},{65,33},{97,65},{1,97},{34,2}... | collective-permute-start | bytes 98312 | tf_op jit(solution)/shard_map/ppermute | solution.py:269
  23.3 17.7 %collective-permute-start.3 = (f32[64,128]{1,0:T(8,128)}, f32[64,128]{1,0:T(8,128)S(1)}, u32[]{:S(2)}, u32[]{:S(2)}) collective-permute-start(f32[64,128]{1,0:T(8,128)} %get-tuple-element.22), channel_id=1, source_target_pairs={{0,32},{32,64},{64,96},{96,0},{1,33},{33,65},{65,97},{97,1},{2,34}... | collective-permute-start | bytes 98312 | tf_op jit(solution)/shard_map/ppermute | solution.py:268
  25.7 18.6 %collective-permute-start.4 = (f32[64,128]{1,0:T(8,128)}, f32[64,128]{1,0:T(8,128)S(1)}, u32[]{:S(2)}, u32[]{:S(2)}) collective-permute-start(f32[64,128]{1,0:T(8,128)} %get-tuple-element.25), channel_id=1, source_target_pairs={{1,0},{2,1},{3,2},{4,3},{5,4},{6,5},{7,6},{8,7},{9,8},{10,9},{11,1... | collective-permute-start | bytes 98312 | tf_op jit(solution)/shard_map/ppermute | solution.py:271
  30.9 16.3 %collective-permute-start.5 = (f32[64,128]{1,0:T(8,128)}, f32[64,128]{1,0:T(8,128)S(1)}, u32[]{:S(2)}, u32[]{:S(2)}) collective-permute-start(f32[64,128]{1,0:T(8,128)} %get-tuple-element.26), channel_id=1, source_target_pairs={{0,1},{1,2},{2,3},{3,4},{4,5},{5,6},{6,7},{7,8},{8,9},{9,10},{10,1... | collective-permute-start | bytes 98312 | tf_op jit(solution)/shard_map/ppermute | solution.py:270
  32.0 3.3 %copy-start.20 = (s32[1,1,1,32]{3,2,1,0:T(1,128)S(1)}, s32[1,1,1,32]{3,2,1,0:T(1,128)}, u32[]{:S(2)}) copy-start(s32[1,1,1,32]{3,2,1,0:T(1,128)} %param.15) | copy-start | bytes 388
  33.4 4.7 %copy-start.18 = (s32[1,1,1,32,2]{3,4,2,1,0:T(2,128)S(1)}, s32[1,1,1,32,2]{3,4,2,1,0:T(2,128)}, u32[]{:S(2)}) copy-start(s32[1,1,1,32,2]{3,4,2,1,0:T(2,128)} %param.13) | copy-start | bytes 772
  33.4 4.9 %copy-start.19 = (s32[1,1,1,32,2]{3,4,2,1,0:T(2,128)S(1)}, s32[1,1,1,32,2]{3,4,2,1,0:T(2,128)}, u32[]{:S(2)}) copy-start(s32[1,1,1,32,2]{3,4,2,1,0:T(2,128)} %param.14) | copy-start | bytes 772
  33.4 5.4 %copy-start.4 = (f32[2,8,4,16,16]{4,3,2,1,0:T(8,128)S(1)}, f32[2,8,4,16,16]{4,3,2,1,0:T(8,128)}, u32[]{:S(2)}) copy-start(f32[2,8,4,16,16]{4,3,2,1,0:T(8,128)} %get-tuple-element.35) | copy-start | bytes 196612
  33.4 7.6 %collective-permute-start = (f32[16,1024]{1,0:T(8,128)S(1)}, f32[16,1024]{1,0:T(8,128)S(1)}, u32[]{:S(2)}, u32[]{:S(2)}) collective-permute-start(f32[16,1024]{1,0:T(8,128)S(1)} %slice.28), channel_id=1, source_target_pairs={{0,128},{128,0},{1,129},{129,1},{2,130},{130,2},{3,131},{131,3},{4... | collective-permute-start | bytes 196616 | tf_op jit(solution)/shard_map/ppermute | solution.py:266
  39.0 2.0 %copy-start.14 = (f32[64,128]{1,0:T(8,128)}, f32[64,128]{1,0:T(8,128)S(1)}, u32[]{:S(2)}) copy-start(f32[64,128]{1,0:T(8,128)S(1)} %collective-permute-done.2.hyp_ref) | copy-start | bytes 98308
  39.1 2.0 %collective-permute-start.1 = (f32[16,1024]{1,0:T(8,128)S(1)}, f32[16,1024]{1,0:T(8,128)S(1)}, u32[]{:S(2)}, u32[]{:S(2)}) collective-permute-start(f32[16,1024]{1,0:T(8,128)S(1)} %slice.30), channel_id=1, source_target_pairs={{128,0},{0,128},{129,1},{1,129},{130,2},{2,130},{131,3},{3,131},{1... | collective-permute-start | bytes 196616 | tf_op jit(solution)/shard_map/ppermute | solution.py:267
  41.0 0.6 copy-start.6
  41.0 0.6 copy-start.9
  44.3 3.7 %copy-start.10 = (f32[64,128]{1,0:T(8,128)}, f32[64,128]{1,0:T(8,128)S(1)}, u32[]{:S(2)}) copy-start(f32[64,128]{1,0:T(8,128)S(1)} %collective-permute-done.4.hzp_ref) | copy-start | bytes 98308
  47.2 0.8 copy-start.11
  48.0 1.0 copy-start.1
  57.7 8.6 %copy-start.3 = (f32[64,1024]{1,0:T(8,128)S(1)}, f32[64,1024]{1,0:T(8,128)}, u32[]{:S(2)}) copy-start(f32[64,1024]{1,0:T(8,128)} %get-tuple-element.28.cur_ref) | copy-start | bytes 786436
  57.8 33.2 %all-to-all-start.1 = ((bf16[32,16,1024]{2,1,0:T(8,128)(2,1)}), bf16[32,16,1024]{2,1,0:T(8,128)(2,1)S(1)}, u32[]{:S(2)}, u32[]{:S(2)}) async-start(bf16[32,16,1024]{2,1,0:T(8,128)(2,1)} %bitcast.36), calls=%async_computation.1 | async-start | bytes 2097152 | tf_op jit(solution)/shard_map/all_to_all | solution.py:273
  66.4 9.1 %collective-permute-start.7 = (f32[16,1024]{1,0:T(8,128)S(1)}, f32[16,1024]{1,0:T(8,128)S(1)}, u32[]{:S(2)}, u32[]{:S(2)}) collective-permute-start(f32[16,1024]{1,0:T(8,128)S(1)} %get-tuple-element.40), channel_id=1, source_target_pairs={{128,0},{0,128},{129,1},{1,129},{130,2},{2,130},{131,3},{3,131},{1... | collective-permute-start | bytes 196616 | tf_op jit(solution)/shard_map/ppermute | solution.py:267
  66.5 9.0 %collective-permute-start.6 = (f32[16,1024]{1,0:T(8,128)S(1)}, f32[16,1024]{1,0:T(8,128)S(1)}, u32[]{:S(2)}, u32[]{:S(2)}) collective-permute-start(f32[16,1024]{1,0:T(8,128)S(1)} %get-tuple-element.41), channel_id=1, source_target_pairs={{0,128},{128,0},{1,129},{129,1},{2,130},{130,2},{3,131},{131,3},{4... | collective-permute-start | bytes 196616 | tf_op jit(solution)/shard_map/ppermute | solution.py:266
  67.0 8.4 %collective-permute-start.8 = (f32[64,128]{1,0:T(8,128)}, f32[64,128]{1,0:T(8,128)S(1)}, u32[]{:S(2)}, u32[]{:S(2)}) collective-permute-start(f32[64,128]{1,0:T(8,128)} %get-tuple-element.29), channel_id=1, source_target_pairs={{32,0},{64,32},{96,64},{0,96},{33,1},{65,33},{97,65},{1,97},{34,2}... | collective-permute-start | bytes 98312 | tf_op jit(solution)/shard_map/ppermute | solution.py:269
  67.8 7.6 %collective-permute-start.9 = (f32[64,128]{1,0:T(8,128)}, f32[64,128]{1,0:T(8,128)S(1)}, u32[]{:S(2)}, u32[]{:S(2)}) collective-permute-start(f32[64,128]{1,0:T(8,128)} %get-tuple-element.30), channel_id=1, source_target_pairs={{0,32},{32,64},{64,96},{96,0},{1,33},{33,65},{65,97},{97,1},{2,34}... | collective-permute-start | bytes 98312 | tf_op jit(solution)/shard_map/ppermute | solution.py:268
  70.2 14.1 %collective-permute-start.10 = (f32[64,128]{1,0:T(8,128)}, f32[64,128]{1,0:T(8,128)S(1)}, u32[]{:S(2)}, u32[]{:S(2)}) collective-permute-start(f32[64,128]{1,0:T(8,128)} %get-tuple-element.33), channel_id=1, source_target_pairs={{1,0},{2,1},{3,2},{4,3},{5,4},{6,5},{7,6},{8,7},{9,8},{10,9},{11,1... | collective-permute-start | bytes 98312 | tf_op jit(solution)/shard_map/ppermute | solution.py:271
  75.4 15.3 %collective-permute-start.11 = (f32[64,128]{1,0:T(8,128)}, f32[64,128]{1,0:T(8,128)S(1)}, u32[]{:S(2)}, u32[]{:S(2)}) collective-permute-start(f32[64,128]{1,0:T(8,128)} %get-tuple-element.34), channel_id=1, source_target_pairs={{0,1},{1,2},{2,3},{3,4},{4,5},{5,6},{6,7},{7,8},{8,9},{9,10},{10,1... | collective-permute-start | bytes 98312 | tf_op jit(solution)/shard_map/ppermute | solution.py:270
  75.5 0.6 copy-start.7
  76.1 0.6 copy-start.8
  84.4 6.6 %copy-start.12 = (f32[64,128]{1,0:T(8,128)}, f32[64,128]{1,0:T(8,128)S(1)}, u32[]{:S(2)}) copy-start(f32[64,128]{1,0:T(8,128)S(1)} %collective-permute-done.10.hzp_ref) | copy-start | bytes 98308
  90.7 0.6 copy-start.13
  90.9 1.0 copy-start.2
  (3 other events, 1.8 us)

commit v9 on v8

--- a/solution.py
+++ b/solution.py
@@ -62,9 +62,13 @@
 
 
 def _emit_send(pick_ref, cur, snd_ref):
-    snd_ref[...] = jnp.dot(
-        pick_ref[...], cur.astype(BF16), preferred_element_type=F32
-    ).astype(BF16)
+    rows = cur.shape[0]
+    shape = (pick_ref.shape[0], rows)
+    pr = lax.broadcasted_iota(jnp.int32, shape, 0)
+    pc = lax.broadcasted_iota(jnp.int32, shape, 1)
+    hit = (pick_ref[...] == (pc >> 3)) & ((pr & 7) == (pc & 7))
+    pick = jnp.where(hit, 1.0, 0.0).astype(BF16)
+    snd_ref[...] = jnp.dot(pick, cur.astype(BF16), preferred_element_type=F32).astype(BF16)
 
 
 def _send_kernel(pick_ref, cur_ref, snd_ref):
@@ -240,9 +244,7 @@
     sel_big = hit.astype(BF16)
     both = slot_cap * drive_count
     flat_plane = jnp.repeat(plane_list, drive_count)
-    pr = lax.broadcasted_iota(jnp.int32, (peer_count * both, rows), 0)
-    pc = lax.broadcasted_iota(jnp.int32, (peer_count * both, rows), 1)
-    pick = ((flat_plane[:, None] == pc // drive_count) & (pr % drive_count == pc % drive_count)).astype(BF16)
+    pick = flat_plane.reshape(peer_count * both, 1)
 
     def spread(a):
         a = a.reshape(width_x, 1, lanes)

time: 104 us -> 104 us (level)
  no operation moved by 1% of the time
where the time goes in v9:
time: 104 us; the launch traced here: 103 us
  starting transfers between devices  35.8 us (34%)
  Pallas kernels  30 us (29%)
  local copies, waits for them, and re-layouts  20.3 us (20%)
  waiting for transfers between devices  15.3 us (15%)
  other arithmetic  1.31 us (1%)
    all_to_all x2, starting transfers between devices, per_device(): lax.all_to_all(outgoing, 'kz', split_axis=0, concat_axis=0, tiled=True)  17.5 us
    pallas_call x2, Pallas kernels, _finish(): pl.pallas_call(functools.partial(_finish_kernel, last), out_shape=shapes,...  16.9 us
    ppermute x2, starting transfers between devices, per_device(): hzp = lax.ppermute(zlo, 'kz', down_z)  10.4 us
    ppermute x2, waiting for transfers between devices, per_device(): hzm = lax.ppermute(zhi, 'kz', up_z)  9.23 us
    pallas_call x2, Pallas kernels, _drift(): pl.pallas_call(_drift_kernel, out_shape=[plane, plane], scratch_shapes=[p...  5.3 us
    pallas_call x2, Pallas kernels, _halos(): return pl.pallas_call(_halo_kernel, out_shape=[halo] * 4)(cur)  5.16 us
    ppermute x2, waiting for transfers between devices, per_device(): hzp = lax.ppermute(zlo, 'kz', down_z)  5.07 us
    ppermute x2, starting transfers between devices, per_device(): hym = lax.ppermute(yhi, 'ky', up_y)  4.82 us
  transfers between devices with their start and end apart: 14, of which 5 were waited for; matrix products, arithmetic and copies ran while one was open for 9% of the time, Pallas kernels for 10%

profile of v9, /device:TPU:6, one launch (start us, length us, event | category | flops | bytes accessed | tf_op | source)
XLA Modules:
  0.0 102.9 jit_solution(3917409154103874012)
XLA Ops:
  0.0 0.8 copy.12
  0.9 0.8 reshape_reshape.12.pick_ref
  1.8 3.9 %reshape.49.cur_ref = f32[64,1024]{1,0:T(8,128)} reshape(f32[8,8,4,16,16]{4,3,2,1,0:T(8,128)} %param.8) | data formatting | bytes 524288 | tf_op jit(solution)/shard_map/reshape | solution.py:262
  5.6 2.6 %shard_map.82 = bf16[512,1024]{1,0:T(8,128)(2,1)} custom-call(s32[512,1]{1,0:T(8,128)} %reshape_reshape.12.pick_ref, f32[64,1024]{1,0:T(8,128)} %reshape.49.cur_ref), custom_call_target="tpu_custom_call" | custom-call | tf_op jit(solution)/shard_map/pallas_call | solution.py:166
  8.3 11.5 %all-to-all-start = ((bf16[32,16,1024]{2,1,0:T(8,128)(2,1)}), bf16[32,16,1024]{2,1,0:T(8,128)(2,1)S(1)}, u32[]{:S(2)}, u32[]{:S(2)}) async-start(bf16[32,16,1024]{2,1,0:T(8,128)(2,1)} %bitcast.33), calls=%async_computation | async-start | bytes 2097152 | tf_op jit(solution)/shard_map/all_to_all | solution.py:275
  19.8 2.6 %shard_map.83 = (f32[64,128]{1,0:T(8,128)}, f32[64,128]{1,0:T(8,128)}, f32[64,128]{1,0:T(8,128)}, f32[64,128]{1,0:T(8,128)}) custom-call(f32[64,1024]{1,0:T(8,128)} %reshape.49.cur_ref), custom_call_target="tpu_custom_call" | custom-call | tf_op jit(solution)/shard_map/pallas_call | solution.py:171
  22.3 0.8 collective-permute-start.2
  23.2 2.4 %collective-permute-start.3 = (f32[64,128]{1,0:T(8,128)}, f32[64,128]{1,0:T(8,128)S(1)}, u32[]{:S(2)}, u32[]{:S(2)}) collective-permute-start(f32[64,128]{1,0:T(8,128)} %get-tuple-element.22), channel_id=1, source_target_pairs={{0,32},{32,64},{64,96},{96,0},{1,33},{33,65},{65,97},{97,1},{2,34}... | collective-permute-start | bytes 98312 | tf_op jit(solution)/shard_map/ppermute | solution.py:270
  25.6 5.2 %collective-permute-start.4 = (f32[64,128]{1,0:T(8,128)}, f32[64,128]{1,0:T(8,128)S(1)}, u32[]{:S(2)}, u32[]{:S(2)}) collective-permute-start(f32[64,128]{1,0:T(8,128)} %get-tuple-element.25), channel_id=1, source_target_pairs={{1,0},{2,1},{3,2},{4,3},{5,4},{6,5},{7,6},{8,7},{9,8},{10,9},{11,1... | collective-permute-start | bytes 98312 | tf_op jit(solution)/shard_map/ppermute | solution.py:273
  30.8 1.1 %fusion.14 = (f32[2,8,4,16,16]{4,3,2,1,0:T(8,128)}, f32[2,8,4,16,16]{4,3,2,1,0:T(8,128)}) fusion(f32[8,8,4,16,16]{4,3,2,1,0:T(8,128)S(1)} %copy-done), kind=kLoop, calls=%fused_computation.36 | loop fusion | bytes 262144 | tf_op jit(solution)/shard_map/slice | solution.py:269
  31.9 1.3 %slice.28 = f32[16,1024]{1,0:T(8,128)S(1)} reshape(f32[2,8,4,16,16]{4,3,2,1,0:T(8,128)} %get-tuple-element.36) | data formatting | bytes 131072 | tf_op jit(solution)/shard_map/slice | solution.py:268
  33.3 1.2 %fusion.15 = (f32[8,1,4,16,16]{4,3,2,1,0:T(8,128)S(1)}, f32[8,1,4,16,16]{4,3,2,1,0:T(8,128)S(1)}, f32[8,1,4,16,16]{4,3,2,1,0:T(8,128)S(1)}) fusion(f32[8,3,4,16,16]{4,3,2,1,0:T(8,128)} %param.9), kind=kLoop, calls=%fused_computation.37 | loop fusion | bytes 196608 | tf_op jit(solution)/shard_map/slice | solution.py:255
  35.3 0.7 broadcast_bitcast_fusion.3.fx_ref
  36.1 0.7 broadcast_bitcast_fusion.fz_ref
  36.8 0.9 broadcast_bitcast_fusion.1
  39.0 0.7 collective-permute-start.1
  39.7 1.2 %fusion.3.sel_ref = bf16[256,512]{1,0:T(8,128)(2,1)} fusion(s32[512]{0:T(512)S(1)} %get-tuple-element.42, s32[512]{0:T(512)S(1)} %get-tuple-element.43, s32[256]{0:T(256)S(1)} %get-tuple-element.48, s32[256]{0:T(256)S(1)} %get-tuple-element.49, s32[512]{0:T(512)S(1)} %eq.30, s32[256]{0:T(256)S(1)} %get-tuple-element.45, s32[256]{0:T(256)S(1)} %get-tuple-element.50, ...), kind=kLoop, calls=%fused_computation.10 | loop fusion | flops 2883584 | bytes 278272 | tf_op jit(solution)/shard_map/convert_element_type | solution.py:244
  41.6 2.6 %shard_map.84 = (f32[64,1024]{1,0:T(8,128)}, f32[64,1024]{1,0:T(8,128)}) custom-call(f32[64,1024]{1,0:T(8,128)} %reshape.49.cur_ref, f32[16,1024]{1,0:T(8,128)} %copy-done.6, f32[16,1024]{1,0:T(8,128)} %copy-done.8, f32[64,128]{1,0:T(8,128)} %copy-done.14, f32[64,128]{1,0:T(8,128)} %copy-done.15, f32[64,1024]{1,0:T(8,128)} %broadcast_bitcast_fusion.3.fx_ref, ...), custom_call_target="tpu_custom_call" | custom-call | tf_op jit(solution)/shard_map/pallas_call | solution.py:201
  44.2 2.8 %collective-permute-done.5.hzm_ref = f32[64,128]{1,0:T(8,128)S(1)} collective-permute-done((f32[64,128]{1,0:T(8,128)}, f32[64,128]{1,0:T(8,128)S(1)}, u32[]{:S(2)}, u32[]{:S(2)}) %collective-permute-start.5) | collective-permute-done | bytes 32800 | tf_op jit(solution)/shard_map/ppermute | solution.py:272
  47.1 0.8 all-to-all-done
  47.8 1.0 copy-done.1
  48.8 8.9 %shard_map.85 = (f32[64,1024]{1,0:T(8,128)}, bf16[512,1024]{1,0:T(8,128)(2,1)}) custom-call(s32[512,1]{1,0:T(8,128)} %reshape_reshape.12.pick_ref, bf16[256,512]{1,0:T(8,128)(2,1)} %fusion.3.sel_ref, bf16[512,1024]{1,0:T(8,128)(2,1)} %bitcast.34, f32[64,1024]{1,0:T(8,128)} %reshape.49.cur_ref, f32[64,1024]{1,0:T(8,128)} %get-tuple-element.23.a_ref, ...), custom_call_target="tpu_custom_call" | custom-call | tf_op jit(solution)/shard_map/pallas_call | solution.py:181
  57.7 6.0 %all-to-all-start.1 = ((bf16[32,16,1024]{2,1,0:T(8,128)(2,1)}), bf16[32,16,1024]{2,1,0:T(8,128)(2,1)S(1)}, u32[]{:S(2)}, u32[]{:S(2)}) async-start(bf16[32,16,1024]{2,1,0:T(8,128)(2,1)} %bitcast.36), calls=%async_computation.1 | async-start | bytes 2097152 | tf_op jit(solution)/shard_map/all_to_all | solution.py:275
  63.7 2.6 %shard_map.86 = (f32[64,128]{1,0:T(8,128)}, f32[64,128]{1,0:T(8,128)}, f32[64,128]{1,0:T(8,128)}, f32[64,128]{1,0:T(8,128)}) custom-call(f32[64,1024]{1,0:T(8,128)} %get-tuple-element.28.cur_ref), custom_call_target="tpu_custom_call" | custom-call | tf_op jit(solution)/shard_map/pallas_call | solution.py:171
  66.9 0.8 collective-permute-start.8
  67.8 2.4 %collective-permute-start.9 = (f32[64,128]{1,0:T(8,128)}, f32[64,128]{1,0:T(8,128)S(1)}, u32[]{:S(2)}, u32[]{:S(2)}) collective-permute-start(f32[64,128]{1,0:T(8,128)} %get-tuple-element.30), channel_id=1, source_target_pairs={{0,32},{32,64},{64,96},{96,0},{1,33},{33,65},{65,97},{97,1},{2,34}... | collective-permute-start | bytes 98312 | tf_op jit(solution)/shard_map/ppermute | solution.py:270
  70.2 5.2 %collective-permute-start.10 = (f32[64,128]{1,0:T(8,128)}, f32[64,128]{1,0:T(8,128)S(1)}, u32[]{:S(2)}, u32[]{:S(2)}) collective-permute-start(f32[64,128]{1,0:T(8,128)} %get-tuple-element.33), channel_id=1, source_target_pairs={{1,0},{2,1},{3,2},{4,3},{5,4},{6,5},{7,6},{8,7},{9,8},{10,9},{11,1... | collective-permute-start | bytes 98312 | tf_op jit(solution)/shard_map/ppermute | solution.py:273
  76.6 2.7 %shard_map.87 = (f32[64,1024]{1,0:T(8,128)}, f32[64,1024]{1,0:T(8,128)}) custom-call(f32[64,1024]{1,0:T(8,128)} %get-tuple-element.28.cur_ref, f32[16,1024]{1,0:T(8,128)} %copy-done.9, f32[16,1024]{1,0:T(8,128)} %copy-done.7, f32[64,128]{1,0:T(8,128)} %copy-done.16, f32[64,128]{1,0:T(8,128)} %copy-done.17, f32[64,1024]{1,0:T(8,128)} %broadcast_bitcast_fusion.3.fx_ref, ...), custom_call_target="tpu_custom_call" | custom-call | tf_op jit(solution)/shard_map/pallas_call | solution.py:201
  79.3 5.1 %collective-permute-done.10.hzp_ref = f32[64,128]{1,0:T(8,128)S(1)} collective-permute-done((f32[64,128]{1,0:T(8,128)}, f32[64,128]{1,0:T(8,128)S(1)}, u32[]{:S(2)}, u32[]{:S(2)}) %collective-permute-start.10) | collective-permute-done | bytes 32800 | tf_op jit(solution)/shard_map/ppermute | solution.py:273
  84.4 6.4 %collective-permute-done.11.hzm_ref = f32[64,128]{1,0:T(8,128)S(1)} collective-permute-done((f32[64,128]{1,0:T(8,128)}, f32[64,128]{1,0:T(8,128)S(1)}, u32[]{:S(2)}, u32[]{:S(2)}) %collective-permute-start.11) | collective-permute-done | bytes 32800 | tf_op jit(solution)/shard_map/ppermute | solution.py:272
  91.9 8.0 %shard_map.88 = f32[64,1024]{1,0:T(8,128)} custom-call(s32[512,1]{1,0:T(8,128)} %reshape_reshape.12.pick_ref, bf16[256,512]{1,0:T(8,128)(2,1)} %fusion.3.sel_ref, bf16[512,1024]{1,0:T(8,128)(2,1)} %bitcast.35, f32[64,1024]{1,0:T(8,128)} %get-tuple-element.28.cur_ref, f32[64,1024]{1,0:T(8,128)} %get-tuple-element.31.a_ref, ...), custom_call_target="tpu_custom_call" | custom-call | tf_op jit(solution)/shard_map/pallas_call | solution.py:181
  100.0 3.0 %reshape.58 = f32[8,8,4,16,16]{4,3,2,1,0:T(8,128)} reshape(f32[64,1024]{1,0:T(8,128)} %shard_map.88) | data formatting | bytes 524288 | tf_op jit(solution)/shard_map/reshape | solution.py:283
  (83 shorter events, 5.9 us)
Async XLA Ops:
  5.6 25.2 %copy-start = (f32[8,8,4,16,16]{4,3,2,1,0:T(8,128)S(1)}, f32[8,8,4,16,16]{4,3,2,1,0:T(8,128)}, u32[]{:S(2)}) copy-start(f32[8,8,4,16,16]{4,3,2,1,0:T(8,128)} %param.8) | copy-start | bytes 786436
  8.3 39.6 %all-to-all-start = ((bf16[32,16,1024]{2,1,0:T(8,128)(2,1)}), bf16[32,16,1024]{2,1,0:T(8,128)(2,1)S(1)}, u32[]{:S(2)}, u32[]{:S(2)}) async-start(bf16[32,16,1024]{2,1,0:T(8,128)(2,1)} %bitcast.33), calls=%async_computation | async-start | bytes 2097152 | tf_op jit(solution)/shard_map/all_to_all | solution.py:275
  22.3 16.6 %collective-permute-start.2 = (f32[64,128]{1,0:T(8,128)}, f32[64,128]{1,0:T(8,128)S(1)}, u32[]{:S(2)}, u32[]{:S(2)}) collective-permute-start(f32[64,128]{1,0:T(8,128)} %get-tuple-element.21), channel_id=1, source_target_pairs={{32,0},{64,32},{96,64},{0,96},{33,1},{65,33},{97,65},{1,97},{34,2}... | collective-permute-start | bytes 98312 | tf_op jit(solution)/shard_map/ppermute | solution.py:271
  23.2 17.7 %collective-permute-start.3 = (f32[64,128]{1,0:T(8,128)}, f32[64,128]{1,0:T(8,128)S(1)}, u32[]{:S(2)}, u32[]{:S(2)}) collective-permute-start(f32[64,128]{1,0:T(8,128)} %get-tuple-element.22), channel_id=1, source_target_pairs={{0,32},{32,64},{64,96},{96,0},{1,33},{33,65},{65,97},{97,1},{2,34}... | collective-permute-start | bytes 98312 | tf_op jit(solution)/shard_map/ppermute | solution.py:270
  25.6 18.6 %collective-permute-start.4 = (f32[64,128]{1,0:T(8,128)}, f32[64,128]{1,0:T(8,128)S(1)}, u32[]{:S(2)}, u32[]{:S(2)}) collective-permute-start(f32[64,128]{1,0:T(8,128)} %get-tuple-element.25), channel_id=1, source_target_pairs={{1,0},{2,1},{3,2},{4,3},{5,4},{6,5},{7,6},{8,7},{9,8},{10,9},{11,1... | collective-permute-start | bytes 98312 | tf_op jit(solution)/shard_map/ppermute | solution.py:273
  30.8 3.8 %copy-start.5 = (f32[8,4,16,16]{3,2,1,0:T(8,128)S(1)}, f32[8,4,16,16]{3,2,1,0:T(8,128)}, u32[]{:S(2)}) copy-start(f32[8,4,16,16]{3,2,1,0:T(8,128)} %param.10) | copy-start | bytes 98308
  30.8 16.3 %collective-permute-start.5 = (f32[64,128]{1,0:T(8,128)}, f32[64,128]{1,0:T(8,128)S(1)}, u32[]{:S(2)}, u32[]{:S(2)}) collective-permute-start(f32[64,128]{1,0:T(8,128)} %get-tuple-element.26), channel_id=1, source_target_pairs={{0,1},{1,2},{2,3},{3,4},{4,5},{5,6},{6,7},{7,8},{8,9},{9,10},{10,1... | collective-permute-start | bytes 98312 | tf_op jit(solution)/shard_map/ppermute | solution.py:272
  31.9 3.4 %copy-start.20 = (s32[1,1,1,32]{3,2,1,0:T(1,128)S(1)}, s32[1,1,1,32]{3,2,1,0:T(1,128)}, u32[]{:S(2)}) copy-start(s32[1,1,1,32]{3,2,1,0:T(1,128)} %param.15) | copy-start | bytes 388
  33.2 4.8 %copy-start.18 = (s32[1,1,1,32,2]{3,4,2,1,0:T(2,128)S(1)}, s32[1,1,1,32,2]{3,4,2,1,0:T(2,128)}, u32[]{:S(2)}) copy-start(s32[1,1,1,32,2]{3,4,2,1,0:T(2,128)} %param.13) | copy-start | bytes 772
  33.2 5.0 %copy-start.19 = (s32[1,1,1,32,2]{3,4,2,1,0:T(2,128)S(1)}, s32[1,1,1,32,2]{3,4,2,1,0:T(2,128)}, u32[]{:S(2)}) copy-start(s32[1,1,1,32,2]{3,4,2,1,0:T(2,128)} %param.14) | copy-start | bytes 772
  33.2 5.5 %copy-start.4 = (f32[2,8,4,16,16]{4,3,2,1,0:T(8,128)S(1)}, f32[2,8,4,16,16]{4,3,2,1,0:T(8,128)}, u32[]{:S(2)}) copy-start(f32[2,8,4,16,16]{4,3,2,1,0:T(8,128)} %get-tuple-element.35) | copy-start | bytes 196612
  33.2 7.7 %collective-permute-start = (f32[16,1024]{1,0:T(8,128)S(1)}, f32[16,1024]{1,0:T(8,128)S(1)}, u32[]{:S(2)}, u32[]{:S(2)}) collective-permute-start(f32[16,1024]{1,0:T(8,128)S(1)} %slice.28), channel_id=1, source_target_pairs={{0,128},{128,0},{1,129},{129,1},{2,130},{130,2},{3,131},{131,3},{4... | collective-permute-start | bytes 196616 | tf_op jit(solution)/shard_map/ppermute | solution.py:268
  39.0 2.0 %copy-start.14 = (f32[64,128]{1,0:T(8,128)}, f32[64,128]{1,0:T(8,128)S(1)}, u32[]{:S(2)}) copy-start(f32[64,128]{1,0:T(8,128)S(1)} %collective-permute-done.2.hyp_ref) | copy-start | bytes 98308
  39.0 1.9 %collective-permute-start.1 = (f32[16,1024]{1,0:T(8,128)S(1)}, f32[16,1024]{1,0:T(8,128)S(1)}, u32[]{:S(2)}, u32[]{:S(2)}) collective-permute-start(f32[16,1024]{1,0:T(8,128)S(1)} %slice.30), channel_id=1, source_target_pairs={{128,0},{0,128},{129,1},{1,129},{130,2},{2,130},{131,3},{3,131},{1... | collective-permute-start | bytes 196616 | tf_op jit(solution)/shard_map/ppermute | solution.py:269
  40.9 0.6 copy-start.6
  40.9 0.6 copy-start.8
  44.2 3.6 %copy-start.10 = (f32[64,128]{1,0:T(8,128)}, f32[64,128]{1,0:T(8,128)S(1)}, u32[]{:S(2)}) copy-start(f32[64,128]{1,0:T(8,128)S(1)} %collective-permute-done.4.hzp_ref) | copy-start | bytes 98308
  47.1 0.8 copy-start.11
  47.8 1.0 copy-start.1
  57.7 8.6 %copy-start.3 = (f32[64,1024]{1,0:T(8,128)S(1)}, f32[64,1024]{1,0:T(8,128)}, u32[]{:S(2)}) copy-start(f32[64,1024]{1,0:T(8,128)} %get-tuple-element.28.cur_ref) | copy-start | bytes 786436
  57.7 33.3 %all-to-all-start.1 = ((bf16[32,16,1024]{2,1,0:T(8,128)(2,1)}), bf16[32,16,1024]{2,1,0:T(8,128)(2,1)S(1)}, u32[]{:S(2)}, u32[]{:S(2)}) async-start(bf16[32,16,1024]{2,1,0:T(8,128)(2,1)} %bitcast.36), calls=%async_computation.1 | async-start | bytes 2097152 | tf_op jit(solution)/shard_map/all_to_all | solution.py:275
  66.3 9.1 %collective-permute-start.7 = (f32[16,1024]{1,0:T(8,128)S(1)}, f32[16,1024]{1,0:T(8,128)S(1)}, u32[]{:S(2)}, u32[]{:S(2)}) collective-permute-start(f32[16,1024]{1,0:T(8,128)S(1)} %get-tuple-element.40), channel_id=1, source_target_pairs={{128,0},{0,128},{129,1},{1,129},{130,2},{2,130},{131,3},{3,131},{1... | collective-permute-start | bytes 196616 | tf_op jit(solution)/shard_map/ppermute | solution.py:269
  66.4 9.0 %collective-permute-start.6 = (f32[16,1024]{1,0:T(8,128)S(1)}, f32[16,1024]{1,0:T(8,128)S(1)}, u32[]{:S(2)}, u32[]{:S(2)}) collective-permute-start(f32[16,1024]{1,0:T(8,128)S(1)} %get-tuple-element.41), channel_id=1, source_target_pairs={{0,128},{128,0},{1,129},{129,1},{2,130},{130,2},{3,131},{131,3},{4... | collective-permute-start | bytes 196616 | tf_op jit(solution)/shard_map/ppermute | solution.py:268
  66.9 8.4 %collective-permute-start.8 = (f32[64,128]{1,0:T(8,128)}, f32[64,128]{1,0:T(8,128)S(1)}, u32[]{:S(2)}, u32[]{:S(2)}) collective-permute-start(f32[64,128]{1,0:T(8,128)} %get-tuple-element.29), channel_id=1, source_target_pairs={{32,0},{64,32},{96,64},{0,96},{33,1},{65,33},{97,65},{1,97},{34,2}... | collective-permute-start | bytes 98312 | tf_op jit(solution)/shard_map/ppermute | solution.py:271
  67.8 7.6 %collective-permute-start.9 = (f32[64,128]{1,0:T(8,128)}, f32[64,128]{1,0:T(8,128)S(1)}, u32[]{:S(2)}, u32[]{:S(2)}) collective-permute-start(f32[64,128]{1,0:T(8,128)} %get-tuple-element.30), channel_id=1, source_target_pairs={{0,32},{32,64},{64,96},{96,0},{1,33},{33,65},{65,97},{97,1},{2,34}... | collective-permute-start | bytes 98312 | tf_op jit(solution)/shard_map/ppermute | solution.py:270
  70.2 14.2 %collective-permute-start.10 = (f32[64,128]{1,0:T(8,128)}, f32[64,128]{1,0:T(8,128)S(1)}, u32[]{:S(2)}, u32[]{:S(2)}) collective-permute-start(f32[64,128]{1,0:T(8,128)} %get-tuple-element.33), channel_id=1, source_target_pairs={{1,0},{2,1},{3,2},{4,3},{5,4},{6,5},{7,6},{8,7},{9,8},{10,9},{11,1... | collective-permute-start | bytes 98312 | tf_op jit(solution)/shard_map/ppermute | solution.py:273
  75.4 15.4 %collective-permute-start.11 = (f32[64,128]{1,0:T(8,128)}, f32[64,128]{1,0:T(8,128)S(1)}, u32[]{:S(2)}, u32[]{:S(2)}) collective-permute-start(f32[64,128]{1,0:T(8,128)} %get-tuple-element.34), channel_id=1, source_target_pairs={{0,1},{1,2},{2,3},{3,4},{4,5},{5,6},{6,7},{7,8},{8,9},{9,10},{10,1... | collective-permute-start | bytes 98312 | tf_op jit(solution)/shard_map/ppermute | solution.py:272
  75.4 0.6 copy-start.17
  75.4 0.6 copy-start.7
  76.0 0.6 copy-start.9
  84.4 6.6 %copy-start.12 = (f32[64,128]{1,0:T(8,128)}, f32[64,128]{1,0:T(8,128)S(1)}, u32[]{:S(2)}) copy-start(f32[64,128]{1,0:T(8,128)S(1)} %collective-permute-done.10.hzp_ref) | copy-start | bytes 98308
  90.9 1.0 copy-start.2
  (3 other events, 1.8 us)
